TPU v7x, 512 devices: a whole 4x8x8 slice. The times are simulated.
512 devices in a mesh: depth: 16 (over z_lo, x, core), height: 8 (over y), sample: 4 (over z_hi).
Axes of the slice: x: 4, y: 8, z: 8 (z_hi: 4, z_lo: 2; z = z_hi * 2 + z_lo), core: 2. Of those that a mesh axis runs over, the one named last changes fastest.
Arguments:
- volume: bfloat16 [4, 4, 64, 32, 512], P('sample', None, 'depth', 'height'), may hold values from -6 to 6
- kernel_one: bfloat16 [32, 108], replicated, may hold values from -0.625 to 0.625
- kernel_two: bfloat16 [64, 864], P('height'), may hold values from -0.21875 to 0.21875
- cotangent: bfloat16 [4, 64, 16, 1024], P('sample', 'height', 'depth'), may hold values from -24 to 24
Outputs:
- pooled_two: bfloat16 [4, 64, 16, 1024], P('sample', 'height', 'depth')
- weight_grad: float32 [64, 864], P('height')
- act_grad: bfloat16 [4, 32, 32, 16, 256], P('sample', None, 'depth', 'height')
All inputs are finite; a program needn't handle non-finite values.
Results may differ from a plain program's by a relative error of at most 0.005.
Values may be sent and summed in bfloat16 or wider, within the bound.
No kernel may reach another device: no remote copies, remote signals or barrier semaphores. Data moves between devices by JAX's collectives and lax.ppermute only.
A program may use at most 64 MiB of HBM per device.

v0:
```python
import jax
import jax.numpy as jnp
from jax import lax
from jax.sharding import PartitionSpec as P

LEAK_SLOPE = 0.3
CONV_DIMS = ("NCDHW", "OIDHW", "NCDHW")


def extended(block, sides, width):
    for axis, dim in sides:
        count = lax.axis_size(axis)
        forward = [(i, i + 1) for i in range(count - 1)]
        backward = [(target, source) for source, target in forward]
        low = lax.ppermute(
            lax.slice_in_dim(block, block.shape[dim] - width, None, axis=dim), axis, forward
        )
        high = lax.ppermute(lax.slice_in_dim(block, 0, width, axis=dim), axis, backward)
        block = jnp.concatenate([low, block, high], axis=dim)
    return block


def butterfly_sum(values, axes):
    sizes = [lax.axis_size(axis) for axis in axes]
    count = 1
    for size in sizes:
        count *= size
    if count & (count - 1):
        return lax.psum(values, axes)
    step = 1
    while step < count:
        pairs = [(i, i ^ step) for i in range(count)]
        values = values + lax.ppermute(values, axes, pairs)
        step *= 2
    return values


def halving_scatter(values, axis, dim):
    count = lax.axis_size(axis)
    if count & (count - 1):
        return lax.psum_scatter(values, axis, scatter_dimension=dim, tiled=True)
    index = lax.axis_index(axis)
    step = count // 2
    while step >= 1:
        half = values.shape[dim] // 2
        bit = (index // step) % 2
        keep = lax.dynamic_slice_in_dim(values, bit * half, half, axis=dim)
        send = lax.dynamic_slice_in_dim(values, (1 - bit) * half, half, axis=dim)
        pairs = [(i, i ^ step) for i in range(count)]
        values = keep + lax.ppermute(send, axis, pairs)
        step //= 2
    return values


def delta_shifts(delta_ext):
    _, _, _, hsize, wsize = delta_ext.shape
    dpad = jnp.pad(delta_ext[0], ((0, 0), (0, 0), (1, 1), (1, 1)))
    return jnp.stack(
        [
            dpad[:, :, 2 - kh : 2 - kh + hsize, 2 - kw : 2 - kw + wsize]
            for kh in range(3)
            for kw in range(3)
        ],
        axis=1,
    )


def weight_gradient(level_ext, shifted):
    chans = level_ext.shape[1]
    filters, _, dsize, _, _ = shifted.shape
    levels = jnp.stack([level_ext[0, :, kd : kd + dsize] for kd in range(3)], axis=0)
    grad = lax.dot_general(
        shifted,
        levels,
        (((2, 3, 4), (2, 3, 4)), ((), ())),
        preferred_element_type=jnp.float32,
    )
    grad = grad.reshape(filters, 3, 3, 3, chans)
    return jnp.transpose(grad, (0, 4, 3, 1, 2)).reshape(filters, chans * 27)


def back_product(shifts_ext, kernel):
    filters, chans = kernel.shape[:2]
    dsize = shifts_ext.shape[2] - 2
    stacked = jnp.stack(
        [shifts_ext[:, :, 2 - kd : 2 - kd + dsize] for kd in range(3)], axis=0
    )
    weights = jnp.transpose(kernel, (1, 2, 0, 3, 4)).reshape(chans, 3, filters, 9)
    grad = lax.dot_general(
        weights,
        stacked,
        (((1, 2, 3), (0, 1, 2)), ((), ())),
        preferred_element_type=jnp.float32,
    )
    return grad[None]


def activate(values):
    return LEAK_SLOPE * values + (1.0 - LEAK_SLOPE) * jax.nn.softplus(values)


def slope_at(values):
    return LEAK_SLOPE + (1.0 - LEAK_SLOPE) * jax.nn.sigmoid(values)


def pooled(values):
    count, chans, dsize, hsize, wsize = values.shape
    blocks = values.reshape(count, chans, dsize // 2, 2, hsize // 2, 2, wsize // 2, 2)
    return blocks.mean(axis=(3, 5, 7))


def spread_up(values):
    values = jnp.repeat(jnp.repeat(jnp.repeat(values, 2, axis=2), 2, axis=3), 2, axis=4)
    return values * 0.125


def conv_valid(inputs, kernel):
    return lax.conv_general_dilated(
        inputs,
        kernel,
        (1, 1, 1),
        "VALID",
        dimension_numbers=CONV_DIMS,
        preferred_element_type=jnp.float32,
    )


def back_conv(delta_pad, kernel):
    flipped = jnp.flip(kernel, axis=(2, 3, 4))
    return lax.conv_general_dilated(
        delta_pad,
        flipped,
        (1, 1, 1),
        "VALID",
        dimension_numbers=("NCDHW", "IODHW", "NCDHW"),
        preferred_element_type=jnp.float32,
    )


def shards(volume, kernel_one, kernel_two, cotangent):
    depth_count = lax.axis_size("depth")
    height_count = lax.axis_size("height")
    sample_count = lax.axis_size("sample")
    chans_in = volume.shape[1]
    depth_loc = volume.shape[2]
    height_loc = volume.shape[3]
    width_all = volume.shape[4]
    chans_mid = kernel_one.shape[0]
    filters = kernel_two.shape[0]
    first_kernel = kernel_one.reshape(chans_mid, chans_in, 3, 3, 3)
    second_kernel = kernel_two.reshape(filters, chans_mid, 3, 3, 3)
    padded = extended(volume, (("depth", 2), ("height", 3)), 1)
    window = jnp.pad(padded, ((0, 0), (0, 0), (0, 0), (0, 0), (1, 1)))
    level_loc = pooled(activate(conv_valid(window, first_kernel))).astype(jnp.bfloat16)
    slab_rows = lax.all_gather(level_loc, "height", axis=3, tiled=True)
    level_one = extended(slab_rows, (("depth", 2),), 1)
    level_pad = jnp.pad(level_one, ((0, 0), (0, 0), (0, 0), (1, 1), (1, 1)))
    pre_two = conv_valid(level_pad, second_kernel)
    pooled_grid = pooled(activate(pre_two)).astype(jnp.bfloat16)
    depth_two = pooled_grid.shape[2]
    pooled_two = pooled_grid.reshape(
        1, filters, depth_two, pooled_grid.shape[3] * pooled_grid.shape[4]
    )
    cot_grid = cotangent.reshape(1, filters, depth_two, pooled_grid.shape[3], pooled_grid.shape[4])
    delta_two = (spread_up(cot_grid.astype(jnp.float32)) * slope_at(pre_two)).astype(jnp.bfloat16)
    scale = 1.0 / float(
        sample_count
        * (depth_loc // 2)
        * depth_count
        * (height_loc // 2)
        * height_count
        * (width_all // 2)
    ) ** 0.5
    delta_ext = extended(delta_two, (("depth", 2),), 1)
    shifts_ext = delta_shifts(delta_ext)
    weight_term = weight_gradient(level_one, delta_shifts(delta_two)) * scale
    flat_size = weight_term.size
    lanes = 128 if flat_size % 128 == 0 else flat_size
    weight_grad = butterfly_sum(
        weight_term.reshape(flat_size // lanes, lanes), ("depth", "sample")
    ).reshape(weight_term.shape)
    back_part = back_product(shifts_ext, second_kernel)
    act_grad = halving_scatter(back_part, "height", 3).astype(jnp.bfloat16)
    return (pooled_two, weight_grad, act_grad)


def solution(mesh):
    in_specs = (
        P("sample", None, "depth", "height", None),
        P(),
        P("height", None),
        P("sample", "height", "depth", None),
    )
    out_specs = (
        P("sample", "height", "depth", None),
        P("height", None),
        P("sample", None, "depth", "height", None),
    )
    return jax.shard_map(shards, mesh=mesh, in_specs=in_specs, out_specs=out_specs, check_vma=False)
```

profile of v0, /device:TPU:6, one launch (start us, length us, event | category | flops | bytes accessed | tf_op | source)
XLA Modules:
  0.0 219.3 jit_solution(2900735150658707794)
XLA Ops:
  3.3 3.6 %collective-permute-start.1 = (bf16[1,4,1,4,512]{4,3,2,1,0:T(4,128)(2,1)S(1)}, bf16[1,4,1,4,512]{4,3,2,1,0:T(4,128)(2,1)S(1)}, u32[]{:S(2)}, u32[]{:S(2)}) collective-permute-start(bf16[1,4,1,4,512]{4,3,2,1,0:T(4,128)(2,1)S(1)} %get-tuple-element.67), channel_id=1, source_target_pairs={{32,0},{64,32},{96,64},{128,96},{160,128},{192,160},{224,192},{256... | collective-permute-start | bytes 49160 | tf_op jit(solution)/shard_map/ppermute | solution.py:18
  8.5 3.5 %collective-permute-start.2 = (bf16[1,4,6,1,512]{4,3,2,1,0:T(2,128)(2,1)S(1)}, bf16[1,4,6,1,512]{4,3,2,1,0:T(2,128)(2,1)S(1)}, u32[]{:S(2)}, u32[]{:S(2)}) collective-permute-start(bf16[1,4,6,1,512]{4,3,2,1,0:T(2,128)(2,1)S(1)} %get-tuple-element.65), channel_id=1, source_target_pairs={{0,4},{4,8},{8,12},{12,16},{16,20},{20,24},{24,28},{1,5},{5,9},{9,... | collective-permute-start | bytes 73736 | tf_op jit(solution)/shard_map/ppermute | solution.py:15
  14.1 3.8 %collective-permute-done.3 = bf16[1,4,6,1,512]{4,3,2,1,0:T(2,128)(2,1)S(1)} collective-permute-done((bf16[1,4,6,1,512]{4,3,2,1,0:T(2,128)(2,1)S(1)}, bf16[1,4,6,1,512]{4,3,2,1,0:T(2,128)(2,1)S(1)}, u32[]{:S(2)}, u32[]{:S(2)}) %collective-permute-start.3) | collective-permute-done | bytes 24608 | tf_op jit(solution)/shard_map/ppermute | solution.py:18
  20.3 10.9 %fusion.17 = f32[4,4,8,65,32]{4,2,3,1,0:T(8,128)} fusion(bf16[4,6,6,1,7,2]{4,0,5,2,1,3:T(4,128)(2,1)S(1)} %slice.127, bf16[4,6,6,1,8,65]{4,0,5,2,1,3:T(4,128)(2,1)S(1)} %copy.515, bf16[32,4,3,3,3]{0,4,3,2,1:T(4,128)(2,1)S(1)} %reshape.101), kind=kOutput, calls=%fused_computation.20 | convolution fusion | flops 57970944 | bytes 1225664 | tf_op jit(solution)/shard_map/conv_general_dilated | solution.py:118
  31.2 3.7 %copy.518 = f32[4,4,8,65,32]{3,4,2,1,0:T(8,128)S(1)} copy(f32[4,4,8,65,32]{4,2,3,1,0:T(8,128)} %fusion.17) | data formatting | bytes 2129920 | tf_op jit(solution)/shard_map/conv_general_dilated | solution.py:118
  41.0 2.6 %copy.520 = f32[1,32,4,4,512]{1,4,3,2,0:T(8,128)} copy(f32[1,32,4,4,512]{4,1,3,2,0:T(8,128)S(1)} %slice_bitcast_fusion.3) | data formatting | bytes 2097152 | tf_op jit(solution)/shard_map/add | solution.py:99
  43.7 4.8 %reduce_sum.21 = f32[32,2,2,256]{0,3,2,1:T(8,128)S(1)} reduce(f32[32,2,2,2,2,256,2]{0,6,5,4,3,2,1:T(2,128)} %bitcast.179, f32[]{:T(128)} %constant.71.clone.1), dimensions={2,4,6}, to_apply=%region_0.1 | reduce | flops 229376 | bytes 1179652 | tf_op jit(solution)/shard_map/reduce_sum | solution.py:109
  48.7 26.5 %all-gather = bf16[32,2,16,256]{3,0,2,1:T(8,128)(2,1)S(1)} all-gather(bf16[32,2,2,256]{3,0,2,1:T(8,128)(2,1)S(1)} %multiply_convert_fusion.1), channel_id=2, replica_groups=mesh['depth'=16,'height'=8,'sample'=4] {'height'}, dimensions={2}, use_global_device_ids=true | all-gather | bytes 589824 | tf_op jit(solution)/shard_map/all_gather | solution.py:155
  77.1 3.6 %collective-permute-start.5 = (bf16[1,32,1,16,256]{4,1,3,2,0:T(8,128)(2,1)S(1)}, bf16[1,32,1,16,256]{4,1,3,2,0:T(8,128)(2,1)}, u32[]{:S(2)}, u32[]{:S(2)}) collective-permute-start(bf16[1,32,1,16,256]{4,1,3,2,0:T(8,128)(2,1)S(1)} %get-tuple-element.54), channel_id=1, source_target_pairs={{32,0},{64,32},{96,64},{128,96},{160,128},{192,160},{224,192},{256... | collective-permute-start | bytes 786440 | tf_op jit(solution)/shard_map/ppermute | solution.py:18
  86.4 4.7 %reshape.138 = bf16[32,4,16,1,8,33]{5,4,0,2,1,3:T(8,128)(2,1)} reshape(bf16[32,4,16,1,264]{4,0,2,1,3:T(8,128)(2,1)S(1)} %pad.16) | data formatting | bytes 2162688 | tf_op jit(solution)/shard_map/conv_general_dilated | solution.py:118
  91.1 8.5 %copy.524 = bf16[32,4,16,1,8,33]{0,4,5,2,1,3:T(8,128)(2,1)} copy(bf16[32,4,16,1,8,33]{5,4,0,2,1,3:T(8,128)(2,1)} %reshape.138) | data formatting | bytes 2162688 | tf_op jit(solution)/shard_map/conv_general_dilated | solution.py:118
  100.7 10.1 %fusion.4 = f32[2,16,8,33,8]{4,2,3,1,0:T(8,128)} fusion(bf16[32,4,16,1,7,2]{0,4,5,2,1,3:T(8,128)(2,1)S(1)} %slice.131, bf16[32,4,16,1,8,33]{0,4,5,2,1,3:T(8,128)(2,1)} %copy.524, bf16[8,32,3,3,3]{0,4,3,2,1:T(4,128)(2,1)S(1)} %reshape.103), kind=kOutput, calls=%fused_computation.7 | convolution fusion | flops 115359744 | bytes 1422848 | tf_op jit(solution)/shard_map/conv_general_dilated | solution.py:118
  110.8 3.4 %copy.527 = f32[2,16,8,33,8]{3,4,2,1,0:T(8,128)S(1)} copy(f32[2,16,8,33,8]{4,2,3,1,0:T(8,128)} %fusion.4) | data formatting | bytes 540672 | tf_op jit(solution)/shard_map/conv_general_dilated | solution.py:118
  115.7 8.7 %collective-permute-start.12 = (bf16[1,8,1,16,256]{4,1,3,2,0:T(8,128)(2,1)S(1)}, bf16[1,8,1,16,256]{4,1,3,2,0:T(8,128)(2,1)S(1)}, u32[]{:S(2)}, u32[]{:S(2)}) collective-permute-start(bf16[1,8,1,16,256]{4,1,3,2,0:T(8,128)(2,1)S(1)} %get-tuple-element.55), channel_id=1, source_target_pairs={{0,32},{32,64},{64,96},{96,128},{128,160},{160,192},{192,224},{224... | collective-permute-start | bytes 196616 | tf_op jit(solution)/shard_map/ppermute | solution.py:15
  131.2 6.7 %collective-permute-start.14 = (f32[1,32,2,8,256]{4,1,3,2,0:T(8,128)}, f32[1,32,2,8,256]{4,1,3,2,0:T(8,128)}, u32[]{:S(2)}, u32[]{:S(2)}) collective-permute-start(f32[1,32,2,8,256]{4,1,3,2,0:T(8,128)} %dynamic-slice_bitcast_fusion), channel_id=1, source_target_pairs={{0,16},{4,20},{8,24},{12,28},{16,0},{20,4},{24,8},{28,12},{1,17},{... | collective-permute-start | bytes 1572872 | tf_op jit(solution)/shard_map/ppermute | solution.py:50
  142.6 10.7 %stack.84 = bf16[8,9,2,16,256]{4,1,3,2,0:T(8,128)(2,1)} concatenate(bf16[8,1,2,16,256]{4,1,3,2,0:T(2,128)(2,1)S(1)} %copy.542, bf16[8,1,2,16,256]{4,1,3,2,0:T(2,128)(2,1)S(1)} %copy.543, bf16[8,1,2,16,256]{4,1,3,2,0:T(2,128)(2,1)S(1)} %copy.544, bf16[8,1,2,16,256]{4,1,3,2,0:T(2,128)(2,1)S(1)} %copy.545, bf16[8,1,2,16,256]{4,1,3,2,0:T(2,128)(2,1)S(1)} %copy.546, ...), dimensions={1} | concatenate | bytes 2359296 | tf_op jit(solution)/shard_map/stack | solution.py:58
  153.3 4.0 %collective-permute-done.14 = f32[1,32,2,8,256]{4,1,3,2,0:T(8,128)} collective-permute-done((f32[1,32,2,8,256]{4,1,3,2,0:T(8,128)}, f32[1,32,2,8,256]{4,1,3,2,0:T(8,128)}, u32[]{:S(2)}, u32[]{:S(2)}) %collective-permute-start.14) | collective-permute-done | bytes 524320 | tf_op jit(solution)/shard_map/ppermute | solution.py:50
  159.4 9.4 %collective-permute-start.15 = (f32[1,32,2,4,256]{4,1,3,2,0:T(8,128)S(1)}, f32[1,32,2,4,256]{4,1,3,2,0:T(8,128)}, u32[]{:S(2)}, u32[]{:S(2)}) collective-permute-start(f32[1,32,2,4,256]{4,1,3,2,0:T(8,128)S(1)} %constant_dynamic-slice_fusion.1), channel_id=1, source_target_pairs={{0,8},{4,12},{8,0},{12,4},{16,24},{20,28},{24,16},{28,20},{1,9},{5... | collective-permute-start | bytes 786440 | tf_op jit(solution)/shard_map/ppermute | solution.py:50
  168.8 3.0 %fusion.41 = f32[8,9,3,32]{3,1,2,0:T(8,128)S(1)} fusion(bf16[1,32,1,16,256]{4,1,3,2,0:T(8,128)(2,1)} %collective-permute-done.5, bf16[1,32,2,16,256]{4,1,3,2,0:T(8,128)(2,1)S(1)} %bitcast.183, bf16[1,32,1,16,256]{4,1,3,2,0:T(8,128)(2,1)S(1)} %copy-done.5, bf16[8,9,2,16,256]{4,1,3,2,0:T(8,128)(2,1)} %stack.84), kind=kOutput, calls=%fused_computation.40 | convolution fusion | flops 121117440 | bytes 2255872 | tf_op jit(solution)/shard_map/dot_general | solution.py:72
  174.1 6.1 %collective-permute-start.6 = (f32[54,128]{1,0:T(8,128)S(1)}, f32[54,128]{1,0:T(8,128)S(1)}, u32[]{:S(2)}, u32[]{:S(2)}) collective-permute-start(f32[54,128]{1,0:T(8,128)S(1)} %mul.97), channel_id=1, source_target_pairs={{0,1},{1,0},{2,3},{3,2},{32,33},{33,32},{34,35},{35,34},{64,65},{6... | collective-permute-start | bytes 82952 | tf_op jit(solution)/shard_map/ppermute | solution.py:33
  182.2 8.6 %collective-permute-start.7 = (f32[54,128]{1,0:T(8,128)S(1)}, f32[54,128]{1,0:T(8,128)S(1)}, u32[]{:S(2)}, u32[]{:S(2)}) collective-permute-start(f32[54,128]{1,0:T(8,128)S(1)} %add.88), channel_id=1, source_target_pairs={{0,2},{1,3},{2,0},{3,1},{32,34},{33,35},{34,32},{35,33},{64,66},{6... | collective-permute-start | bytes 82952 | tf_op jit(solution)/shard_map/ppermute | solution.py:33
  198.2 3.3 %collective-permute-done.9 = f32[54,128]{1,0:T(8,128)S(1)} collective-permute-done((f32[54,128]{1,0:T(8,128)S(1)}, f32[54,128]{1,0:T(8,128)S(1)}, u32[]{:S(2)}, u32[]{:S(2)}) %collective-permute-start.9) | collective-permute-done | bytes 27680 | tf_op jit(solution)/shard_map/ppermute | solution.py:33
  205.8 3.0 %collective-permute-done.10 = f32[54,128]{1,0:T(8,128)S(1)} collective-permute-done((f32[54,128]{1,0:T(8,128)S(1)}, f32[54,128]{1,0:T(8,128)S(1)}, u32[]{:S(2)}, u32[]{:S(2)}) %collective-permute-start.10) | collective-permute-done | bytes 27680 | tf_op jit(solution)/shard_map/ppermute | solution.py:33
  215.2 3.4 %collective-permute-done.16 = f32[1,32,2,2,256]{4,1,3,2,0:T(8,128)S(1)} collective-permute-done((f32[1,32,2,2,256]{4,1,3,2,0:T(8,128)S(1)}, f32[1,32,2,2,256]{4,1,3,2,0:T(8,128)S(1)}, u32[]{:S(2)}, u32[]{:S(2)}) %collective-permute-start.16) | collective-permute-done | bytes 131104 | tf_op jit(solution)/shard_map/ppermute | solution.py:50
  (124 shorter events, 61.2 us)
Async XLA Ops:
  1.4 5.6 %collective-permute-start = (bf16[1,4,1,4,512]{4,3,2,1,0:T(4,128)(2,1)S(1)}, bf16[1,4,1,4,512]{4,3,2,1,0:T(4,128)(2,1)S(1)}, u32[]{:S(2)}, u32[]{:S(2)}) collective-permute-start(bf16[1,4,1,4,512]{4,3,2,1,0:T(4,128)(2,1)S(1)} %get-tuple-element.68), channel_id=1, source_target_pairs={{0,32},{32,64},{64,96},{96,128},{128,160},{160,192},{192,224},{224... | collective-permute-start | bytes 49160 | tf_op jit(solution)/shard_map/ppermute | solution.py:15
  3.3 5.1 %collective-permute-start.1 = (bf16[1,4,1,4,512]{4,3,2,1,0:T(4,128)(2,1)S(1)}, bf16[1,4,1,4,512]{4,3,2,1,0:T(4,128)(2,1)S(1)}, u32[]{:S(2)}, u32[]{:S(2)}) collective-permute-start(bf16[1,4,1,4,512]{4,3,2,1,0:T(4,128)(2,1)S(1)} %get-tuple-element.67), channel_id=1, source_target_pairs={{32,0},{64,32},{96,64},{128,96},{160,128},{192,160},{224,192},{256... | collective-permute-start | bytes 49160 | tf_op jit(solution)/shard_map/ppermute | solution.py:18
  8.5 5.6 %collective-permute-start.2 = (bf16[1,4,6,1,512]{4,3,2,1,0:T(2,128)(2,1)S(1)}, bf16[1,4,6,1,512]{4,3,2,1,0:T(2,128)(2,1)S(1)}, u32[]{:S(2)}, u32[]{:S(2)}) collective-permute-start(bf16[1,4,6,1,512]{4,3,2,1,0:T(2,128)(2,1)S(1)} %get-tuple-element.65), channel_id=1, source_target_pairs={{0,4},{4,8},{8,12},{12,16},{16,20},{20,24},{24,28},{1,5},{5,9},{9,... | collective-permute-start | bytes 73736 | tf_op jit(solution)/shard_map/ppermute | solution.py:15
  12.0 6.0 %collective-permute-start.3 = (bf16[1,4,6,1,512]{4,3,2,1,0:T(2,128)(2,1)S(1)}, bf16[1,4,6,1,512]{4,3,2,1,0:T(2,128)(2,1)S(1)}, u32[]{:S(2)}, u32[]{:S(2)}) collective-permute-start(bf16[1,4,6,1,512]{4,3,2,1,0:T(2,128)(2,1)S(1)} %get-tuple-element.66), channel_id=1, source_target_pairs={{4,0},{8,4},{12,8},{16,12},{20,16},{24,20},{28,24},{5,1},{9,5},{13... | collective-permute-start | bytes 73736 | tf_op jit(solution)/shard_map/ppermute | solution.py:18
  31.2 3.8 %copy-start.9 = (pred[8,65]{1,0:T(8,128)(4,1)S(1)}, pred[8,65]{1,0:T(8,128)(4,1)}, u32[]{:S(2)}) copy-start(pred[8,65]{1,0:T(8,128)(4,1)} %constant.102) | copy-start | bytes 1564
  48.4 32.3 %copy-start.7 = (bf16[8,864]{1,0:T(8,128)(2,1)S(1)}, bf16[8,864]{1,0:T(8,128)(2,1)}, u32[]{:S(2)}) copy-start(bf16[8,864]{1,0:T(8,128)(2,1)} %param.6) | copy-start | bytes 41476
  48.5 32.7 %copy-start.6 = (bf16[1,8,1,1024]{3,1,2,0:T(8,128)(2,1)S(1)}, bf16[1,8,1,1024]{3,1,2,0:T(8,128)(2,1)}, u32[]{:S(2)}) copy-start(bf16[1,8,1,1024]{3,1,2,0:T(8,128)(2,1)} %param.7) | copy-start | bytes 49156
  75.2 7.7 %collective-permute-start.4 = (bf16[1,32,1,16,256]{4,1,3,2,0:T(8,128)(2,1)S(1)}, bf16[1,32,1,16,256]{4,1,3,2,0:T(8,128)(2,1)S(1)}, u32[]{:S(2)}, u32[]{:S(2)}) collective-permute-start(bf16[1,32,1,16,256]{4,1,3,2,0:T(8,128)(2,1)S(1)} %get-tuple-element.53), channel_id=1, source_target_pairs={{0,32},{32,64},{64,96},{96,128},{128,160},{160,192},{192,224},{224... | collective-permute-start | bytes 786440 | tf_op jit(solution)/shard_map/ppermute | solution.py:15
  77.1 7.5 %collective-permute-start.5 = (bf16[1,32,1,16,256]{4,1,3,2,0:T(8,128)(2,1)S(1)}, bf16[1,32,1,16,256]{4,1,3,2,0:T(8,128)(2,1)}, u32[]{:S(2)}, u32[]{:S(2)}) collective-permute-start(bf16[1,32,1,16,256]{4,1,3,2,0:T(8,128)(2,1)S(1)} %get-tuple-element.54), channel_id=1, source_target_pairs={{32,0},{64,32},{96,64},{128,96},{160,128},{192,160},{224,192},{256... | collective-permute-start | bytes 786440 | tf_op jit(solution)/shard_map/ppermute | solution.py:18
  81.1 19.6 %copy-start.2 = (bf16[8,32,3,3,3]{0,4,3,2,1:T(4,128)(2,1)}, bf16[8,32,3,3,3]{0,4,3,2,1:T(4,128)(2,1)S(1)}, u32[]{:S(2)}) copy-start(bf16[8,32,3,3,3]{0,4,3,2,1:T(4,128)(2,1)S(1)} %reshape.103) | copy-start | bytes 41476
  115.7 12.0 %collective-permute-start.12 = (bf16[1,8,1,16,256]{4,1,3,2,0:T(8,128)(2,1)S(1)}, bf16[1,8,1,16,256]{4,1,3,2,0:T(8,128)(2,1)S(1)}, u32[]{:S(2)}, u32[]{:S(2)}) collective-permute-start(bf16[1,8,1,16,256]{4,1,3,2,0:T(8,128)(2,1)S(1)} %get-tuple-element.55), channel_id=1, source_target_pairs={{0,32},{32,64},{64,96},{96,128},{128,160},{160,192},{192,224},{224... | collective-permute-start | bytes 196616 | tf_op jit(solution)/shard_map/ppermute | solution.py:15
  124.4 3.8 %collective-permute-start.13 = (bf16[1,8,1,16,256]{4,1,3,2,0:T(8,128)(2,1)S(1)}, bf16[1,8,1,16,256]{4,1,3,2,0:T(8,128)(2,1)S(1)}, u32[]{:S(2)}, u32[]{:S(2)}) collective-permute-start(bf16[1,8,1,16,256]{4,1,3,2,0:T(8,128)(2,1)S(1)} %get-tuple-element.56), channel_id=1, source_target_pairs={{32,0},{64,32},{96,64},{128,96},{160,128},{192,160},{224,192},{256... | collective-permute-start | bytes 196616 | tf_op jit(solution)/shard_map/ppermute | solution.py:18
  130.3 9.2 %copy-start.3 = (f32[2,16,256,32]{2,3,1,0:T(8,128)}, f32[2,16,256,32]{2,3,1,0:T(8,128)S(1)}, u32[]{:S(2)}) copy-start(f32[2,16,256,32]{2,3,1,0:T(8,128)S(1)} %fusion.32) | copy-start | bytes 3145732
  131.2 26.1 %collective-permute-start.14 = (f32[1,32,2,8,256]{4,1,3,2,0:T(8,128)}, f32[1,32,2,8,256]{4,1,3,2,0:T(8,128)}, u32[]{:S(2)}, u32[]{:S(2)}) collective-permute-start(f32[1,32,2,8,256]{4,1,3,2,0:T(8,128)} %dynamic-slice_bitcast_fusion), channel_id=1, source_target_pairs={{0,16},{4,20},{8,24},{12,28},{16,0},{20,4},{24,8},{28,12},{1,17},{... | collective-permute-start | bytes 1572872 | tf_op jit(solution)/shard_map/ppermute | solution.py:50
  142.6 26.2 %copy-start.5 = (bf16[1,32,1,16,256]{4,1,3,2,0:T(8,128)(2,1)S(1)}, bf16[1,32,1,16,256]{4,1,3,2,0:T(8,128)(2,1)}, u32[]{:S(2)}) copy-start(bf16[1,32,1,16,256]{4,1,3,2,0:T(8,128)(2,1)} %copy-done.4) | copy-start | bytes 786436
  159.4 51.3 %collective-permute-start.15 = (f32[1,32,2,4,256]{4,1,3,2,0:T(8,128)S(1)}, f32[1,32,2,4,256]{4,1,3,2,0:T(8,128)}, u32[]{:S(2)}, u32[]{:S(2)}) collective-permute-start(f32[1,32,2,4,256]{4,1,3,2,0:T(8,128)S(1)} %constant_dynamic-slice_fusion.1), channel_id=1, source_target_pairs={{0,8},{4,12},{8,0},{12,4},{16,24},{20,28},{24,16},{28,20},{1,9},{5... | collective-permute-start | bytes 786440 | tf_op jit(solution)/shard_map/ppermute | solution.py:50
  174.1 8.1 %collective-permute-start.6 = (f32[54,128]{1,0:T(8,128)S(1)}, f32[54,128]{1,0:T(8,128)S(1)}, u32[]{:S(2)}, u32[]{:S(2)}) collective-permute-start(f32[54,128]{1,0:T(8,128)S(1)} %mul.97), channel_id=1, source_target_pairs={{0,1},{1,0},{2,3},{3,2},{32,33},{33,32},{34,35},{35,34},{64,65},{6... | collective-permute-start | bytes 82952 | tf_op jit(solution)/shard_map/ppermute | solution.py:33
  182.2 10.4 %collective-permute-start.7 = (f32[54,128]{1,0:T(8,128)S(1)}, f32[54,128]{1,0:T(8,128)S(1)}, u32[]{:S(2)}, u32[]{:S(2)}) collective-permute-start(f32[54,128]{1,0:T(8,128)S(1)} %add.88), channel_id=1, source_target_pairs={{0,2},{1,3},{2,0},{3,1},{32,34},{33,35},{34,32},{35,33},{64,66},{6... | collective-permute-start | bytes 82952 | tf_op jit(solution)/shard_map/ppermute | solution.py:33
  192.7 3.1 %collective-permute-start.8 = (f32[54,128]{1,0:T(8,128)S(1)}, f32[54,128]{1,0:T(8,128)S(1)}, u32[]{:S(2)}, u32[]{:S(2)}) collective-permute-start(f32[54,128]{1,0:T(8,128)S(1)} %add.89), channel_id=1, source_target_pairs={{0,32},{1,33},{2,34},{3,35},{32,0},{33,1},{34,2},{35,3},{64,96},{6... | collective-permute-start | bytes 82952 | tf_op jit(solution)/shard_map/ppermute | solution.py:33
  195.7 5.8 %collective-permute-start.9 = (f32[54,128]{1,0:T(8,128)S(1)}, f32[54,128]{1,0:T(8,128)S(1)}, u32[]{:S(2)}, u32[]{:S(2)}) collective-permute-start(f32[54,128]{1,0:T(8,128)S(1)} %add.90), channel_id=1, source_target_pairs={{0,64},{1,65},{2,66},{3,67},{32,96},{33,97},{34,98},{35,99},{64,0}... | collective-permute-start | bytes 82952 | tf_op jit(solution)/shard_map/ppermute | solution.py:33
  201.5 7.3 %collective-permute-start.10 = (f32[54,128]{1,0:T(8,128)S(1)}, f32[54,128]{1,0:T(8,128)S(1)}, u32[]{:S(2)}, u32[]{:S(2)}) collective-permute-start(f32[54,128]{1,0:T(8,128)S(1)} %add.91), channel_id=1, source_target_pairs={{0,128},{1,129},{2,130},{3,131},{32,160},{33,161},{34,162},{35,163... | collective-permute-start | bytes 82952 | tf_op jit(solution)/shard_map/ppermute | solution.py:33
  203.4 7.3 %copy-start.1 = (f32[1,32,2,8,256]{4,1,3,2,0:T(8,128)S(1)}, f32[1,32,2,8,256]{4,1,3,2,0:T(8,128)}, u32[]{:S(2)}) copy-start(f32[1,32,2,8,256]{4,1,3,2,0:T(8,128)} %copy-done) | copy-start | bytes 1572868
  208.8 5.8 %collective-permute-start.11 = (f32[54,128]{1,0:T(8,128)S(1)}, f32[54,128]{1,0:T(8,128)S(1)}, u32[]{:S(2)}, u32[]{:S(2)}) collective-permute-start(f32[54,128]{1,0:T(8,128)S(1)} %add.92), channel_id=1, source_target_pairs={{0,256},{1,257},{2,258},{3,259},{32,288},{33,289},{34,290},{35,291... | collective-permute-start | bytes 82952 | tf_op jit(solution)/shard_map/ppermute | solution.py:33
  211.7 6.9 %collective-permute-start.16 = (f32[1,32,2,2,256]{4,1,3,2,0:T(8,128)S(1)}, f32[1,32,2,2,256]{4,1,3,2,0:T(8,128)S(1)}, u32[]{:S(2)}, u32[]{:S(2)}) collective-permute-start(f32[1,32,2,2,256]{4,1,3,2,0:T(8,128)S(1)} %constant_dynamic-slice_fusion), channel_id=1, source_target_pairs={{0,4},{4,0},{8,12},{12,8},{16,20},{20,16},{24,28},{28,24},{1,5},{5... | collective-permute-start | bytes 393224 | tf_op jit(solution)/shard_map/ppermute | solution.py:50
  (3 other events, 7.7 us)
where the time goes:
time: 221 us; the launch traced here: 219 us
  starting transfers between devices  67 us (30%)
  local copies, waits for them, and re-layouts  60.6 us (27%)
  blocking collectives  26.5 us (12%)
  waiting for transfers between devices  26.3 us (12%)
  matrix products  24.9 us (11%)
  other arithmetic  12.5 us (6%)
    all_gather x1, blocking collectives, shards(): slab_rows = lax.all_gather(level_loc, 'height', axis=3, tiled=True)  26.5 us
    conv_general_dilated x8, local copies, waits for them, and re-layouts, conv_valid(): lax.conv_general_dilated(inputs, kernel, (1, 1, 1), 'VALID', dimension_nu...  23.4 us
    ppermute x6, starting transfers between devices, butterfly_sum(): values = values + lax.ppermute(values, axes, pairs)  22.3 us
    conv_general_dilated x2, matrix products, conv_valid(): lax.conv_general_dilated(inputs, kernel, (1, 1, 1), 'VALID', dimension_nu...  21 us
    ppermute x3, starting transfers between devices, halving_scatter(): values = keep + lax.ppermute(send, axis, pairs)  18 us
    ppermute x4, starting transfers between devices, extended(): lax.ppermute(lax.slice_in_dim(block, block.shape[dim] - width, None, axis...  16 us
    another operation x12, local copies, waits for them, and re-layouts, delta_shifts(): jnp.stack([dpad[:, :, 2 - kh:2 - kh + hsize, 2 - kw:2 - kw + wsize] for k...  15.4 us
    ppermute x6, waiting for transfers between devices, butterfly_sum(): values = values + lax.ppermute(values, axes, pairs)  11.4 us
  transfers between devices with their start and end apart: 17, of which 13 were waited for; matrix products, arithmetic and copies ran while one was open for 14% of the time, Pallas kernels for 0%

commit v1 on v0

--- a/solution.py
+++ b/solution.py
@@ -86,6 +86,22 @@
         [shifts_ext[:, :, 2 - kd : 2 - kd + dsize] for kd in range(3)], axis=0
     )
     weights = jnp.transpose(kernel, (1, 2, 0, 3, 4)).reshape(chans, 3, filters, 9)
+    grad = lax.dot_general(
+        weights,
+        stacked,
+        (((1, 2, 3), (0, 1, 2)), ((), ())),
+        preferred_element_type=jnp.float32,
+    )
+    return grad[None]
+
+
+def forward_product(level_ext, kernel):
+    filters, chans = kernel.shape[:2]
+    dsize = level_ext.shape[2] - 2
+    shifts = delta_shifts(level_ext)
+    stacked = jnp.stack([shifts[:, :, kd : kd + dsize] for kd in range(3)], axis=0)
+    flipped = jnp.flip(kernel, axis=(3, 4))
+    weights = jnp.transpose(flipped, (0, 2, 1, 3, 4)).reshape(filters, 3, chans, 9)
     grad = lax.dot_general(
         weights,
         stacked,
@@ -154,8 +170,7 @@
     level_loc = pooled(activate(conv_valid(window, first_kernel))).astype(jnp.bfloat16)
     slab_rows = lax.all_gather(level_loc, "height", axis=3, tiled=True)
     level_one = extended(slab_rows, (("depth", 2),), 1)
-    level_pad = jnp.pad(level_one, ((0, 0), (0, 0), (0, 0), (1, 1), (1, 1)))
-    pre_two = conv_valid(level_pad, second_kernel)
+    pre_two = forward_product(level_one, second_kernel)
     pooled_grid = pooled(activate(pre_two)).astype(jnp.bfloat16)
     depth_two = pooled_grid.shape[2]
     pooled_two = pooled_grid.reshape(

time: 221 us -> 194 us (0.88)
  local copies, waits for them, and re-layouts: 60.6 us -> 32.4 us
  waiting for transfers between devices: 26.3 us -> 40.8 us
  matrix products: 24.9 us -> 15.7 us
  other arithmetic: 12.5 us -> 9.45 us
    conv_general_dilated x8 -> x4, local copies, waits for them, and re-layouts: 23.4 us -> 5.71 us  [conv_valid(): lax.conv_general_dilated(inputs, kernel, (1, 1, 1), 'VALID', dimension_nu...]
    another operation x12 -> x3, local copies, waits for them, and re-layouts: 15.4 us -> 0.66 us  [delta_shifts(): jnp.stack([dpad[:, :, 2 - kh:2 - kh + hsize, 2 - kw:2 - kw + wsize] for k...]
    ppermute x3, waiting for transfers between devices: 7.37 us -> 22.1 us  [halving_scatter(): values = keep + lax.ppermute(send, axis, pairs)]
    conv_general_dilated x2 -> x1, matrix products: 21 us -> 10.9 us  [conv_valid(): lax.conv_general_dilated(inputs, kernel, (1, 1, 1), 'VALID', dimension_nu...]
    another operation x0 -> x1, local copies, waits for them, and re-layouts: none -> 2.75 us  [forward_product(): jnp.stack([shifts[:, :, kd:kd + dsize] for kd in range(3)], axis=0)]
    dot_general x0 -> x1, matrix products: none -> 2.65 us  [forward_product(): lax.dot_general(weights, stacked, (((1, 2, 3), (0, 1, 2)), ((), ())), pre...]
    unnamed x33 -> x40, local copies, waits for them, and re-layouts: 4.84 us -> 6.86 us
    add x6 -> x4, local copies, waits for them, and re-layouts: 7.86 us -> 7.36 us  [activate(): return LEAK_SLOPE * values + (1.0 - LEAK_SLOPE) * jax.nn.softplus(values)]
  transfers between devices with their start and end apart: 17 -> 17, of which waited for: 13 -> 12; matrix products, arithmetic and copies ran while one was open for 14% -> 7% of each run, Pallas kernels for 0% -> 0%
where the time goes in v1:
time: 194 us; the launch traced here: 193 us
  starting transfers between devices  67 us (35%)
  waiting for transfers between devices  40.8 us (21%)
  local copies, waits for them, and re-layouts  32.4 us (17%)
  blocking collectives  26.5 us (14%)
  matrix products  15.7 us (8%)
  other arithmetic  9.45 us (5%)
    all_gather x1, blocking collectives, shards(): slab_rows = lax.all_gather(level_loc, 'height', axis=3, tiled=True)  26.5 us
    ppermute x6, starting transfers between devices, butterfly_sum(): values = values + lax.ppermute(values, axes, pairs)  22.5 us
    ppermute x3, waiting for transfers between devices, halving_scatter(): values = keep + lax.ppermute(send, axis, pairs)  22.1 us
    ppermute x3, starting transfers between devices, halving_scatter(): values = keep + lax.ppermute(send, axis, pairs)  18.1 us
    ppermute x4, starting transfers between devices, extended(): lax.ppermute(lax.slice_in_dim(block, block.shape[dim] - width, None, axis...  15.9 us
    ppermute x6, waiting for transfers between devices, butterfly_sum(): values = values + lax.ppermute(values, axes, pairs)  11.7 us
    conv_general_dilated x1, matrix products, conv_valid(): lax.conv_general_dilated(inputs, kernel, (1, 1, 1), 'VALID', dimension_nu...  10.9 us
    ppermute x4, starting transfers between devices, extended(): lax.ppermute(lax.slice_in_dim(block, 0, width, axis=dim), axis, backward)  10.5 us
  transfers between devices with their start and end apart: 17, of which 12 were waited for; matrix products, arithmetic and copies ran while one was open for 7% of the time, Pallas kernels for 0%

profile of v1, /device:TPU:6, one launch (start us, length us, event | category | flops | bytes accessed | tf_op | source)
XLA Modules:
  0.0 193.3 jit_solution(8223023339156268502)
XLA Ops:
  1.4 1.9 collective-permute-start
  3.3 3.6 %collective-permute-start.1 = (bf16[1,4,1,4,512]{4,3,2,1,0:T(4,128)(2,1)S(1)}, bf16[1,4,1,4,512]{4,3,2,1,0:T(4,128)(2,1)S(1)}, u32[]{:S(2)}, u32[]{:S(2)}) collective-permute-start(bf16[1,4,1,4,512]{4,3,2,1,0:T(4,128)(2,1)S(1)} %get-tuple-element.35), channel_id=1, source_target_pairs={{32,0},{64,32},{96,64},{128,96},{160,128},{192,160},{224,192},{256... | collective-permute-start | bytes 49160 | tf_op jit(solution)/shard_map/ppermute | solution.py:18
  8.5 3.5 %collective-permute-start.2 = (bf16[1,4,6,1,512]{4,3,2,1,0:T(2,128)(2,1)S(1)}, bf16[1,4,6,1,512]{4,3,2,1,0:T(2,128)(2,1)S(1)}, u32[]{:S(2)}, u32[]{:S(2)}) collective-permute-start(bf16[1,4,6,1,512]{4,3,2,1,0:T(2,128)(2,1)S(1)} %get-tuple-element.33), channel_id=1, source_target_pairs={{0,4},{4,8},{8,12},{12,16},{16,20},{20,24},{24,28},{1,5},{5,9},{9,... | collective-permute-start | bytes 73736 | tf_op jit(solution)/shard_map/ppermute | solution.py:15
  14.1 3.8 %collective-permute-done.3 = bf16[1,4,6,1,512]{4,3,2,1,0:T(2,128)(2,1)S(1)} collective-permute-done((bf16[1,4,6,1,512]{4,3,2,1,0:T(2,128)(2,1)S(1)}, bf16[1,4,6,1,512]{4,3,2,1,0:T(2,128)(2,1)S(1)}, u32[]{:S(2)}, u32[]{:S(2)}) %collective-permute-start.3) | collective-permute-done | bytes 24608 | tf_op jit(solution)/shard_map/ppermute | solution.py:18
  20.3 10.9 %fusion.15 = f32[4,4,8,65,32]{4,2,3,1,0:T(8,128)} fusion(bf16[4,6,6,1,7,2]{4,0,5,2,1,3:T(4,128)(2,1)S(1)} %slice.169, bf16[4,6,6,1,8,65]{4,0,5,2,1,3:T(4,128)(2,1)S(1)} %copy.131, bf16[32,4,3,3,3]{0,4,3,2,1:T(4,128)(2,1)S(1)} %reshape.120), kind=kOutput, calls=%fused_computation.28 | convolution fusion | flops 57970944 | bytes 1225664 | tf_op jit(solution)/shard_map/conv_general_dilated | solution.py:134
  31.2 3.7 %copy.134 = f32[4,4,8,65,32]{3,4,2,1,0:T(8,128)S(1)} copy(f32[4,4,8,65,32]{4,2,3,1,0:T(8,128)} %fusion.15) | data formatting | bytes 2129920 | tf_op jit(solution)/shard_map/conv_general_dilated | solution.py:134
  41.0 2.6 %copy.136 = f32[1,32,4,4,512]{1,4,3,2,0:T(8,128)} copy(f32[1,32,4,4,512]{4,1,3,2,0:T(8,128)S(1)} %slice_bitcast_fusion.6) | data formatting | bytes 2097152 | tf_op jit(solution)/shard_map/add | solution.py:115
  43.7 4.8 %reduce_sum.21 = f32[32,2,2,256]{0,3,2,1:T(8,128)S(1)} reduce(f32[32,2,2,2,2,256,2]{0,6,5,4,3,2,1:T(2,128)} %bitcast.224, f32[]{:T(128)} %constant.71.clone.1), dimensions={2,4,6}, to_apply=%region_0.1 | reduce | flops 229376 | bytes 1179652 | tf_op jit(solution)/shard_map/reduce_sum | solution.py:125
  48.7 26.5 %all-gather = bf16[32,2,16,256]{3,0,2,1:T(8,128)(2,1)S(1)} all-gather(bf16[32,2,2,256]{3,0,2,1:T(8,128)(2,1)S(1)} %multiply_convert_fusion.2), channel_id=2, replica_groups=mesh['depth'=16,'height'=8,'sample'=4] {'height'}, dimensions={2}, use_global_device_ids=true | all-gather | bytes 589824 | tf_op jit(solution)/shard_map/all_gather | solution.py:171
  77.8 3.6 %collective-permute-start.5 = (bf16[1,32,1,16,256]{4,1,3,2,0:T(8,128)(2,1)S(1)}, bf16[1,32,1,16,256]{4,1,3,2,0:T(8,128)(2,1)S(1)}, u32[]{:S(2)}, u32[]{:S(2)}) collective-permute-start(bf16[1,32,1,16,256]{4,1,3,2,0:T(8,128)(2,1)S(1)} %get-tuple-element.28), channel_id=1, source_target_pairs={{32,0},{64,32},{96,64},{128,96},{160,128},{192,160},{224,192},{256... | collective-permute-start | bytes 786440 | tf_op jit(solution)/shard_map/ppermute | solution.py:18
  88.3 2.8 %slice_bitcast_fusion.2 = (bf16[1,32,9,2,16,256]{5,1,2,0,4,3:T(8,128)(2,1)S(1)}, bf16[1,32,9,2,16,256]{5,1,2,0,4,3:T(8,128)(2,1)S(1)}, bf16[1,32,9,2,16,256]{5,1,2,0,4,3:T(8,128)(2,1)S(1)}) fusion(bf16[32,9,4,16,256]{4,0,1,3,2:T(8,128)(2,1)S(1)} %fusion.61), kind=kLoop, calls=%fused_computation.11 | loop fusion | bytes 28311552 | tf_op jit(solution)/shard_map/stack | solution.py:102
  91.1 2.6 %multiply_convert_fusion.1 = (bf16[8,2,16,256]{3,0,2,1:T(8,128)(2,1)S(1)}, f32[8,16,256]{2,0,1:T(8,128)S(1)}) fusion(f32[8,16,256]{2,0,1:T(8,128)S(1)} %copy.152, bf16[8,3,32,9,1,1]{2,0,3,1,5,4:T(8,128)(2,1)S(1)} %bitcast.237, bf16[1,32,9,2,16,256]{5,1,2,0,4,3:T(8,128)(2,1)S(1)} %get-tuple-element.22, ...), kind=kOutput, calls=%fused_computation.111 | convolution fusion | flops 128483328 | bytes 14562816 | tf_op jit(solution)/shard_map/dot_general | solution.py:105
  93.9 8.6 %collective-permute-start.12 = (bf16[1,8,1,16,256]{4,1,3,2,0:T(8,128)(2,1)S(1)}, bf16[1,8,1,16,256]{4,1,3,2,0:T(8,128)(2,1)S(1)}, u32[]{:S(2)}, u32[]{:S(2)}) collective-permute-start(bf16[1,8,1,16,256]{4,1,3,2,0:T(8,128)(2,1)S(1)} %get-tuple-element.31), channel_id=1, source_target_pairs={{0,32},{32,64},{64,96},{96,128},{128,160},{160,192},{192,224},{224... | collective-permute-start | bytes 196616 | tf_op jit(solution)/shard_map/ppermute | solution.py:15
  102.4 1.9 collective-permute-start.13
  108.6 6.8 %collective-permute-start.14 = (f32[1,32,2,8,256]{4,1,3,2,0:T(8,128)S(1)}, f32[1,32,2,8,256]{4,1,3,2,0:T(8,128)S(1)}, u32[]{:S(2)}, u32[]{:S(2)}) collective-permute-start(f32[1,32,2,8,256]{4,1,3,2,0:T(8,128)S(1)} %dynamic-slice_bitcast_fusion), channel_id=1, source_target_pairs={{0,16},{4,20},{8,24},{12,28},{16,0},{20,4},{24,8},{28,12},{1,17},{... | collective-permute-start | bytes 1572872 | tf_op jit(solution)/shard_map/ppermute | solution.py:50
  115.8 18.8 %collective-permute-done.14 = f32[1,32,2,8,256]{4,1,3,2,0:T(8,128)S(1)} collective-permute-done((f32[1,32,2,8,256]{4,1,3,2,0:T(8,128)S(1)}, f32[1,32,2,8,256]{4,1,3,2,0:T(8,128)S(1)}, u32[]{:S(2)}, u32[]{:S(2)}) %collective-permute-start.14) | collective-permute-done | bytes 524320 | tf_op jit(solution)/shard_map/ppermute | solution.py:50
  135.3 9.4 %collective-permute-start.15 = (f32[1,32,2,4,256]{4,1,3,2,0:T(8,128)}, f32[1,32,2,4,256]{4,1,3,2,0:T(8,128)}, u32[]{:S(2)}, u32[]{:S(2)}) collective-permute-start(f32[1,32,2,4,256]{4,1,3,2,0:T(8,128)} %constant_dynamic-slice_fusion.1), channel_id=1, source_target_pairs={{0,8},{4,12},{8,0},{12,4},{16,24},{20,28},{24,16},{28,20},{1,9},{5... | collective-permute-start | bytes 786440 | tf_op jit(solution)/shard_map/ppermute | solution.py:50
  148.2 6.1 %collective-permute-start.6 = (f32[54,128]{1,0:T(8,128)S(1)}, f32[54,128]{1,0:T(8,128)S(1)}, u32[]{:S(2)}, u32[]{:S(2)}) collective-permute-start(f32[54,128]{1,0:T(8,128)S(1)} %mul.98), channel_id=1, source_target_pairs={{0,1},{1,0},{2,3},{3,2},{32,33},{33,32},{34,35},{35,34},{64,65},{6... | collective-permute-start | bytes 82952 | tf_op jit(solution)/shard_map/ppermute | solution.py:33
  154.2 2.0 %collective-permute-done.6 = f32[54,128]{1,0:T(8,128)S(1)} collective-permute-done((f32[54,128]{1,0:T(8,128)S(1)}, f32[54,128]{1,0:T(8,128)S(1)}, u32[]{:S(2)}, u32[]{:S(2)}) %collective-permute-start.6) | collective-permute-done | bytes 27680 | tf_op jit(solution)/shard_map/ppermute | solution.py:33
  156.3 8.6 %collective-permute-start.7 = (f32[54,128]{1,0:T(8,128)S(1)}, f32[54,128]{1,0:T(8,128)S(1)}, u32[]{:S(2)}, u32[]{:S(2)}) collective-permute-start(f32[54,128]{1,0:T(8,128)S(1)} %add.94), channel_id=1, source_target_pairs={{0,2},{1,3},{2,0},{3,1},{32,34},{33,35},{34,32},{35,33},{64,66},{6... | collective-permute-start | bytes 82952 | tf_op jit(solution)/shard_map/ppermute | solution.py:33
  171.7 3.8 %collective-permute-done.9 = f32[54,128]{1,0:T(8,128)S(1)} collective-permute-done((f32[54,128]{1,0:T(8,128)S(1)}, f32[54,128]{1,0:T(8,128)S(1)}, u32[]{:S(2)}, u32[]{:S(2)}) %collective-permute-start.9) | collective-permute-done | bytes 27680 | tf_op jit(solution)/shard_map/ppermute | solution.py:33
  175.6 2.1 %collective-permute-start.10 = (f32[54,128]{1,0:T(8,128)S(1)}, f32[54,128]{1,0:T(8,128)S(1)}, u32[]{:S(2)}, u32[]{:S(2)}) collective-permute-start(f32[54,128]{1,0:T(8,128)S(1)} %add.97), channel_id=1, source_target_pairs={{0,128},{1,129},{2,130},{3,131},{32,160},{33,161},{34,162},{35,163... | collective-permute-start | bytes 82952 | tf_op jit(solution)/shard_map/ppermute | solution.py:33
  180.0 2.8 %collective-permute-done.10 = f32[54,128]{1,0:T(8,128)S(1)} collective-permute-done((f32[54,128]{1,0:T(8,128)S(1)}, f32[54,128]{1,0:T(8,128)S(1)}, u32[]{:S(2)}, u32[]{:S(2)}) %collective-permute-start.10) | collective-permute-done | bytes 27680 | tf_op jit(solution)/shard_map/ppermute | solution.py:33
  189.3 3.4 %collective-permute-done.16 = f32[1,32,2,2,256]{4,1,3,2,0:T(8,128)S(1)} collective-permute-done((f32[1,32,2,2,256]{4,1,3,2,0:T(8,128)S(1)}, f32[1,32,2,2,256]{4,1,3,2,0:T(8,128)S(1)}, u32[]{:S(2)}, u32[]{:S(2)}) %collective-permute-start.16) | collective-permute-done | bytes 131104 | tf_op jit(solution)/shard_map/ppermute | solution.py:50
  (111 shorter events, 47.2 us)
Async XLA Ops:
  1.4 5.6 %collective-permute-start = (bf16[1,4,1,4,512]{4,3,2,1,0:T(4,128)(2,1)S(1)}, bf16[1,4,1,4,512]{4,3,2,1,0:T(4,128)(2,1)S(1)}, u32[]{:S(2)}, u32[]{:S(2)}) collective-permute-start(bf16[1,4,1,4,512]{4,3,2,1,0:T(4,128)(2,1)S(1)} %get-tuple-element.36), channel_id=1, source_target_pairs={{0,32},{32,64},{64,96},{96,128},{128,160},{160,192},{192,224},{224... | collective-permute-start | bytes 49160 | tf_op jit(solution)/shard_map/ppermute | solution.py:15
  3.3 5.1 %collective-permute-start.1 = (bf16[1,4,1,4,512]{4,3,2,1,0:T(4,128)(2,1)S(1)}, bf16[1,4,1,4,512]{4,3,2,1,0:T(4,128)(2,1)S(1)}, u32[]{:S(2)}, u32[]{:S(2)}) collective-permute-start(bf16[1,4,1,4,512]{4,3,2,1,0:T(4,128)(2,1)S(1)} %get-tuple-element.35), channel_id=1, source_target_pairs={{32,0},{64,32},{96,64},{128,96},{160,128},{192,160},{224,192},{256... | collective-permute-start | bytes 49160 | tf_op jit(solution)/shard_map/ppermute | solution.py:18
  8.5 5.6 %collective-permute-start.2 = (bf16[1,4,6,1,512]{4,3,2,1,0:T(2,128)(2,1)S(1)}, bf16[1,4,6,1,512]{4,3,2,1,0:T(2,128)(2,1)S(1)}, u32[]{:S(2)}, u32[]{:S(2)}) collective-permute-start(bf16[1,4,6,1,512]{4,3,2,1,0:T(2,128)(2,1)S(1)} %get-tuple-element.33), channel_id=1, source_target_pairs={{0,4},{4,8},{8,12},{12,16},{16,20},{20,24},{24,28},{1,5},{5,9},{9,... | collective-permute-start | bytes 73736 | tf_op jit(solution)/shard_map/ppermute | solution.py:15
  12.0 6.0 %collective-permute-start.3 = (bf16[1,4,6,1,512]{4,3,2,1,0:T(2,128)(2,1)S(1)}, bf16[1,4,6,1,512]{4,3,2,1,0:T(2,128)(2,1)S(1)}, u32[]{:S(2)}, u32[]{:S(2)}) collective-permute-start(bf16[1,4,6,1,512]{4,3,2,1,0:T(2,128)(2,1)S(1)} %get-tuple-element.34), channel_id=1, source_target_pairs={{4,0},{8,4},{12,8},{16,12},{20,16},{24,20},{28,24},{5,1},{9,5},{13... | collective-permute-start | bytes 73736 | tf_op jit(solution)/shard_map/ppermute | solution.py:18
  31.2 3.8 %copy-start.5 = (pred[8,65]{1,0:T(8,128)(4,1)S(1)}, pred[8,65]{1,0:T(8,128)(4,1)}, u32[]{:S(2)}) copy-start(pred[8,65]{1,0:T(8,128)(4,1)} %constant.99) | copy-start | bytes 1564
  48.5 33.1 %copy-start.4 = (bf16[8,864]{1,0:T(8,128)(2,1)S(1)}, bf16[8,864]{1,0:T(8,128)(2,1)}, u32[]{:S(2)}) copy-start(bf16[8,864]{1,0:T(8,128)(2,1)} %param.6) | copy-start | bytes 41476
  48.5 34.9 %copy-start.3 = (bf16[1,8,1,1024]{3,1,2,0:T(8,128)(2,1)S(1)}, bf16[1,8,1,1024]{3,1,2,0:T(8,128)(2,1)}, u32[]{:S(2)}) copy-start(bf16[1,8,1,1024]{3,1,2,0:T(8,128)(2,1)} %param.7) | copy-start | bytes 49156
  75.9 8.4 %collective-permute-start.4 = (bf16[1,32,1,16,256]{4,1,3,2,0:T(8,128)(2,1)}, bf16[1,32,1,16,256]{4,1,3,2,0:T(8,128)(2,1)S(1)}, u32[]{:S(2)}, u32[]{:S(2)}) collective-permute-start(bf16[1,32,1,16,256]{4,1,3,2,0:T(8,128)(2,1)} %get-tuple-element.27), channel_id=1, source_target_pairs={{0,32},{32,64},{64,96},{96,128},{128,160},{160,192},{192,224},{224... | collective-permute-start | bytes 786440 | tf_op jit(solution)/shard_map/ppermute | solution.py:15
  77.8 7.5 %collective-permute-start.5 = (bf16[1,32,1,16,256]{4,1,3,2,0:T(8,128)(2,1)S(1)}, bf16[1,32,1,16,256]{4,1,3,2,0:T(8,128)(2,1)S(1)}, u32[]{:S(2)}, u32[]{:S(2)}) collective-permute-start(bf16[1,32,1,16,256]{4,1,3,2,0:T(8,128)(2,1)S(1)} %get-tuple-element.28), channel_id=1, source_target_pairs={{32,0},{64,32},{96,64},{128,96},{160,128},{192,160},{224,192},{256... | collective-permute-start | bytes 786440 | tf_op jit(solution)/shard_map/ppermute | solution.py:18
  85.3 1.5 copy-start
  88.3 2.8 %copy-start.2 = (bf16[8,3,32,3,3]{2,0,4,3,1:T(8,128)(2,1)S(1)}, bf16[8,3,32,3,3]{2,0,4,3,1:T(8,128)(2,1)}, u32[]{:S(2)}) copy-start(bf16[8,3,32,3,3]{2,0,4,3,1:T(8,128)(2,1)} %copy.149) | copy-start | bytes 41476
  93.9 10.7 %collective-permute-start.12 = (bf16[1,8,1,16,256]{4,1,3,2,0:T(8,128)(2,1)S(1)}, bf16[1,8,1,16,256]{4,1,3,2,0:T(8,128)(2,1)S(1)}, u32[]{:S(2)}, u32[]{:S(2)}) collective-permute-start(bf16[1,8,1,16,256]{4,1,3,2,0:T(8,128)(2,1)S(1)} %get-tuple-element.31), channel_id=1, source_target_pairs={{0,32},{32,64},{64,96},{96,128},{128,160},{160,192},{192,224},{224... | collective-permute-start | bytes 196616 | tf_op jit(solution)/shard_map/ppermute | solution.py:15
  102.4 3.8 %collective-permute-start.13 = (bf16[1,8,1,16,256]{4,1,3,2,0:T(8,128)(2,1)S(1)}, bf16[1,8,1,16,256]{4,1,3,2,0:T(8,128)(2,1)S(1)}, u32[]{:S(2)}, u32[]{:S(2)}) collective-permute-start(bf16[1,8,1,16,256]{4,1,3,2,0:T(8,128)(2,1)S(1)} %get-tuple-element.32), channel_id=1, source_target_pairs={{32,0},{64,32},{96,64},{128,96},{160,128},{192,160},{224,192},{256... | collective-permute-start | bytes 196616 | tf_op jit(solution)/shard_map/ppermute | solution.py:18
  108.5 36.2 %copy-start.1 = (bf16[1,32,1,16,256]{4,1,3,2,0:T(8,128)(2,1)S(1)}, bf16[1,32,1,16,256]{4,1,3,2,0:T(8,128)(2,1)}, u32[]{:S(2)}) copy-start(bf16[1,32,1,16,256]{4,1,3,2,0:T(8,128)(2,1)} %copy-done) | copy-start | bytes 786436
  108.6 25.9 %collective-permute-start.14 = (f32[1,32,2,8,256]{4,1,3,2,0:T(8,128)S(1)}, f32[1,32,2,8,256]{4,1,3,2,0:T(8,128)S(1)}, u32[]{:S(2)}, u32[]{:S(2)}) collective-permute-start(f32[1,32,2,8,256]{4,1,3,2,0:T(8,128)S(1)} %dynamic-slice_bitcast_fusion), channel_id=1, source_target_pairs={{0,16},{4,20},{8,24},{12,28},{16,0},{20,4},{24,8},{28,12},{1,17},{... | collective-permute-start | bytes 1572872 | tf_op jit(solution)/shard_map/ppermute | solution.py:50
  135.3 49.4 %collective-permute-start.15 = (f32[1,32,2,4,256]{4,1,3,2,0:T(8,128)}, f32[1,32,2,4,256]{4,1,3,2,0:T(8,128)}, u32[]{:S(2)}, u32[]{:S(2)}) collective-permute-start(f32[1,32,2,4,256]{4,1,3,2,0:T(8,128)} %constant_dynamic-slice_fusion.1), channel_id=1, source_target_pairs={{0,8},{4,12},{8,0},{12,4},{16,24},{20,28},{24,16},{28,20},{1,9},{5... | collective-permute-start | bytes 786440 | tf_op jit(solution)/shard_map/ppermute | solution.py:50
  148.2 8.1 %collective-permute-start.6 = (f32[54,128]{1,0:T(8,128)S(1)}, f32[54,128]{1,0:T(8,128)S(1)}, u32[]{:S(2)}, u32[]{:S(2)}) collective-permute-start(f32[54,128]{1,0:T(8,128)S(1)} %mul.98), channel_id=1, source_target_pairs={{0,1},{1,0},{2,3},{3,2},{32,33},{33,32},{34,35},{35,34},{64,65},{6... | collective-permute-start | bytes 82952 | tf_op jit(solution)/shard_map/ppermute | solution.py:33
  156.3 10.4 %collective-permute-start.7 = (f32[54,128]{1,0:T(8,128)S(1)}, f32[54,128]{1,0:T(8,128)S(1)}, u32[]{:S(2)}, u32[]{:S(2)}) collective-permute-start(f32[54,128]{1,0:T(8,128)S(1)} %add.94), channel_id=1, source_target_pairs={{0,2},{1,3},{2,0},{3,1},{32,34},{33,35},{34,32},{35,33},{64,66},{6... | collective-permute-start | bytes 82952 | tf_op jit(solution)/shard_map/ppermute | solution.py:33
  166.7 3.1 %collective-permute-start.8 = (f32[54,128]{1,0:T(8,128)S(1)}, f32[54,128]{1,0:T(8,128)S(1)}, u32[]{:S(2)}, u32[]{:S(2)}) collective-permute-start(f32[54,128]{1,0:T(8,128)S(1)} %add.95), channel_id=1, source_target_pairs={{0,32},{1,33},{2,34},{3,35},{32,0},{33,1},{34,2},{35,3},{64,96},{6... | collective-permute-start | bytes 82952 | tf_op jit(solution)/shard_map/ppermute | solution.py:33
  169.8 5.8 %collective-permute-start.9 = (f32[54,128]{1,0:T(8,128)S(1)}, f32[54,128]{1,0:T(8,128)S(1)}, u32[]{:S(2)}, u32[]{:S(2)}) collective-permute-start(f32[54,128]{1,0:T(8,128)S(1)} %add.96), channel_id=1, source_target_pairs={{0,64},{1,65},{2,66},{3,67},{32,96},{33,97},{34,98},{35,99},{64,0}... | collective-permute-start | bytes 82952 | tf_op jit(solution)/shard_map/ppermute | solution.py:33
  175.6 7.3 %collective-permute-start.10 = (f32[54,128]{1,0:T(8,128)S(1)}, f32[54,128]{1,0:T(8,128)S(1)}, u32[]{:S(2)}, u32[]{:S(2)}) collective-permute-start(f32[54,128]{1,0:T(8,128)S(1)} %add.97), channel_id=1, source_target_pairs={{0,128},{1,129},{2,130},{3,131},{32,160},{33,161},{34,162},{35,163... | collective-permute-start | bytes 82952 | tf_op jit(solution)/shard_map/ppermute | solution.py:33
  182.8 5.8 %collective-permute-start.11 = (f32[54,128]{1,0:T(8,128)S(1)}, f32[54,128]{1,0:T(8,128)S(1)}, u32[]{:S(2)}, u32[]{:S(2)}) collective-permute-start(f32[54,128]{1,0:T(8,128)S(1)} %add.98), channel_id=1, source_target_pairs={{0,256},{1,257},{2,258},{3,259},{32,288},{33,289},{34,290},{35,291... | collective-permute-start | bytes 82952 | tf_op jit(solution)/shard_map/ppermute | solution.py:33
  185.8 6.9 %collective-permute-start.16 = (f32[1,32,2,2,256]{4,1,3,2,0:T(8,128)S(1)}, f32[1,32,2,2,256]{4,1,3,2,0:T(8,128)S(1)}, u32[]{:S(2)}, u32[]{:S(2)}) collective-permute-start(f32[1,32,2,2,256]{4,1,3,2,0:T(8,128)S(1)} %constant_dynamic-slice_fusion), channel_id=1, source_target_pairs={{0,4},{4,0},{8,12},{12,8},{16,20},{20,16},{24,28},{28,24},{1,5},{5... | collective-permute-start | bytes 393224 | tf_op jit(solution)/shard_map/ppermute | solution.py:50

commit v2 on v1

--- a/solution.py
+++ b/solution.py
@@ -109,6 +109,26 @@
         preferred_element_type=jnp.float32,
     )
     return grad[None]
+
+
+def near_first_scatter(values, axis):
+    count = lax.axis_size(axis)
+    chans, dsize, hsize, wsize = values.shape[1:]
+    if count & (count - 1):
+        return lax.psum_scatter(values, axis, scatter_dimension=3, tiled=True)
+    bits = count.bit_length() - 1
+    rows = hsize // count
+    index = lax.axis_index(axis)
+    grid = jnp.transpose(values[0], (2, 1, 0, 3))
+    grid = grid.reshape((2,) * bits + (rows, dsize, chans, wsize))
+    for t in range(bits):
+        axis_pos = bits - 1 - t
+        bit = (index >> t) & 1
+        keep = lax.dynamic_slice_in_dim(grid, bit, 1, axis=axis_pos)
+        send = lax.dynamic_slice_in_dim(grid, 1 - bit, 1, axis=axis_pos)
+        pairs = [(i, i ^ (1 << t)) for i in range(count)]
+        grid = jnp.squeeze(keep + lax.ppermute(send, axis, pairs), axis_pos)
+    return jnp.transpose(grid, (2, 1, 0, 3))[None]
 
 
 def activate(values):
@@ -195,7 +215,7 @@
         weight_term.reshape(flat_size // lanes, lanes), ("depth", "sample")
     ).reshape(weight_term.shape)
     back_part = back_product(shifts_ext, second_kernel)
-    act_grad = halving_scatter(back_part, "height", 3).astype(jnp.bfloat16)
+    act_grad = near_first_scatter(back_part, "height").astype(jnp.bfloat16)
     return (pooled_two, weight_grad, act_grad)
 
 

time: 194 us -> 186 us (0.959)
  the two profiles are of different devices: /device:TPU:6 before, /device:TPU:8 now
where the time goes in v2:
time: 186 us; the launch traced here: 185 us
  starting transfers between devices  64.5 us (35%)
  waiting for transfers between devices  33 us (18%)
  local copies, waits for them, and re-layouts  32.5 us (17%)
  blocking collectives  28.1 us (15%)
  matrix products  15.7 us (8%)
  other arithmetic  9.45 us (5%)
    ppermute x6, starting transfers between devices, butterfly_sum(): values = values + lax.ppermute(values, axes, pairs)  33.3 us
    all_gather x1, blocking collectives, shards(): slab_rows = lax.all_gather(level_loc, 'height', axis=3, tiled=True)  28.1 us
    ppermute x3, waiting for transfers between devices, near_first_scatter(): grid = jnp.squeeze(keep + lax.ppermute(send, axis, pairs), axis_pos)  19.4 us
    ppermute x4, starting transfers between devices, extended(): lax.ppermute(lax.slice_in_dim(block, block.shape[dim] - width, None, axis...  13.2 us
    conv_general_dilated x1, matrix products, conv_valid(): lax.conv_general_dilated(inputs, kernel, (1, 1, 1), 'VALID', dimension_nu...  10.9 us
    ppermute x3, starting transfers between devices, near_first_scatter(): grid = jnp.squeeze(keep + lax.ppermute(send, axis, pairs), axis_pos)  10.3 us
    ppermute x4, starting transfers between devices, extended(): lax.ppermute(lax.slice_in_dim(block, 0, width, axis=dim), axis, backward)  7.66 us
    add x4, local copies, waits for them, and re-layouts, activate(): return LEAK_SLOPE * values + (1.0 - LEAK_SLOPE) * jax.nn.softplus(values)  7.35 us
  transfers between devices with their start and end apart: 17, of which 10 were waited for; matrix products, arithmetic and copies ran while one was open for 7% of the time, Pallas kernels for 0%

profile of v2, /device:TPU:8, one launch (start us, length us, event | category | flops | bytes accessed | tf_op | source)
XLA Modules:
  0.0 184.6 jit_solution(17166811072527939890)
XLA Ops:
  5.3 2.2 %collective-permute-done.1 = bf16[1,4,1,4,512]{4,3,2,1,0:T(4,128)(2,1)S(1)} collective-permute-done((bf16[1,4,1,4,512]{4,3,2,1,0:T(4,128)(2,1)S(1)}, bf16[1,4,1,4,512]{4,3,2,1,0:T(4,128)(2,1)S(1)}, u32[]{:S(2)}, u32[]{:S(2)}) %collective-permute-start.1) | collective-permute-done | bytes 16416 | tf_op jit(solution)/shard_map/ppermute | solution.py:18
  7.6 3.5 %collective-permute-start.2 = (bf16[1,4,6,1,512]{4,3,2,1,0:T(2,128)(2,1)S(1)}, bf16[1,4,6,1,512]{4,3,2,1,0:T(2,128)(2,1)S(1)}, u32[]{:S(2)}, u32[]{:S(2)}) collective-permute-start(bf16[1,4,6,1,512]{4,3,2,1,0:T(2,128)(2,1)S(1)} %get-tuple-element.29), channel_id=1, source_target_pairs={{0,4},{4,8},{8,12},{12,16},{16,20},{20,24},{24,28},{1,5},{5,9},{9,... | collective-permute-start | bytes 73736 | tf_op jit(solution)/shard_map/ppermute | solution.py:15
  11.1 3.8 %collective-permute-start.3 = (bf16[1,4,6,1,512]{4,3,2,1,0:T(2,128)(2,1)S(1)}, bf16[1,4,6,1,512]{4,3,2,1,0:T(2,128)(2,1)S(1)}, u32[]{:S(2)}, u32[]{:S(2)}) collective-permute-start(bf16[1,4,6,1,512]{4,3,2,1,0:T(2,128)(2,1)S(1)} %get-tuple-element.30), channel_id=1, source_target_pairs={{4,0},{8,4},{12,8},{16,12},{20,16},{24,20},{28,24},{5,1},{9,5},{13... | collective-permute-start | bytes 73736 | tf_op jit(solution)/shard_map/ppermute | solution.py:18
  19.4 10.9 %fusion.15 = f32[4,4,8,65,32]{4,2,3,1,0:T(8,128)} fusion(bf16[4,6,6,1,7,2]{4,0,5,2,1,3:T(4,128)(2,1)S(1)} %slice.169, bf16[4,6,6,1,8,65]{4,0,5,2,1,3:T(4,128)(2,1)S(1)} %copy.137, bf16[32,4,3,3,3]{0,4,3,2,1:T(4,128)(2,1)S(1)} %reshape.127), kind=kOutput, calls=%fused_computation.28 | convolution fusion | flops 57970944 | bytes 1225664 | tf_op jit(solution)/shard_map/conv_general_dilated | solution.py:154
  30.3 3.7 %copy.140 = f32[4,4,8,65,32]{3,4,2,1,0:T(8,128)S(1)} copy(f32[4,4,8,65,32]{4,2,3,1,0:T(8,128)} %fusion.15) | data formatting | bytes 2129920 | tf_op jit(solution)/shard_map/conv_general_dilated | solution.py:154
  40.1 2.6 %copy.142 = f32[1,32,4,4,512]{1,4,3,2,0:T(8,128)} copy(f32[1,32,4,4,512]{4,1,3,2,0:T(8,128)S(1)} %slice_bitcast_fusion.6) | data formatting | bytes 2097152 | tf_op jit(solution)/shard_map/add | solution.py:135
  42.8 4.8 %reduce_sum.21 = f32[32,2,2,256]{0,3,2,1:T(8,128)S(1)} reduce(f32[32,2,2,2,2,256,2]{0,6,5,4,3,2,1:T(2,128)} %bitcast.237, f32[]{:T(128)} %constant.15.clone.1), dimensions={2,4,6}, to_apply=%region_0.1 | reduce | flops 229376 | bytes 1179652 | tf_op jit(solution)/shard_map/reduce_sum | solution.py:145
  47.8 28.1 %all-gather = bf16[32,2,16,256]{3,0,2,1:T(8,128)(2,1)S(1)} all-gather(bf16[32,2,2,256]{3,0,2,1:T(8,128)(2,1)S(1)} %multiply_convert_fusion.2), channel_id=2, replica_groups=mesh['depth'=16,'height'=8,'sample'=4] {'height'}, dimensions={2}, use_global_device_ids=true | all-gather | bytes 589824 | tf_op jit(solution)/shard_map/all_gather | solution.py:191
  82.0 1.9 %collective-permute-done.5 = bf16[1,32,1,16,256]{4,1,3,2,0:T(8,128)(2,1)S(1)} collective-permute-done((bf16[1,32,1,16,256]{4,1,3,2,0:T(8,128)(2,1)S(1)}, bf16[1,32,1,16,256]{4,1,3,2,0:T(8,128)(2,1)S(1)}, u32[]{:S(2)}, u32[]{:S(2)}) %collective-permute-start.5) | collective-permute-done | bytes 262176 | tf_op jit(solution)/shard_map/ppermute | solution.py:18
  86.9 2.8 %slice_bitcast_fusion.2 = (bf16[1,32,9,2,16,256]{5,1,2,0,4,3:T(8,128)(2,1)S(1)}, bf16[1,32,9,2,16,256]{5,1,2,0,4,3:T(8,128)(2,1)S(1)}, bf16[1,32,9,2,16,256]{5,1,2,0,4,3:T(8,128)(2,1)S(1)}) fusion(bf16[32,9,4,16,256]{4,0,1,3,2:T(8,128)(2,1)S(1)} %fusion.58), kind=kLoop, calls=%fused_computation.11 | loop fusion | bytes 28311552 | tf_op jit(solution)/shard_map/stack | solution.py:102
  89.6 2.6 %multiply_convert_fusion.1 = (bf16[8,2,16,256]{3,0,2,1:T(8,128)(2,1)S(1)}, f32[8,16,256]{2,0,1:T(8,128)S(1)}) fusion(f32[8,16,256]{2,0,1:T(8,128)S(1)} %copy.158, bf16[8,3,32,9,1,1]{2,0,3,1,5,4:T(8,128)(2,1)S(1)} %bitcast.251, bf16[1,32,9,2,16,256]{5,1,2,0,4,3:T(8,128)(2,1)S(1)} %get-tuple-element.16, ...), kind=kOutput, calls=%fused_computation.110 | convolution fusion | flops 128483328 | bytes 14562816 | tf_op jit(solution)/shard_map/dot_general | solution.py:105
  92.4 6.7 %collective-permute-start.12 = (bf16[1,8,1,16,256]{4,1,3,2,0:T(8,128)(2,1)S(1)}, bf16[1,8,1,16,256]{4,1,3,2,0:T(8,128)(2,1)S(1)}, u32[]{:S(2)}, u32[]{:S(2)}) collective-permute-start(bf16[1,8,1,16,256]{4,1,3,2,0:T(8,128)(2,1)S(1)} %get-tuple-element.27), channel_id=1, source_target_pairs={{0,32},{32,64},{64,96},{96,128},{128,160},{160,192},{192,224},{224... | collective-permute-start | bytes 196616 | tf_op jit(solution)/shard_map/ppermute | solution.py:15
  104.7 2.1 %collective-permute-start.14 = (f32[2,2,1,2,2,32,256]{6,5,4,3,0,2,1:T(8,128)S(1)}, f32[2,2,1,2,2,32,256]{6,5,4,3,0,2,1:T(8,128)S(1)}, u32[]{:S(2)}, u32[]{:S(2)}) collective-permute-start(f32[2,2,1,2,2,32,256]{6,5,4,3,0,2,1:T(8,128)S(1)} %copy.174), channel_id=1, source_target_pairs={{0,4},{4,0},{8,12},{12,8},{16,20},{20,16},{24,28},{28,24},{1,5},{5... | collective-permute-start | bytes 1572872 | tf_op jit(solution)/shard_map/ppermute | solution.py:130
  107.1 12.7 %collective-permute-done.14 = f32[2,2,1,2,2,32,256]{6,5,4,3,0,2,1:T(8,128)S(1)} collective-permute-done((f32[2,2,1,2,2,32,256]{6,5,4,3,0,2,1:T(8,128)S(1)}, f32[2,2,1,2,2,32,256]{6,5,4,3,0,2,1:T(8,128)S(1)}, u32[]{:S(2)}, u32[]{:S(2)}) %collective-permute-start.14) | collective-permute-done | bytes 524320 | tf_op jit(solution)/shard_map/ppermute | solution.py:130
  120.6 4.6 %collective-permute-start.15 = (f32[2,1,2,2,32,256]{5,4,3,2,0,1:T(8,128)}, f32[2,1,2,2,32,256]{5,4,3,2,0,1:T(8,128)}, u32[]{:S(2)}, u32[]{:S(2)}) collective-permute-start(f32[2,1,2,2,32,256]{5,4,3,2,0,1:T(8,128)} %dynamic-slice_bitcast_fusion), channel_id=1, source_target_pairs={{0,8},{4,12},{8,0},{12,4},{16,24},{20,28},{24,16},{28,20},{1,9},{5... | collective-permute-start | bytes 786440 | tf_op jit(solution)/shard_map/ppermute | solution.py:130
  128.6 6.1 %collective-permute-start.6 = (f32[54,128]{1,0:T(8,128)S(1)}, f32[54,128]{1,0:T(8,128)S(1)}, u32[]{:S(2)}, u32[]{:S(2)}) collective-permute-start(f32[54,128]{1,0:T(8,128)S(1)} %mul.80), channel_id=1, source_target_pairs={{0,1},{1,0},{2,3},{3,2},{32,33},{33,32},{34,35},{35,34},{64,65},{6... | collective-permute-start | bytes 82952 | tf_op jit(solution)/shard_map/ppermute | solution.py:33
  136.5 9.6 %collective-permute-start.7 = (f32[54,128]{1,0:T(8,128)S(1)}, f32[54,128]{1,0:T(8,128)S(1)}, u32[]{:S(2)}, u32[]{:S(2)}) collective-permute-start(f32[54,128]{1,0:T(8,128)S(1)} %add.84), channel_id=1, source_target_pairs={{0,2},{1,3},{2,0},{3,1},{32,34},{33,35},{34,32},{35,33},{64,66},{6... | collective-permute-start | bytes 82952 | tf_op jit(solution)/shard_map/ppermute | solution.py:33
  146.2 1.8 collective-permute-done.7
  148.0 1.9 %collective-permute-start.8 = (f32[54,128]{1,0:T(8,128)S(1)}, f32[54,128]{1,0:T(8,128)S(1)}, u32[]{:S(2)}, u32[]{:S(2)}) collective-permute-start(f32[54,128]{1,0:T(8,128)S(1)} %add.85), channel_id=1, source_target_pairs={{0,32},{1,33},{2,34},{3,35},{32,0},{33,1},{34,2},{35,3},{64,96},{6... | collective-permute-start | bytes 82952 | tf_op jit(solution)/shard_map/ppermute | solution.py:33
  151.1 5.3 %collective-permute-start.9 = (f32[54,128]{1,0:T(8,128)S(1)}, f32[54,128]{1,0:T(8,128)S(1)}, u32[]{:S(2)}, u32[]{:S(2)}) collective-permute-start(f32[54,128]{1,0:T(8,128)S(1)} %add.86), channel_id=1, source_target_pairs={{0,64},{1,65},{2,66},{3,67},{32,96},{33,97},{34,98},{35,99},{64,0}... | collective-permute-start | bytes 82952 | tf_op jit(solution)/shard_map/ppermute | solution.py:33
  158.3 6.4 %collective-permute-start.10 = (f32[54,128]{1,0:T(8,128)S(1)}, f32[54,128]{1,0:T(8,128)S(1)}, u32[]{:S(2)}, u32[]{:S(2)}) collective-permute-start(f32[54,128]{1,0:T(8,128)S(1)} %add.87), channel_id=1, source_target_pairs={{0,128},{1,129},{2,130},{3,131},{32,160},{33,161},{34,162},{35,163... | collective-permute-start | bytes 82952 | tf_op jit(solution)/shard_map/ppermute | solution.py:33
  167.1 3.9 %collective-permute-start.11 = (f32[54,128]{1,0:T(8,128)S(1)}, f32[54,128]{1,0:T(8,128)S(1)}, u32[]{:S(2)}, u32[]{:S(2)}) collective-permute-start(f32[54,128]{1,0:T(8,128)S(1)} %add.88), channel_id=1, source_target_pairs={{0,256},{1,257},{2,258},{3,259},{32,288},{33,289},{34,290},{35,291... | collective-permute-start | bytes 82952 | tf_op jit(solution)/shard_map/ppermute | solution.py:33
  172.1 3.7 %collective-permute-start.16 = (f32[1,2,2,32,256]{4,3,2,1,0:T(8,128)S(1)}, f32[1,2,2,32,256]{4,3,2,1,0:T(8,128)S(1)}, u32[]{:S(2)}, u32[]{:S(2)}) collective-permute-start(f32[1,2,2,32,256]{4,3,2,1,0:T(8,128)S(1)} %dynamic-slice_bitcast_fusion.1), channel_id=1, source_target_pairs={{0,16},{4,20},{8,24},{12,28},{16,0},{20,4},{24,8},{28,12},{1,17},{... | collective-permute-start | bytes 393224 | tf_op jit(solution)/shard_map/ppermute | solution.py:130
  177.2 6.7 %collective-permute-done.16 = f32[1,2,2,32,256]{4,3,2,1,0:T(8,128)S(1)} collective-permute-done((f32[1,2,2,32,256]{4,3,2,1,0:T(8,128)S(1)}, f32[1,2,2,32,256]{4,3,2,1,0:T(8,128)S(1)}, u32[]{:S(2)}, u32[]{:S(2)}) %collective-permute-start.16) | collective-permute-done | bytes 131104 | tf_op jit(solution)/shard_map/ppermute | solution.py:130
  (112 shorter events, 44.9 us)
Async XLA Ops:
  1.4 3.0 %collective-permute-start = (bf16[1,4,1,4,512]{4,3,2,1,0:T(4,128)(2,1)S(1)}, bf16[1,4,1,4,512]{4,3,2,1,0:T(4,128)(2,1)S(1)}, u32[]{:S(2)}, u32[]{:S(2)}) collective-permute-start(bf16[1,4,1,4,512]{4,3,2,1,0:T(4,128)(2,1)S(1)} %get-tuple-element.32), channel_id=1, source_target_pairs={{0,32},{32,64},{64,96},{96,128},{128,160},{160,192},{192,224},{224... | collective-permute-start | bytes 49160 | tf_op jit(solution)/shard_map/ppermute | solution.py:15
  3.1 4.4 %collective-permute-start.1 = (bf16[1,4,1,4,512]{4,3,2,1,0:T(4,128)(2,1)S(1)}, bf16[1,4,1,4,512]{4,3,2,1,0:T(4,128)(2,1)S(1)}, u32[]{:S(2)}, u32[]{:S(2)}) collective-permute-start(bf16[1,4,1,4,512]{4,3,2,1,0:T(4,128)(2,1)S(1)} %get-tuple-element.31), channel_id=1, source_target_pairs={{32,0},{64,32},{96,64},{128,96},{160,128},{192,160},{224,192},{256... | collective-permute-start | bytes 49160 | tf_op jit(solution)/shard_map/ppermute | solution.py:18
  7.6 8.1 %collective-permute-start.2 = (bf16[1,4,6,1,512]{4,3,2,1,0:T(2,128)(2,1)S(1)}, bf16[1,4,6,1,512]{4,3,2,1,0:T(2,128)(2,1)S(1)}, u32[]{:S(2)}, u32[]{:S(2)}) collective-permute-start(bf16[1,4,6,1,512]{4,3,2,1,0:T(2,128)(2,1)S(1)} %get-tuple-element.29), channel_id=1, source_target_pairs={{0,4},{4,8},{8,12},{12,16},{16,20},{20,24},{24,28},{1,5},{5,9},{9,... | collective-permute-start | bytes 73736 | tf_op jit(solution)/shard_map/ppermute | solution.py:15
  11.1 6.0 %collective-permute-start.3 = (bf16[1,4,6,1,512]{4,3,2,1,0:T(2,128)(2,1)S(1)}, bf16[1,4,6,1,512]{4,3,2,1,0:T(2,128)(2,1)S(1)}, u32[]{:S(2)}, u32[]{:S(2)}) collective-permute-start(bf16[1,4,6,1,512]{4,3,2,1,0:T(2,128)(2,1)S(1)} %get-tuple-element.30), channel_id=1, source_target_pairs={{4,0},{8,4},{12,8},{16,12},{20,16},{24,20},{28,24},{5,1},{9,5},{13... | collective-permute-start | bytes 73736 | tf_op jit(solution)/shard_map/ppermute | solution.py:18
  30.3 3.8 %copy-start.5 = (pred[8,65]{1,0:T(8,128)(4,1)S(1)}, pred[8,65]{1,0:T(8,128)(4,1)}, u32[]{:S(2)}) copy-start(pred[8,65]{1,0:T(8,128)(4,1)} %constant.56) | copy-start | bytes 1564
  47.5 31.7 %copy-start.4 = (bf16[8,864]{1,0:T(8,128)(2,1)S(1)}, bf16[8,864]{1,0:T(8,128)(2,1)}, u32[]{:S(2)}) copy-start(bf16[8,864]{1,0:T(8,128)(2,1)} %param.6) | copy-start | bytes 41476
  47.6 33.5 %copy-start.3 = (bf16[1,8,1,1024]{3,1,2,0:T(8,128)(2,1)S(1)}, bf16[1,8,1,1024]{3,1,2,0:T(8,128)(2,1)}, u32[]{:S(2)}) copy-start(bf16[1,8,1,1024]{3,1,2,0:T(8,128)(2,1)} %param.7) | copy-start | bytes 49156
  76.6 5.4 %collective-permute-start.4 = (bf16[1,32,1,16,256]{4,1,3,2,0:T(8,128)(2,1)}, bf16[1,32,1,16,256]{4,1,3,2,0:T(8,128)(2,1)S(1)}, u32[]{:S(2)}, u32[]{:S(2)}) collective-permute-start(bf16[1,32,1,16,256]{4,1,3,2,0:T(8,128)(2,1)} %get-tuple-element.23), channel_id=1, source_target_pairs={{0,32},{32,64},{64,96},{96,128},{128,160},{160,192},{192,224},{224... | collective-permute-start | bytes 786440 | tf_op jit(solution)/shard_map/ppermute | solution.py:15
  77.9 6.0 %collective-permute-start.5 = (bf16[1,32,1,16,256]{4,1,3,2,0:T(8,128)(2,1)S(1)}, bf16[1,32,1,16,256]{4,1,3,2,0:T(8,128)(2,1)S(1)}, u32[]{:S(2)}, u32[]{:S(2)}) collective-permute-start(bf16[1,32,1,16,256]{4,1,3,2,0:T(8,128)(2,1)S(1)} %get-tuple-element.24), channel_id=1, source_target_pairs={{32,0},{64,32},{96,64},{128,96},{160,128},{192,160},{224,192},{256... | collective-permute-start | bytes 786440 | tf_op jit(solution)/shard_map/ppermute | solution.py:18
  83.9 1.5 copy-start
  86.8 2.8 %copy-start.2 = (bf16[8,3,32,3,3]{2,0,4,3,1:T(8,128)(2,1)S(1)}, bf16[8,3,32,3,3]{2,0,4,3,1:T(8,128)(2,1)}, u32[]{:S(2)}) copy-start(bf16[8,3,32,3,3]{2,0,4,3,1:T(8,128)(2,1)} %copy.155) | copy-start | bytes 41476
  92.4 8.2 %collective-permute-start.12 = (bf16[1,8,1,16,256]{4,1,3,2,0:T(8,128)(2,1)S(1)}, bf16[1,8,1,16,256]{4,1,3,2,0:T(8,128)(2,1)S(1)}, u32[]{:S(2)}, u32[]{:S(2)}) collective-permute-start(bf16[1,8,1,16,256]{4,1,3,2,0:T(8,128)(2,1)S(1)} %get-tuple-element.27), channel_id=1, source_target_pairs={{0,32},{32,64},{64,96},{96,128},{128,160},{160,192},{192,224},{224... | collective-permute-start | bytes 196616 | tf_op jit(solution)/shard_map/ppermute | solution.py:15
  99.1 3.1 %collective-permute-start.13 = (bf16[1,8,1,16,256]{4,1,3,2,0:T(8,128)(2,1)S(1)}, bf16[1,8,1,16,256]{4,1,3,2,0:T(8,128)(2,1)S(1)}, u32[]{:S(2)}, u32[]{:S(2)}) collective-permute-start(bf16[1,8,1,16,256]{4,1,3,2,0:T(8,128)(2,1)S(1)} %get-tuple-element.28), channel_id=1, source_target_pairs={{32,0},{64,32},{96,64},{128,96},{160,128},{192,160},{224,192},{256... | collective-permute-start | bytes 196616 | tf_op jit(solution)/shard_map/ppermute | solution.py:18
  104.6 20.5 %copy-start.1 = (bf16[1,32,1,16,256]{4,1,3,2,0:T(8,128)(2,1)S(1)}, bf16[1,32,1,16,256]{4,1,3,2,0:T(8,128)(2,1)}, u32[]{:S(2)}) copy-start(bf16[1,32,1,16,256]{4,1,3,2,0:T(8,128)(2,1)} %copy-done) | copy-start | bytes 786436
  104.7 15.1 %collective-permute-start.14 = (f32[2,2,1,2,2,32,256]{6,5,4,3,0,2,1:T(8,128)S(1)}, f32[2,2,1,2,2,32,256]{6,5,4,3,0,2,1:T(8,128)S(1)}, u32[]{:S(2)}, u32[]{:S(2)}) collective-permute-start(f32[2,2,1,2,2,32,256]{6,5,4,3,0,2,1:T(8,128)S(1)} %copy.174), channel_id=1, source_target_pairs={{0,4},{4,0},{8,12},{12,8},{16,20},{20,16},{24,28},{28,24},{1,5},{5... | collective-permute-start | bytes 1572872 | tf_op jit(solution)/shard_map/ppermute | solution.py:130
  120.6 50.4 %collective-permute-start.15 = (f32[2,1,2,2,32,256]{5,4,3,2,0,1:T(8,128)}, f32[2,1,2,2,32,256]{5,4,3,2,0,1:T(8,128)}, u32[]{:S(2)}, u32[]{:S(2)}) collective-permute-start(f32[2,1,2,2,32,256]{5,4,3,2,0,1:T(8,128)} %dynamic-slice_bitcast_fusion), channel_id=1, source_target_pairs={{0,8},{4,12},{8,0},{12,4},{16,24},{20,28},{24,16},{28,20},{1,9},{5... | collective-permute-start | bytes 786440 | tf_op jit(solution)/shard_map/ppermute | solution.py:130
  128.6 7.9 %collective-permute-start.6 = (f32[54,128]{1,0:T(8,128)S(1)}, f32[54,128]{1,0:T(8,128)S(1)}, u32[]{:S(2)}, u32[]{:S(2)}) collective-permute-start(f32[54,128]{1,0:T(8,128)S(1)} %mul.80), channel_id=1, source_target_pairs={{0,1},{1,0},{2,3},{3,2},{32,33},{33,32},{34,35},{35,34},{64,65},{6... | collective-permute-start | bytes 82952 | tf_op jit(solution)/shard_map/ppermute | solution.py:33
  136.5 11.5 %collective-permute-start.7 = (f32[54,128]{1,0:T(8,128)S(1)}, f32[54,128]{1,0:T(8,128)S(1)}, u32[]{:S(2)}, u32[]{:S(2)}) collective-permute-start(f32[54,128]{1,0:T(8,128)S(1)} %add.84), channel_id=1, source_target_pairs={{0,2},{1,3},{2,0},{3,1},{32,34},{33,35},{34,32},{35,33},{64,66},{6... | collective-permute-start | bytes 82952 | tf_op jit(solution)/shard_map/ppermute | solution.py:33
  148.0 3.1 %collective-permute-start.8 = (f32[54,128]{1,0:T(8,128)S(1)}, f32[54,128]{1,0:T(8,128)S(1)}, u32[]{:S(2)}, u32[]{:S(2)}) collective-permute-start(f32[54,128]{1,0:T(8,128)S(1)} %add.85), channel_id=1, source_target_pairs={{0,32},{1,33},{2,34},{3,35},{32,0},{33,1},{34,2},{35,3},{64,96},{6... | collective-permute-start | bytes 82952 | tf_op jit(solution)/shard_map/ppermute | solution.py:33
  151.1 7.2 %collective-permute-start.9 = (f32[54,128]{1,0:T(8,128)S(1)}, f32[54,128]{1,0:T(8,128)S(1)}, u32[]{:S(2)}, u32[]{:S(2)}) collective-permute-start(f32[54,128]{1,0:T(8,128)S(1)} %add.86), channel_id=1, source_target_pairs={{0,64},{1,65},{2,66},{3,67},{32,96},{33,97},{34,98},{35,99},{64,0}... | collective-permute-start | bytes 82952 | tf_op jit(solution)/shard_map/ppermute | solution.py:33
  158.3 8.8 %collective-permute-start.10 = (f32[54,128]{1,0:T(8,128)S(1)}, f32[54,128]{1,0:T(8,128)S(1)}, u32[]{:S(2)}, u32[]{:S(2)}) collective-permute-start(f32[54,128]{1,0:T(8,128)S(1)} %add.87), channel_id=1, source_target_pairs={{0,128},{1,129},{2,130},{3,131},{32,160},{33,161},{34,162},{35,163... | collective-permute-start | bytes 82952 | tf_op jit(solution)/shard_map/ppermute | solution.py:33
  167.1 9.4 %collective-permute-start.11 = (f32[54,128]{1,0:T(8,128)S(1)}, f32[54,128]{1,0:T(8,128)S(1)}, u32[]{:S(2)}, u32[]{:S(2)}) collective-permute-start(f32[54,128]{1,0:T(8,128)S(1)} %add.88), channel_id=1, source_target_pairs={{0,256},{1,257},{2,258},{3,259},{32,288},{33,289},{34,290},{35,291... | collective-permute-start | bytes 82952 | tf_op jit(solution)/shard_map/ppermute | solution.py:33
  172.1 11.9 %collective-permute-start.16 = (f32[1,2,2,32,256]{4,3,2,1,0:T(8,128)S(1)}, f32[1,2,2,32,256]{4,3,2,1,0:T(8,128)S(1)}, u32[]{:S(2)}, u32[]{:S(2)}) collective-permute-start(f32[1,2,2,32,256]{4,3,2,1,0:T(8,128)S(1)} %dynamic-slice_bitcast_fusion.1), channel_id=1, source_target_pairs={{0,16},{4,20},{8,24},{12,28},{16,0},{20,4},{24,8},{28,12},{1,17},{... | collective-permute-start | bytes 393224 | tf_op jit(solution)/shard_map/ppermute | solution.py:130

commit v3 on v2

--- a/solution.py
+++ b/solution.py
@@ -186,8 +186,8 @@
     first_kernel = kernel_one.reshape(chans_mid, chans_in, 3, 3, 3)
     second_kernel = kernel_two.reshape(filters, chans_mid, 3, 3, 3)
     padded = extended(volume, (("depth", 2), ("height", 3)), 1)
-    window = jnp.pad(padded, ((0, 0), (0, 0), (0, 0), (0, 0), (1, 1)))
-    level_loc = pooled(activate(conv_valid(window, first_kernel))).astype(jnp.bfloat16)
+    pre_one = forward_product(padded, first_kernel)[:, :, :, 1:-1]
+    level_loc = pooled(activate(pre_one)).astype(jnp.bfloat16)
     slab_rows = lax.all_gather(level_loc, "height", axis=3, tiled=True)
     level_one = extended(slab_rows, (("depth", 2),), 1)
     pre_two = forward_product(level_one, second_kernel)

time: 186 us -> 185 us (level)
  matrix products: 15.7 us -> 6.18 us
  local copies, waits for them, and re-layouts: 32.5 us -> 39.8 us
    another operation x3 -> x14, local copies, waits for them, and re-layouts: 0.66 us -> 18.5 us  [delta_shifts(): jnp.stack([dpad[:, :, 2 - kh:2 - kh + hsize, 2 - kw:2 - kw + wsize] for k...]
    conv_general_dilated x1 -> x0, matrix products: 10.9 us -> none  [conv_valid(): lax.conv_general_dilated(inputs, kernel, (1, 1, 1), 'VALID', dimension_nu...]
    conv_general_dilated x4 -> x0, local copies, waits for them, and re-layouts: 5.71 us -> none  [conv_valid(): lax.conv_general_dilated(inputs, kernel, (1, 1, 1), 'VALID', dimension_nu...]
    add x4 -> x1, local copies, waits for them, and re-layouts: 7.35 us -> 2.64 us  [activate(): return LEAK_SLOPE * values + (1.0 - LEAK_SLOPE) * jax.nn.softplus(values)]
    dot_general x1 -> x2, matrix products: 2.65 us -> 4.02 us  [forward_product(): lax.dot_general(weights, stacked, (((1, 2, 3), (0, 1, 2)), ((), ())), pre...]
    unnamed x41 -> x37, local copies, waits for them, and re-layouts: 6.89 us -> 7.03 us
  transfers between devices with their start and end apart: 17 -> 17, of which waited for: 10 -> 10; matrix products, arithmetic and copies ran while one was open for 7% -> 8% of each run, Pallas kernels for 0% -> 0%
where the time goes in v3:
time: 185 us; the launch traced here: 183 us
  starting transfers between devices  65.8 us (36%)
  local copies, waits for them, and re-layouts  39.8 us (22%)
  waiting for transfers between devices  31.5 us (17%)
  blocking collectives  27.9 us (15%)
  other arithmetic  10.1 us (5%)
  matrix products  6.18 us (3%)
    ppermute x6, starting transfers between devices, butterfly_sum(): values = values + lax.ppermute(values, axes, pairs)  33.6 us
    all_gather x1, blocking collectives, shards(): slab_rows = lax.all_gather(level_loc, 'height', axis=3, tiled=True)  27.9 us
    ppermute x3, waiting for transfers between devices, near_first_scatter(): grid = jnp.squeeze(keep + lax.ppermute(send, axis, pairs), axis_pos)  18.8 us
    another operation x14, local copies, waits for them, and re-layouts, delta_shifts(): jnp.stack([dpad[:, :, 2 - kh:2 - kh + hsize, 2 - kw:2 - kw + wsize] for k...  18.5 us
    ppermute x4, starting transfers between devices, extended(): lax.ppermute(lax.slice_in_dim(block, block.shape[dim] - width, None, axis...  13.2 us
    ppermute x3, starting transfers between devices, near_first_scatter(): grid = jnp.squeeze(keep + lax.ppermute(send, axis, pairs), axis_pos)  11.1 us
    ppermute x4, starting transfers between devices, extended(): lax.ppermute(lax.slice_in_dim(block, 0, width, axis=dim), axis, backward)  7.84 us
    unnamed x37, local copies, waits for them, and re-layouts  7.03 us
  transfers between devices with their start and end apart: 17, of which 10 were waited for; matrix products, arithmetic and copies ran while one was open for 8% of the time, Pallas kernels for 0%

profile of v3, /device:TPU:8, one launch (start us, length us, event | category | flops | bytes accessed | tf_op | source)
XLA Modules:
  0.0 182.7 jit_solution(6919112435977799330)
XLA Ops:
  5.3 2.2 %collective-permute-done.1 = bf16[1,4,1,4,512]{4,3,2,1,0:T(4,128)(2,1)S(1)} collective-permute-done((bf16[1,4,1,4,512]{4,3,2,1,0:T(4,128)(2,1)S(1)}, bf16[1,4,1,4,512]{4,3,2,1,0:T(4,128)(2,1)S(1)}, u32[]{:S(2)}, u32[]{:S(2)}) %collective-permute-start.1) | collective-permute-done | bytes 16416 | tf_op jit(solution)/shard_map/ppermute | solution.py:18
  7.6 3.5 %collective-permute-start.2 = (bf16[1,4,6,1,512]{4,3,2,1,0:T(2,128)(2,1)S(1)}, bf16[1,4,6,1,512]{4,3,2,1,0:T(2,128)(2,1)S(1)}, u32[]{:S(2)}, u32[]{:S(2)}) collective-permute-start(bf16[1,4,6,1,512]{4,3,2,1,0:T(2,128)(2,1)S(1)} %get-tuple-element.57), channel_id=1, source_target_pairs={{0,4},{4,8},{8,12},{12,16},{16,20},{20,24},{24,28},{1,5},{5,9},{9,... | collective-permute-start | bytes 73736 | tf_op jit(solution)/shard_map/ppermute | solution.py:15
  11.1 3.8 %collective-permute-start.3 = (bf16[1,4,6,1,512]{4,3,2,1,0:T(2,128)(2,1)S(1)}, bf16[1,4,6,1,512]{4,3,2,1,0:T(2,128)(2,1)S(1)}, u32[]{:S(2)}, u32[]{:S(2)}) collective-permute-start(bf16[1,4,6,1,512]{4,3,2,1,0:T(2,128)(2,1)S(1)} %get-tuple-element.58), channel_id=1, source_target_pairs={{4,0},{8,4},{12,8},{16,12},{20,16},{24,20},{28,24},{5,1},{9,5},{13... | collective-permute-start | bytes 73736 | tf_op jit(solution)/shard_map/ppermute | solution.py:18
  23.7 11.4 %stack.168 = bf16[4,9,6,6,512]{4,1,0,3,2:T(8,128)(2,1)S(1)} concatenate(bf16[4,1,6,6,512]{4,1,0,3,2:T(2,128)(2,1)S(1)} %copy.378, bf16[4,1,6,6,512]{4,1,0,3,2:T(2,128)(2,1)S(1)} %copy.379, bf16[4,1,6,6,512]{4,1,0,3,2:T(2,128)(2,1)S(1)} %copy.380, bf16[4,1,6,6,512]{4,1,0,3,2:T(2,128)(2,1)S(1)} %copy.381, bf16[4,1,6,6,512]{4,1,0,3,2:T(2,128)(2,1)} %copy.382, ...), dimensions={1} | concatenate | bytes 2654208 | tf_op jit(solution)/shard_map/stack | solution.py:58
  37.9 2.6 %copy.392 = f32[1,32,4,4,512]{1,4,3,2,0:T(8,128)} copy(f32[1,32,4,4,512]{4,1,3,2,0:T(8,128)S(1)} %fusion.61) | data formatting | bytes 2097152 | tf_op jit(solution)/shard_map/add | solution.py:135
  40.5 4.8 %reduce_sum.21 = f32[32,2,2,256]{0,3,2,1:T(8,128)S(1)} reduce(f32[32,2,2,2,2,256,2]{0,6,5,4,3,2,1:T(2,128)} %bitcast.266, f32[]{:T(128)} %constant.17.clone.1), dimensions={2,4,6}, to_apply=%region_0.1 | reduce | flops 229376 | bytes 1179652 | tf_op jit(solution)/shard_map/reduce_sum | solution.py:145
  45.5 27.9 %all-gather = bf16[32,2,16,256]{3,0,2,1:T(8,128)(2,1)S(1)} all-gather(bf16[32,2,2,256]{3,0,2,1:T(8,128)(2,1)S(1)} %multiply_convert_fusion.2), channel_id=2, replica_groups=mesh['depth'=16,'height'=8,'sample'=4] {'height'}, dimensions={2}, use_global_device_ids=true | all-gather | bytes 589824 | tf_op jit(solution)/shard_map/all_gather | solution.py:191
  83.8 2.8 %slice_bitcast_fusion.2 = (bf16[1,32,9,2,16,256]{5,1,2,0,4,3:T(8,128)(2,1)S(1)}, bf16[1,32,9,2,16,256]{5,1,2,0,4,3:T(8,128)(2,1)S(1)}, bf16[1,32,9,2,16,256]{5,1,2,0,4,3:T(8,128)(2,1)S(1)}) fusion(bf16[32,9,4,16,256]{4,0,1,3,2:T(8,128)(2,1)S(1)} %fusion.59), kind=kLoop, calls=%fused_computation.8 | loop fusion | bytes 28311552 | tf_op jit(solution)/shard_map/stack | solution.py:102
  86.5 2.6 %multiply_convert_fusion.1 = (bf16[8,2,16,256]{3,0,2,1:T(8,128)(2,1)S(1)}, f32[8,16,256]{2,0,1:T(8,128)S(1)}) fusion(f32[8,16,256]{2,0,1:T(8,128)S(1)} %copy.408, bf16[8,3,32,9,1,1]{2,0,3,1,5,4:T(8,128)(2,1)S(1)} %bitcast.281, bf16[1,32,9,2,16,256]{5,1,2,0,4,3:T(8,128)(2,1)S(1)} %get-tuple-element.31, ...), kind=kOutput, calls=%fused_computation.113 | convolution fusion | flops 128483328 | bytes 14562816 | tf_op jit(solution)/shard_map/dot_general | solution.py:105
  89.3 6.7 %collective-permute-start.12 = (bf16[1,8,1,16,256]{4,1,3,2,0:T(8,128)(2,1)S(1)}, bf16[1,8,1,16,256]{4,1,3,2,0:T(8,128)(2,1)S(1)}, u32[]{:S(2)}, u32[]{:S(2)}) collective-permute-start(bf16[1,8,1,16,256]{4,1,3,2,0:T(8,128)(2,1)S(1)} %get-tuple-element.55), channel_id=1, source_target_pairs={{0,32},{32,64},{64,96},{96,128},{128,160},{160,192},{192,224},{224... | collective-permute-start | bytes 196616 | tf_op jit(solution)/shard_map/ppermute | solution.py:15
  101.6 1.9 %collective-permute-start.14 = (f32[2,2,1,2,2,32,256]{6,5,4,3,0,2,1:T(8,128)S(1)}, f32[2,2,1,2,2,32,256]{6,5,4,3,0,2,1:T(8,128)S(1)}, u32[]{:S(2)}, u32[]{:S(2)}) collective-permute-start(f32[2,2,1,2,2,32,256]{6,5,4,3,0,2,1:T(8,128)S(1)} %copy.444), channel_id=1, source_target_pairs={{0,4},{4,0},{8,12},{12,8},{16,20},{20,16},{24,28},{28,24},{1,5},{5... | collective-permute-start | bytes 1572872 | tf_op jit(solution)/shard_map/ppermute | solution.py:130
  103.9 12.7 %collective-permute-done.14 = f32[2,2,1,2,2,32,256]{6,5,4,3,0,2,1:T(8,128)S(1)} collective-permute-done((f32[2,2,1,2,2,32,256]{6,5,4,3,0,2,1:T(8,128)S(1)}, f32[2,2,1,2,2,32,256]{6,5,4,3,0,2,1:T(8,128)S(1)}, u32[]{:S(2)}, u32[]{:S(2)}) %collective-permute-start.14) | collective-permute-done | bytes 524320 | tf_op jit(solution)/shard_map/ppermute | solution.py:130
  116.7 4.6 %collective-permute-start.15 = (f32[2,1,2,2,32,256]{5,4,3,2,0,1:T(8,128)S(1)}, f32[2,1,2,2,32,256]{5,4,3,2,0,1:T(8,128)}, u32[]{:S(2)}, u32[]{:S(2)}) collective-permute-start(f32[2,1,2,2,32,256]{5,4,3,2,0,1:T(8,128)S(1)} %dynamic-slice_bitcast_fusion), channel_id=1, source_target_pairs={{0,8},{4,12},{8,0},{12,4},{16,24},{20,28},{24,16},{28,20},{1,9},{5... | collective-permute-start | bytes 786440 | tf_op jit(solution)/shard_map/ppermute | solution.py:130
  124.7 6.1 %collective-permute-start.6 = (f32[54,128]{1,0:T(8,128)S(1)}, f32[54,128]{1,0:T(8,128)S(1)}, u32[]{:S(2)}, u32[]{:S(2)}) collective-permute-start(f32[54,128]{1,0:T(8,128)S(1)} %mul.80), channel_id=1, source_target_pairs={{0,1},{1,0},{2,3},{3,2},{32,33},{33,32},{34,35},{35,34},{64,65},{6... | collective-permute-start | bytes 82952 | tf_op jit(solution)/shard_map/ppermute | solution.py:33
  130.8 1.8 %collective-permute-done.6 = f32[54,128]{1,0:T(8,128)S(1)} collective-permute-done((f32[54,128]{1,0:T(8,128)S(1)}, f32[54,128]{1,0:T(8,128)S(1)}, u32[]{:S(2)}, u32[]{:S(2)}) %collective-permute-start.6) | collective-permute-done | bytes 27680 | tf_op jit(solution)/shard_map/ppermute | solution.py:33
  132.6 9.7 %collective-permute-start.7 = (f32[54,128]{1,0:T(8,128)S(1)}, f32[54,128]{1,0:T(8,128)S(1)}, u32[]{:S(2)}, u32[]{:S(2)}) collective-permute-start(f32[54,128]{1,0:T(8,128)S(1)} %add.86), channel_id=1, source_target_pairs={{0,2},{1,3},{2,0},{3,1},{32,34},{33,35},{34,32},{35,33},{64,66},{6... | collective-permute-start | bytes 82952 | tf_op jit(solution)/shard_map/ppermute | solution.py:33
  142.3 1.8 %collective-permute-done.7 = f32[54,128]{1,0:T(8,128)S(1)} collective-permute-done((f32[54,128]{1,0:T(8,128)S(1)}, f32[54,128]{1,0:T(8,128)S(1)}, u32[]{:S(2)}, u32[]{:S(2)}) %collective-permute-start.7) | collective-permute-done | bytes 27680 | tf_op jit(solution)/shard_map/ppermute | solution.py:33
  144.1 1.9 %collective-permute-start.8 = (f32[54,128]{1,0:T(8,128)S(1)}, f32[54,128]{1,0:T(8,128)S(1)}, u32[]{:S(2)}, u32[]{:S(2)}) collective-permute-start(f32[54,128]{1,0:T(8,128)S(1)} %add.87), channel_id=1, source_target_pairs={{0,32},{1,33},{2,34},{3,35},{32,0},{33,1},{34,2},{35,3},{64,96},{6... | collective-permute-start | bytes 82952 | tf_op jit(solution)/shard_map/ppermute | solution.py:33
  147.2 5.3 %collective-permute-start.9 = (f32[54,128]{1,0:T(8,128)S(1)}, f32[54,128]{1,0:T(8,128)S(1)}, u32[]{:S(2)}, u32[]{:S(2)}) collective-permute-start(f32[54,128]{1,0:T(8,128)S(1)} %add.88), channel_id=1, source_target_pairs={{0,64},{1,65},{2,66},{3,67},{32,96},{33,97},{34,98},{35,99},{64,0}... | collective-permute-start | bytes 82952 | tf_op jit(solution)/shard_map/ppermute | solution.py:33
  152.6 1.8 %collective-permute-done.9 = f32[54,128]{1,0:T(8,128)S(1)} collective-permute-done((f32[54,128]{1,0:T(8,128)S(1)}, f32[54,128]{1,0:T(8,128)S(1)}, u32[]{:S(2)}, u32[]{:S(2)}) %collective-permute-start.9) | collective-permute-done | bytes 27680 | tf_op jit(solution)/shard_map/ppermute | solution.py:33
  155.0 6.4 %collective-permute-start.10 = (f32[54,128]{1,0:T(8,128)}, f32[54,128]{1,0:T(8,128)}, u32[]{:S(2)}, u32[]{:S(2)}) collective-permute-start(f32[54,128]{1,0:T(8,128)} %add.89), channel_id=1, source_target_pairs={{0,128},{1,129},{2,130},{3,131},{32,160},{33,161},{34,162},{35,163... | collective-permute-start | bytes 82952 | tf_op jit(solution)/shard_map/ppermute | solution.py:33
  164.6 4.2 %collective-permute-start.11 = (f32[54,128]{1,0:T(8,128)S(1)}, f32[54,128]{1,0:T(8,128)S(1)}, u32[]{:S(2)}, u32[]{:S(2)}) collective-permute-start(f32[54,128]{1,0:T(8,128)S(1)} %add.90), channel_id=1, source_target_pairs={{0,256},{1,257},{2,258},{3,259},{32,288},{33,289},{34,290},{35,291... | collective-permute-start | bytes 82952 | tf_op jit(solution)/shard_map/ppermute | solution.py:33
  169.8 4.6 %collective-permute-start.16 = (f32[1,2,2,32,256]{4,3,2,1,0:T(8,128)S(1)}, f32[1,2,2,32,256]{4,3,2,1,0:T(8,128)S(1)}, u32[]{:S(2)}, u32[]{:S(2)}) collective-permute-start(f32[1,2,2,32,256]{4,3,2,1,0:T(8,128)S(1)} %dynamic-slice_bitcast_fusion.1), channel_id=1, source_target_pairs={{0,16},{4,20},{8,24},{12,28},{16,0},{20,4},{24,8},{28,12},{1,17},{... | collective-permute-start | bytes 393224 | tf_op jit(solution)/shard_map/ppermute | solution.py:130
  175.9 6.1 %collective-permute-done.16 = f32[1,2,2,32,256]{4,3,2,1,0:T(8,128)S(1)} collective-permute-done((f32[1,2,2,32,256]{4,3,2,1,0:T(8,128)S(1)}, f32[1,2,2,32,256]{4,3,2,1,0:T(8,128)S(1)}, u32[]{:S(2)}, u32[]{:S(2)}) %collective-permute-start.16) | collective-permute-done | bytes 131104 | tf_op jit(solution)/shard_map/ppermute | solution.py:130
  (114 shorter events, 44.1 us)
Async XLA Ops:
  1.4 3.0 %collective-permute-start = (bf16[1,4,1,4,512]{4,3,2,1,0:T(4,128)(2,1)S(1)}, bf16[1,4,1,4,512]{4,3,2,1,0:T(4,128)(2,1)S(1)}, u32[]{:S(2)}, u32[]{:S(2)}) collective-permute-start(bf16[1,4,1,4,512]{4,3,2,1,0:T(4,128)(2,1)S(1)} %get-tuple-element.60), channel_id=1, source_target_pairs={{0,32},{32,64},{64,96},{96,128},{128,160},{160,192},{192,224},{224... | collective-permute-start | bytes 49160 | tf_op jit(solution)/shard_map/ppermute | solution.py:15
  3.1 4.4 %collective-permute-start.1 = (bf16[1,4,1,4,512]{4,3,2,1,0:T(4,128)(2,1)S(1)}, bf16[1,4,1,4,512]{4,3,2,1,0:T(4,128)(2,1)S(1)}, u32[]{:S(2)}, u32[]{:S(2)}) collective-permute-start(bf16[1,4,1,4,512]{4,3,2,1,0:T(4,128)(2,1)S(1)} %get-tuple-element.59), channel_id=1, source_target_pairs={{32,0},{64,32},{96,64},{128,96},{160,128},{192,160},{224,192},{256... | collective-permute-start | bytes 49160 | tf_op jit(solution)/shard_map/ppermute | solution.py:18
  7.6 8.8 %collective-permute-start.2 = (bf16[1,4,6,1,512]{4,3,2,1,0:T(2,128)(2,1)S(1)}, bf16[1,4,6,1,512]{4,3,2,1,0:T(2,128)(2,1)S(1)}, u32[]{:S(2)}, u32[]{:S(2)}) collective-permute-start(bf16[1,4,6,1,512]{4,3,2,1,0:T(2,128)(2,1)S(1)} %get-tuple-element.57), channel_id=1, source_target_pairs={{0,4},{4,8},{8,12},{12,16},{16,20},{20,24},{24,28},{1,5},{5,9},{9,... | collective-permute-start | bytes 73736 | tf_op jit(solution)/shard_map/ppermute | solution.py:15
  11.1 6.0 %collective-permute-start.3 = (bf16[1,4,6,1,512]{4,3,2,1,0:T(2,128)(2,1)S(1)}, bf16[1,4,6,1,512]{4,3,2,1,0:T(2,128)(2,1)S(1)}, u32[]{:S(2)}, u32[]{:S(2)}) collective-permute-start(bf16[1,4,6,1,512]{4,3,2,1,0:T(2,128)(2,1)S(1)} %get-tuple-element.58), channel_id=1, source_target_pairs={{4,0},{8,4},{12,8},{16,12},{20,16},{24,20},{28,24},{5,1},{9,5},{13... | collective-permute-start | bytes 73736 | tf_op jit(solution)/shard_map/ppermute | solution.py:18
  35.1 0.7 copy-start.1
  45.3 31.0 %copy-start.3 = (bf16[8,864]{1,0:T(8,128)(2,1)S(1)}, bf16[8,864]{1,0:T(8,128)(2,1)}, u32[]{:S(2)}) copy-start(bf16[8,864]{1,0:T(8,128)(2,1)} %param.6) | copy-start | bytes 41476
  45.3 32.8 %copy-start.2 = (bf16[1,8,1,1024]{3,1,2,0:T(8,128)(2,1)S(1)}, bf16[1,8,1,1024]{3,1,2,0:T(8,128)(2,1)}, u32[]{:S(2)}) copy-start(bf16[1,8,1,1024]{3,1,2,0:T(8,128)(2,1)} %param.7) | copy-start | bytes 49156
  73.5 5.6 %collective-permute-start.4 = (bf16[1,32,1,16,256]{4,1,3,2,0:T(8,128)(2,1)S(1)}, bf16[1,32,1,16,256]{4,1,3,2,0:T(8,128)(2,1)S(1)}, u32[]{:S(2)}, u32[]{:S(2)}) collective-permute-start(bf16[1,32,1,16,256]{4,1,3,2,0:T(8,128)(2,1)S(1)} %get-tuple-element.41), channel_id=1, source_target_pairs={{0,32},{32,64},{64,96},{96,128},{128,160},{160,192},{192,224},{224... | collective-permute-start | bytes 786440 | tf_op jit(solution)/shard_map/ppermute | solution.py:15
  74.8 6.0 %collective-permute-start.5 = (bf16[1,32,1,16,256]{4,1,3,2,0:T(8,128)(2,1)S(1)}, bf16[1,32,1,16,256]{4,1,3,2,0:T(8,128)(2,1)S(1)}, u32[]{:S(2)}, u32[]{:S(2)}) collective-permute-start(bf16[1,32,1,16,256]{4,1,3,2,0:T(8,128)(2,1)S(1)} %get-tuple-element.42), channel_id=1, source_target_pairs={{32,0},{64,32},{96,64},{128,96},{160,128},{192,160},{224,192},{256... | collective-permute-start | bytes 786440 | tf_op jit(solution)/shard_map/ppermute | solution.py:18
  83.8 2.8 %copy-start = (bf16[8,3,32,3,3]{2,0,4,3,1:T(8,128)(2,1)S(1)}, bf16[8,3,32,3,3]{2,0,4,3,1:T(8,128)(2,1)}, u32[]{:S(2)}) copy-start(bf16[8,3,32,3,3]{2,0,4,3,1:T(8,128)(2,1)} %copy.405) | copy-start | bytes 41476
  89.3 8.2 %collective-permute-start.12 = (bf16[1,8,1,16,256]{4,1,3,2,0:T(8,128)(2,1)S(1)}, bf16[1,8,1,16,256]{4,1,3,2,0:T(8,128)(2,1)S(1)}, u32[]{:S(2)}, u32[]{:S(2)}) collective-permute-start(bf16[1,8,1,16,256]{4,1,3,2,0:T(8,128)(2,1)S(1)} %get-tuple-element.55), channel_id=1, source_target_pairs={{0,32},{32,64},{64,96},{96,128},{128,160},{160,192},{192,224},{224... | collective-permute-start | bytes 196616 | tf_op jit(solution)/shard_map/ppermute | solution.py:15
  96.0 3.1 %collective-permute-start.13 = (bf16[1,8,1,16,256]{4,1,3,2,0:T(8,128)(2,1)S(1)}, bf16[1,8,1,16,256]{4,1,3,2,0:T(8,128)(2,1)S(1)}, u32[]{:S(2)}, u32[]{:S(2)}) collective-permute-start(bf16[1,8,1,16,256]{4,1,3,2,0:T(8,128)(2,1)S(1)} %get-tuple-element.56), channel_id=1, source_target_pairs={{32,0},{64,32},{96,64},{128,96},{160,128},{192,160},{224,192},{256... | collective-permute-start | bytes 196616 | tf_op jit(solution)/shard_map/ppermute | solution.py:18
  101.6 15.0 %collective-permute-start.14 = (f32[2,2,1,2,2,32,256]{6,5,4,3,0,2,1:T(8,128)S(1)}, f32[2,2,1,2,2,32,256]{6,5,4,3,0,2,1:T(8,128)S(1)}, u32[]{:S(2)}, u32[]{:S(2)}) collective-permute-start(f32[2,2,1,2,2,32,256]{6,5,4,3,0,2,1:T(8,128)S(1)} %copy.444), channel_id=1, source_target_pairs={{0,4},{4,0},{8,12},{12,8},{16,20},{20,16},{24,28},{28,24},{1,5},{5... | collective-permute-start | bytes 1572872 | tf_op jit(solution)/shard_map/ppermute | solution.py:130
  116.7 52.1 %collective-permute-start.15 = (f32[2,1,2,2,32,256]{5,4,3,2,0,1:T(8,128)S(1)}, f32[2,1,2,2,32,256]{5,4,3,2,0,1:T(8,128)}, u32[]{:S(2)}, u32[]{:S(2)}) collective-permute-start(f32[2,1,2,2,32,256]{5,4,3,2,0,1:T(8,128)S(1)} %dynamic-slice_bitcast_fusion), channel_id=1, source_target_pairs={{0,8},{4,12},{8,0},{12,4},{16,24},{20,28},{24,16},{28,20},{1,9},{5... | collective-permute-start | bytes 786440 | tf_op jit(solution)/shard_map/ppermute | solution.py:130
  124.7 7.9 %collective-permute-start.6 = (f32[54,128]{1,0:T(8,128)S(1)}, f32[54,128]{1,0:T(8,128)S(1)}, u32[]{:S(2)}, u32[]{:S(2)}) collective-permute-start(f32[54,128]{1,0:T(8,128)S(1)} %mul.80), channel_id=1, source_target_pairs={{0,1},{1,0},{2,3},{3,2},{32,33},{33,32},{34,35},{35,34},{64,65},{6... | collective-permute-start | bytes 82952 | tf_op jit(solution)/shard_map/ppermute | solution.py:33
  132.6 11.5 %collective-permute-start.7 = (f32[54,128]{1,0:T(8,128)S(1)}, f32[54,128]{1,0:T(8,128)S(1)}, u32[]{:S(2)}, u32[]{:S(2)}) collective-permute-start(f32[54,128]{1,0:T(8,128)S(1)} %add.86), channel_id=1, source_target_pairs={{0,2},{1,3},{2,0},{3,1},{32,34},{33,35},{34,32},{35,33},{64,66},{6... | collective-permute-start | bytes 82952 | tf_op jit(solution)/shard_map/ppermute | solution.py:33
  144.1 3.1 %collective-permute-start.8 = (f32[54,128]{1,0:T(8,128)S(1)}, f32[54,128]{1,0:T(8,128)S(1)}, u32[]{:S(2)}, u32[]{:S(2)}) collective-permute-start(f32[54,128]{1,0:T(8,128)S(1)} %add.87), channel_id=1, source_target_pairs={{0,32},{1,33},{2,34},{3,35},{32,0},{33,1},{34,2},{35,3},{64,96},{6... | collective-permute-start | bytes 82952 | tf_op jit(solution)/shard_map/ppermute | solution.py:33
  147.2 7.1 %collective-permute-start.9 = (f32[54,128]{1,0:T(8,128)S(1)}, f32[54,128]{1,0:T(8,128)S(1)}, u32[]{:S(2)}, u32[]{:S(2)}) collective-permute-start(f32[54,128]{1,0:T(8,128)S(1)} %add.88), channel_id=1, source_target_pairs={{0,64},{1,65},{2,66},{3,67},{32,96},{33,97},{34,98},{35,99},{64,0}... | collective-permute-start | bytes 82952 | tf_op jit(solution)/shard_map/ppermute | solution.py:33
  155.0 8.8 %collective-permute-start.10 = (f32[54,128]{1,0:T(8,128)}, f32[54,128]{1,0:T(8,128)}, u32[]{:S(2)}, u32[]{:S(2)}) collective-permute-start(f32[54,128]{1,0:T(8,128)} %add.89), channel_id=1, source_target_pairs={{0,128},{1,129},{2,130},{3,131},{32,160},{33,161},{34,162},{35,163... | collective-permute-start | bytes 82952 | tf_op jit(solution)/shard_map/ppermute | solution.py:33
  164.6 10.6 %collective-permute-start.11 = (f32[54,128]{1,0:T(8,128)S(1)}, f32[54,128]{1,0:T(8,128)S(1)}, u32[]{:S(2)}, u32[]{:S(2)}) collective-permute-start(f32[54,128]{1,0:T(8,128)S(1)} %add.90), channel_id=1, source_target_pairs={{0,256},{1,257},{2,258},{3,259},{32,288},{33,289},{34,290},{35,291... | collective-permute-start | bytes 82952 | tf_op jit(solution)/shard_map/ppermute | solution.py:33
  169.8 12.1 %collective-permute-start.16 = (f32[1,2,2,32,256]{4,3,2,1,0:T(8,128)S(1)}, f32[1,2,2,32,256]{4,3,2,1,0:T(8,128)S(1)}, u32[]{:S(2)}, u32[]{:S(2)}) collective-permute-start(f32[1,2,2,32,256]{4,3,2,1,0:T(8,128)S(1)} %dynamic-slice_bitcast_fusion.1), channel_id=1, source_target_pairs={{0,16},{4,20},{8,24},{12,28},{16,0},{20,4},{24,8},{28,12},{1,17},{... | collective-permute-start | bytes 393224 | tf_op jit(solution)/shard_map/ppermute | solution.py:130

commit v4 on v3

--- a/solution.py
+++ b/solution.py
@@ -131,6 +131,27 @@
     return jnp.transpose(grid, (2, 1, 0, 3))[None]
 
 
+def first_product(volume_ext, kernel):
+    filters, chans = kernel.shape[:2]
+    _, _, dext, hext, wsize = volume_ext.shape
+    dsize, hsize = dext - 2, hext - 2
+    merged = volume_ext.reshape(1, chans, 1, dext * hext, wsize)
+    shifts = delta_shifts(merged)[:, :, 0]
+    stacked = jnp.stack(
+        [shifts[:, :, kd * hext : (kd + dsize) * hext] for kd in range(3)], axis=0
+    )
+    flipped = jnp.flip(kernel, axis=(3, 4))
+    weights = jnp.transpose(flipped, (0, 2, 1, 3, 4)).reshape(filters, 3, chans, 9)
+    grad = lax.dot_general(
+        weights,
+        stacked,
+        (((1, 2, 3), (0, 1, 2)), ((), ())),
+        preferred_element_type=jnp.float32,
+    )
+    grad = grad.reshape(1, filters, dsize, hext, wsize)
+    return grad[:, :, :, 1 : 1 + hsize]
+
+
 def activate(values):
     return LEAK_SLOPE * values + (1.0 - LEAK_SLOPE) * jax.nn.softplus(values)
 
@@ -186,7 +207,7 @@
     first_kernel = kernel_one.reshape(chans_mid, chans_in, 3, 3, 3)
     second_kernel = kernel_two.reshape(filters, chans_mid, 3, 3, 3)
     padded = extended(volume, (("depth", 2), ("height", 3)), 1)
-    pre_one = forward_product(padded, first_kernel)[:, :, :, 1:-1]
+    pre_one = first_product(padded, first_kernel)
     level_loc = pooled(activate(pre_one)).astype(jnp.bfloat16)
     slab_rows = lax.all_gather(level_loc, "height", axis=3, tiled=True)
     level_one = extended(slab_rows, (("depth", 2),), 1)

time: 185 us -> 189 us (1.022)
  other arithmetic: 10.1 us -> 16.2 us
    add x1, other arithmetic: 0.65 us -> 6.69 us  [activate(): return LEAK_SLOPE * values + (1.0 - LEAK_SLOPE) * jax.nn.softplus(values)]
    unnamed x37 -> x38, local copies, waits for them, and re-layouts: 7.03 us -> 9.67 us
    add x1 -> x0, local copies, waits for them, and re-layouts: 2.64 us -> none  [activate(): return LEAK_SLOPE * values + (1.0 - LEAK_SLOPE) * jax.nn.softplus(values)]
    dot_general x2 -> x1, matrix products: 4.02 us -> 2.65 us  [forward_product(): lax.dot_general(weights, stacked, (((1, 2, 3), (0, 1, 2)), ((), ())), pre...]
where the time goes in v4:
time: 189 us; the launch traced here: 187 us
  starting transfers between devices  65.6 us (35%)
  local copies, waits for them, and re-layouts  38.3 us (20%)
  waiting for transfers between devices  31.7 us (17%)
  blocking collectives  28.1 us (15%)
  other arithmetic  16.2 us (9%)
  matrix products  6.18 us (3%)
    ppermute x6, starting transfers between devices, butterfly_sum(): values = values + lax.ppermute(values, axes, pairs)  33.6 us
    all_gather x1, blocking collectives, shards(): slab_rows = lax.all_gather(level_loc, 'height', axis=3, tiled=True)  28.1 us
    ppermute x3, waiting for transfers between devices, near_first_scatter(): grid = jnp.squeeze(keep + lax.ppermute(send, axis, pairs), axis_pos)  18.7 us
    another operation x14, local copies, waits for them, and re-layouts, delta_shifts(): jnp.stack([dpad[:, :, 2 - kh:2 - kh + hsize, 2 - kw:2 - kw + wsize] for k...  16.8 us
    ppermute x4, starting transfers between devices, extended(): lax.ppermute(lax.slice_in_dim(block, block.shape[dim] - width, None, axis...  13.2 us
    ppermute x3, starting transfers between devices, near_first_scatter(): grid = jnp.squeeze(keep + lax.ppermute(send, axis, pairs), axis_pos)  11.1 us
    unnamed x38, local copies, waits for them, and re-layouts  9.67 us
    ppermute x4, starting transfers between devices, extended(): lax.ppermute(lax.slice_in_dim(block, 0, width, axis=dim), axis, backward)  7.66 us
  transfers between devices with their start and end apart: 17, of which 10 were waited for; matrix products, arithmetic and copies ran while one was open for 8% of the time, Pallas kernels for 0%

profile of v4, /device:TPU:8, one launch (start us, length us, event | category | flops | bytes accessed | tf_op | source)
XLA Modules:
  0.0 187.5 jit_solution(17820566094033019227)
XLA Ops:
  5.3 2.2 %collective-permute-done.1 = bf16[1,4,1,4,512]{4,3,2,1,0:T(4,128)(2,1)S(1)} collective-permute-done((bf16[1,4,1,4,512]{4,3,2,1,0:T(4,128)(2,1)S(1)}, bf16[1,4,1,4,512]{4,3,2,1,0:T(4,128)(2,1)S(1)}, u32[]{:S(2)}, u32[]{:S(2)}) %collective-permute-start.1) | collective-permute-done | bytes 16416 | tf_op jit(solution)/shard_map/ppermute | solution.py:18
  7.6 3.5 %collective-permute-start.2 = (bf16[1,4,6,1,512]{4,3,2,1,0:T(2,128)(2,1)S(1)}, bf16[1,4,6,1,512]{4,3,2,1,0:T(2,128)(2,1)S(1)}, u32[]{:S(2)}, u32[]{:S(2)}) collective-permute-start(bf16[1,4,6,1,512]{4,3,2,1,0:T(2,128)(2,1)S(1)} %get-tuple-element.55), channel_id=1, source_target_pairs={{0,4},{4,8},{8,12},{12,16},{16,20},{20,24},{24,28},{1,5},{5,9},{9,... | collective-permute-start | bytes 73736 | tf_op jit(solution)/shard_map/ppermute | solution.py:15
  11.1 3.8 %collective-permute-start.3 = (bf16[1,4,6,1,512]{4,3,2,1,0:T(2,128)(2,1)S(1)}, bf16[1,4,6,1,512]{4,3,2,1,0:T(2,128)(2,1)S(1)}, u32[]{:S(2)}, u32[]{:S(2)}) collective-permute-start(bf16[1,4,6,1,512]{4,3,2,1,0:T(2,128)(2,1)S(1)} %get-tuple-element.56), channel_id=1, source_target_pairs={{4,0},{8,4},{12,8},{16,12},{20,16},{24,20},{28,24},{5,1},{9,5},{13... | collective-permute-start | bytes 73736 | tf_op jit(solution)/shard_map/ppermute | solution.py:18
  23.6 10.0 %stack.168 = bf16[4,9,1,36,512]{4,1,0,3,2:T(8,128)(2,1)S(1)} concatenate(bf16[4,1,1,36,512]{4,1,0,3,2:T(2,128)(2,1)S(1)} %copy.339, bf16[4,1,1,36,512]{4,1,0,3,2:T(2,128)(2,1)S(1)} %copy.340, bf16[4,1,1,36,512]{4,1,0,3,2:T(2,128)(2,1)S(1)} %copy.341, bf16[4,1,1,36,512]{4,1,0,3,2:T(2,128)(2,1)S(1)} %copy.342, bf16[4,1,1,36,512]{4,1,0,3,2:T(2,128)(2,1)} %copy.343, ...), dimensions={1} | concatenate | bytes 2654208 | tf_op jit(solution)/shard_map/stack | solution.py:58
  35.8 2.6 %copy.384 = f32[1,32,4,4,512]{1,4,3,2,0:T(8,128)} copy(f32[1,32,4,4,512]{4,1,3,2,0:T(8,128)S(1)} %slice.219) | data formatting | bytes 2097152
  38.4 6.7 %fusion.13 = f32[1,32,4,4,512]{1,4,3,2,0:T(8,128)} fusion(f32[1,32,4,4,512]{1,4,3,2,0:T(8,128)} %copy.384), kind=kLoop, calls=%fused_computation.17 | loop fusion | flops 2359296 | bytes 2097152 | tf_op jit(solution)/shard_map/add | solution.py:156
  45.1 4.8 %reduce_sum.21 = f32[32,2,2,256]{0,3,2,1:T(8,128)S(1)} reduce(f32[32,2,2,2,2,256,2]{0,6,5,4,3,2,1:T(2,128)} %bitcast.261, f32[]{:T(128)} %constant.17.clone.1), dimensions={2,4,6}, to_apply=%region_0.1 | reduce | flops 229376 | bytes 1179652 | tf_op jit(solution)/shard_map/reduce_sum | solution.py:166
  50.1 28.1 %all-gather = bf16[32,2,16,256]{3,0,2,1:T(8,128)(2,1)S(1)} all-gather(bf16[32,2,2,256]{3,0,2,1:T(8,128)(2,1)S(1)} %multiply_convert_fusion.2), channel_id=2, replica_groups=mesh['depth'=16,'height'=8,'sample'=4] {'height'}, dimensions={2}, use_global_device_ids=true | all-gather | bytes 589824 | tf_op jit(solution)/shard_map/all_gather | solution.py:212
  83.7 1.9 %collective-permute-done.5 = bf16[1,32,1,16,256]{4,1,3,2,0:T(8,128)(2,1)S(1)} collective-permute-done((bf16[1,32,1,16,256]{4,1,3,2,0:T(8,128)(2,1)S(1)}, bf16[1,32,1,16,256]{4,1,3,2,0:T(8,128)(2,1)S(1)}, u32[]{:S(2)}, u32[]{:S(2)}) %collective-permute-start.5) | collective-permute-done | bytes 262176 | tf_op jit(solution)/shard_map/ppermute | solution.py:18
  88.5 2.8 %slice_bitcast_fusion.2 = (bf16[1,32,9,2,16,256]{5,1,2,0,4,3:T(8,128)(2,1)S(1)}, bf16[1,32,9,2,16,256]{5,1,2,0,4,3:T(8,128)(2,1)S(1)}, bf16[1,32,9,2,16,256]{5,1,2,0,4,3:T(8,128)(2,1)S(1)}) fusion(bf16[32,9,4,16,256]{4,0,1,3,2:T(8,128)(2,1)S(1)} %fusion.58), kind=kLoop, calls=%fused_computation.9 | loop fusion | bytes 28311552 | tf_op jit(solution)/shard_map/stack | solution.py:102
  91.3 2.6 %multiply_convert_fusion.1 = (bf16[8,2,16,256]{3,0,2,1:T(8,128)(2,1)S(1)}, f32[8,16,256]{2,0,1:T(8,128)S(1)}) fusion(f32[8,16,256]{2,0,1:T(8,128)S(1)} %copy.367, bf16[8,3,32,9,1,1]{2,0,3,1,5,4:T(8,128)(2,1)S(1)} %bitcast.279, bf16[1,32,9,2,16,256]{5,1,2,0,4,3:T(8,128)(2,1)S(1)} %get-tuple-element.31, ...), kind=kOutput, calls=%fused_computation.112 | convolution fusion | flops 128483328 | bytes 14562816 | tf_op jit(solution)/shard_map/dot_general | solution.py:105
  94.1 6.7 %collective-permute-start.12 = (bf16[1,8,1,16,256]{4,1,3,2,0:T(8,128)(2,1)S(1)}, bf16[1,8,1,16,256]{4,1,3,2,0:T(8,128)(2,1)S(1)}, u32[]{:S(2)}, u32[]{:S(2)}) collective-permute-start(bf16[1,8,1,16,256]{4,1,3,2,0:T(8,128)(2,1)S(1)} %get-tuple-element.53), channel_id=1, source_target_pairs={{0,32},{32,64},{64,96},{96,128},{128,160},{160,192},{192,224},{224... | collective-permute-start | bytes 196616 | tf_op jit(solution)/shard_map/ppermute | solution.py:15
  106.3 1.9 %collective-permute-start.14 = (f32[2,2,1,2,2,32,256]{6,5,4,3,0,2,1:T(8,128)S(1)}, f32[2,2,1,2,2,32,256]{6,5,4,3,0,2,1:T(8,128)S(1)}, u32[]{:S(2)}, u32[]{:S(2)}) collective-permute-start(f32[2,2,1,2,2,32,256]{6,5,4,3,0,2,1:T(8,128)S(1)} %copy.386), channel_id=1, source_target_pairs={{0,4},{4,0},{8,12},{12,8},{16,20},{20,16},{24,28},{28,24},{1,5},{5... | collective-permute-start | bytes 1572872 | tf_op jit(solution)/shard_map/ppermute | solution.py:130
  108.6 12.7 %collective-permute-done.14 = f32[2,2,1,2,2,32,256]{6,5,4,3,0,2,1:T(8,128)S(1)} collective-permute-done((f32[2,2,1,2,2,32,256]{6,5,4,3,0,2,1:T(8,128)S(1)}, f32[2,2,1,2,2,32,256]{6,5,4,3,0,2,1:T(8,128)S(1)}, u32[]{:S(2)}, u32[]{:S(2)}) %collective-permute-start.14) | collective-permute-done | bytes 524320 | tf_op jit(solution)/shard_map/ppermute | solution.py:130
  121.4 4.6 %collective-permute-start.15 = (f32[2,1,2,2,32,256]{5,4,3,2,0,1:T(8,128)S(1)}, f32[2,1,2,2,32,256]{5,4,3,2,0,1:T(8,128)}, u32[]{:S(2)}, u32[]{:S(2)}) collective-permute-start(f32[2,1,2,2,32,256]{5,4,3,2,0,1:T(8,128)S(1)} %dynamic-slice_bitcast_fusion), channel_id=1, source_target_pairs={{0,8},{4,12},{8,0},{12,4},{16,24},{20,28},{24,16},{28,20},{1,9},{5... | collective-permute-start | bytes 786440 | tf_op jit(solution)/shard_map/ppermute | solution.py:130
  129.5 6.1 %collective-permute-start.6 = (f32[54,128]{1,0:T(8,128)S(1)}, f32[54,128]{1,0:T(8,128)S(1)}, u32[]{:S(2)}, u32[]{:S(2)}) collective-permute-start(f32[54,128]{1,0:T(8,128)S(1)} %mul.80), channel_id=1, source_target_pairs={{0,1},{1,0},{2,3},{3,2},{32,33},{33,32},{34,35},{35,34},{64,65},{6... | collective-permute-start | bytes 82952 | tf_op jit(solution)/shard_map/ppermute | solution.py:33
  137.4 9.7 %collective-permute-start.7 = (f32[54,128]{1,0:T(8,128)S(1)}, f32[54,128]{1,0:T(8,128)S(1)}, u32[]{:S(2)}, u32[]{:S(2)}) collective-permute-start(f32[54,128]{1,0:T(8,128)S(1)} %add.86), channel_id=1, source_target_pairs={{0,2},{1,3},{2,0},{3,1},{32,34},{33,35},{34,32},{35,33},{64,66},{6... | collective-permute-start | bytes 82952 | tf_op jit(solution)/shard_map/ppermute | solution.py:33
  147.1 1.8 collective-permute-done.7
  148.9 1.9 %collective-permute-start.8 = (f32[54,128]{1,0:T(8,128)S(1)}, f32[54,128]{1,0:T(8,128)S(1)}, u32[]{:S(2)}, u32[]{:S(2)}) collective-permute-start(f32[54,128]{1,0:T(8,128)S(1)} %add.87), channel_id=1, source_target_pairs={{0,32},{1,33},{2,34},{3,35},{32,0},{33,1},{34,2},{35,3},{64,96},{6... | collective-permute-start | bytes 82952 | tf_op jit(solution)/shard_map/ppermute | solution.py:33
  152.0 5.3 %collective-permute-start.9 = (f32[54,128]{1,0:T(8,128)S(1)}, f32[54,128]{1,0:T(8,128)S(1)}, u32[]{:S(2)}, u32[]{:S(2)}) collective-permute-start(f32[54,128]{1,0:T(8,128)S(1)} %add.88), channel_id=1, source_target_pairs={{0,64},{1,65},{2,66},{3,67},{32,96},{33,97},{34,98},{35,99},{64,0}... | collective-permute-start | bytes 82952 | tf_op jit(solution)/shard_map/ppermute | solution.py:33
  159.8 6.4 %collective-permute-start.10 = (f32[54,128]{1,0:T(8,128)}, f32[54,128]{1,0:T(8,128)}, u32[]{:S(2)}, u32[]{:S(2)}) collective-permute-start(f32[54,128]{1,0:T(8,128)} %add.89), channel_id=1, source_target_pairs={{0,128},{1,129},{2,130},{3,131},{32,160},{33,161},{34,162},{35,163... | collective-permute-start | bytes 82952 | tf_op jit(solution)/shard_map/ppermute | solution.py:33
  169.3 4.2 %collective-permute-start.11 = (f32[54,128]{1,0:T(8,128)S(1)}, f32[54,128]{1,0:T(8,128)S(1)}, u32[]{:S(2)}, u32[]{:S(2)}) collective-permute-start(f32[54,128]{1,0:T(8,128)S(1)} %add.90), channel_id=1, source_target_pairs={{0,256},{1,257},{2,258},{3,259},{32,288},{33,289},{34,290},{35,291... | collective-permute-start | bytes 82952 | tf_op jit(solution)/shard_map/ppermute | solution.py:33
  174.6 4.6 %collective-permute-start.16 = (f32[1,2,2,32,256]{4,3,2,1,0:T(8,128)S(1)}, f32[1,2,2,32,256]{4,3,2,1,0:T(8,128)S(1)}, u32[]{:S(2)}, u32[]{:S(2)}) collective-permute-start(f32[1,2,2,32,256]{4,3,2,1,0:T(8,128)S(1)} %dynamic-slice_bitcast_fusion.1), channel_id=1, source_target_pairs={{0,16},{4,20},{8,24},{12,28},{16,0},{20,4},{24,8},{28,12},{1,17},{... | collective-permute-start | bytes 393224 | tf_op jit(solution)/shard_map/ppermute | solution.py:130
  180.7 6.1 %collective-permute-done.16 = f32[1,2,2,32,256]{4,3,2,1,0:T(8,128)S(1)} collective-permute-done((f32[1,2,2,32,256]{4,3,2,1,0:T(8,128)S(1)}, f32[1,2,2,32,256]{4,3,2,1,0:T(8,128)S(1)}, u32[]{:S(2)}, u32[]{:S(2)}) %collective-permute-start.16) | collective-permute-done | bytes 131104 | tf_op jit(solution)/shard_map/ppermute | solution.py:130
  (116 shorter events, 45.2 us)
Async XLA Ops:
  1.4 3.0 %collective-permute-start = (bf16[1,4,1,4,512]{4,3,2,1,0:T(4,128)(2,1)S(1)}, bf16[1,4,1,4,512]{4,3,2,1,0:T(4,128)(2,1)S(1)}, u32[]{:S(2)}, u32[]{:S(2)}) collective-permute-start(bf16[1,4,1,4,512]{4,3,2,1,0:T(4,128)(2,1)S(1)} %get-tuple-element.58), channel_id=1, source_target_pairs={{0,32},{32,64},{64,96},{96,128},{128,160},{160,192},{192,224},{224... | collective-permute-start | bytes 49160 | tf_op jit(solution)/shard_map/ppermute | solution.py:15
  3.1 4.4 %collective-permute-start.1 = (bf16[1,4,1,4,512]{4,3,2,1,0:T(4,128)(2,1)S(1)}, bf16[1,4,1,4,512]{4,3,2,1,0:T(4,128)(2,1)S(1)}, u32[]{:S(2)}, u32[]{:S(2)}) collective-permute-start(bf16[1,4,1,4,512]{4,3,2,1,0:T(4,128)(2,1)S(1)} %get-tuple-element.57), channel_id=1, source_target_pairs={{32,0},{64,32},{96,64},{128,96},{160,128},{192,160},{224,192},{256... | collective-permute-start | bytes 49160 | tf_op jit(solution)/shard_map/ppermute | solution.py:18
  7.6 8.8 %collective-permute-start.2 = (bf16[1,4,6,1,512]{4,3,2,1,0:T(2,128)(2,1)S(1)}, bf16[1,4,6,1,512]{4,3,2,1,0:T(2,128)(2,1)S(1)}, u32[]{:S(2)}, u32[]{:S(2)}) collective-permute-start(bf16[1,4,6,1,512]{4,3,2,1,0:T(2,128)(2,1)S(1)} %get-tuple-element.55), channel_id=1, source_target_pairs={{0,4},{4,8},{8,12},{12,16},{16,20},{20,24},{24,28},{1,5},{5,9},{9,... | collective-permute-start | bytes 73736 | tf_op jit(solution)/shard_map/ppermute | solution.py:15
  11.1 6.0 %collective-permute-start.3 = (bf16[1,4,6,1,512]{4,3,2,1,0:T(2,128)(2,1)S(1)}, bf16[1,4,6,1,512]{4,3,2,1,0:T(2,128)(2,1)S(1)}, u32[]{:S(2)}, u32[]{:S(2)}) collective-permute-start(bf16[1,4,6,1,512]{4,3,2,1,0:T(2,128)(2,1)S(1)} %get-tuple-element.56), channel_id=1, source_target_pairs={{4,0},{8,4},{12,8},{16,12},{20,16},{24,20},{28,24},{5,1},{9,5},{13... | collective-permute-start | bytes 73736 | tf_op jit(solution)/shard_map/ppermute | solution.py:18
  33.6 0.7 copy-start.1
  49.9 31.0 %copy-start.3 = (bf16[8,864]{1,0:T(8,128)(2,1)S(1)}, bf16[8,864]{1,0:T(8,128)(2,1)}, u32[]{:S(2)}) copy-start(bf16[8,864]{1,0:T(8,128)(2,1)} %param.6) | copy-start | bytes 41476
  49.9 32.8 %copy-start.2 = (bf16[1,8,1,1024]{3,1,2,0:T(8,128)(2,1)S(1)}, bf16[1,8,1,1024]{3,1,2,0:T(8,128)(2,1)}, u32[]{:S(2)}) copy-start(bf16[1,8,1,1024]{3,1,2,0:T(8,128)(2,1)} %param.7) | copy-start | bytes 49156
  78.3 5.4 %collective-permute-start.4 = (bf16[1,32,1,16,256]{4,1,3,2,0:T(8,128)(2,1)S(1)}, bf16[1,32,1,16,256]{4,1,3,2,0:T(8,128)(2,1)S(1)}, u32[]{:S(2)}, u32[]{:S(2)}) collective-permute-start(bf16[1,32,1,16,256]{4,1,3,2,0:T(8,128)(2,1)S(1)} %get-tuple-element.41), channel_id=1, source_target_pairs={{0,32},{32,64},{64,96},{96,128},{128,160},{160,192},{192,224},{224... | collective-permute-start | bytes 786440 | tf_op jit(solution)/shard_map/ppermute | solution.py:15
  79.6 6.0 %collective-permute-start.5 = (bf16[1,32,1,16,256]{4,1,3,2,0:T(8,128)(2,1)S(1)}, bf16[1,32,1,16,256]{4,1,3,2,0:T(8,128)(2,1)S(1)}, u32[]{:S(2)}, u32[]{:S(2)}) collective-permute-start(bf16[1,32,1,16,256]{4,1,3,2,0:T(8,128)(2,1)S(1)} %get-tuple-element.42), channel_id=1, source_target_pairs={{32,0},{64,32},{96,64},{128,96},{160,128},{192,160},{224,192},{256... | collective-permute-start | bytes 786440 | tf_op jit(solution)/shard_map/ppermute | solution.py:18
  88.5 2.8 %copy-start = (bf16[8,3,32,3,3]{2,0,4,3,1:T(8,128)(2,1)S(1)}, bf16[8,3,32,3,3]{2,0,4,3,1:T(8,128)(2,1)}, u32[]{:S(2)}) copy-start(bf16[8,3,32,3,3]{2,0,4,3,1:T(8,128)(2,1)} %copy.364) | copy-start | bytes 41476
  94.1 8.2 %collective-permute-start.12 = (bf16[1,8,1,16,256]{4,1,3,2,0:T(8,128)(2,1)S(1)}, bf16[1,8,1,16,256]{4,1,3,2,0:T(8,128)(2,1)S(1)}, u32[]{:S(2)}, u32[]{:S(2)}) collective-permute-start(bf16[1,8,1,16,256]{4,1,3,2,0:T(8,128)(2,1)S(1)} %get-tuple-element.53), channel_id=1, source_target_pairs={{0,32},{32,64},{64,96},{96,128},{128,160},{160,192},{192,224},{224... | collective-permute-start | bytes 196616 | tf_op jit(solution)/shard_map/ppermute | solution.py:15
  100.8 3.1 %collective-permute-start.13 = (bf16[1,8,1,16,256]{4,1,3,2,0:T(8,128)(2,1)S(1)}, bf16[1,8,1,16,256]{4,1,3,2,0:T(8,128)(2,1)S(1)}, u32[]{:S(2)}, u32[]{:S(2)}) collective-permute-start(bf16[1,8,1,16,256]{4,1,3,2,0:T(8,128)(2,1)S(1)} %get-tuple-element.54), channel_id=1, source_target_pairs={{32,0},{64,32},{96,64},{128,96},{160,128},{192,160},{224,192},{256... | collective-permute-start | bytes 196616 | tf_op jit(solution)/shard_map/ppermute | solution.py:18
  106.3 15.0 %collective-permute-start.14 = (f32[2,2,1,2,2,32,256]{6,5,4,3,0,2,1:T(8,128)S(1)}, f32[2,2,1,2,2,32,256]{6,5,4,3,0,2,1:T(8,128)S(1)}, u32[]{:S(2)}, u32[]{:S(2)}) collective-permute-start(f32[2,2,1,2,2,32,256]{6,5,4,3,0,2,1:T(8,128)S(1)} %copy.386), channel_id=1, source_target_pairs={{0,4},{4,0},{8,12},{12,8},{16,20},{20,16},{24,28},{28,24},{1,5},{5... | collective-permute-start | bytes 1572872 | tf_op jit(solution)/shard_map/ppermute | solution.py:130
  121.4 52.1 %collective-permute-start.15 = (f32[2,1,2,2,32,256]{5,4,3,2,0,1:T(8,128)S(1)}, f32[2,1,2,2,32,256]{5,4,3,2,0,1:T(8,128)}, u32[]{:S(2)}, u32[]{:S(2)}) collective-permute-start(f32[2,1,2,2,32,256]{5,4,3,2,0,1:T(8,128)S(1)} %dynamic-slice_bitcast_fusion), channel_id=1, source_target_pairs={{0,8},{4,12},{8,0},{12,4},{16,24},{20,28},{24,16},{28,20},{1,9},{5... | collective-permute-start | bytes 786440 | tf_op jit(solution)/shard_map/ppermute | solution.py:130
  129.5 7.9 %collective-permute-start.6 = (f32[54,128]{1,0:T(8,128)S(1)}, f32[54,128]{1,0:T(8,128)S(1)}, u32[]{:S(2)}, u32[]{:S(2)}) collective-permute-start(f32[54,128]{1,0:T(8,128)S(1)} %mul.80), channel_id=1, source_target_pairs={{0,1},{1,0},{2,3},{3,2},{32,33},{33,32},{34,35},{35,34},{64,65},{6... | collective-permute-start | bytes 82952 | tf_op jit(solution)/shard_map/ppermute | solution.py:33
  137.4 11.5 %collective-permute-start.7 = (f32[54,128]{1,0:T(8,128)S(1)}, f32[54,128]{1,0:T(8,128)S(1)}, u32[]{:S(2)}, u32[]{:S(2)}) collective-permute-start(f32[54,128]{1,0:T(8,128)S(1)} %add.86), channel_id=1, source_target_pairs={{0,2},{1,3},{2,0},{3,1},{32,34},{33,35},{34,32},{35,33},{64,66},{6... | collective-permute-start | bytes 82952 | tf_op jit(solution)/shard_map/ppermute | solution.py:33
  148.9 3.1 %collective-permute-start.8 = (f32[54,128]{1,0:T(8,128)S(1)}, f32[54,128]{1,0:T(8,128)S(1)}, u32[]{:S(2)}, u32[]{:S(2)}) collective-permute-start(f32[54,128]{1,0:T(8,128)S(1)} %add.87), channel_id=1, source_target_pairs={{0,32},{1,33},{2,34},{3,35},{32,0},{33,1},{34,2},{35,3},{64,96},{6... | collective-permute-start | bytes 82952 | tf_op jit(solution)/shard_map/ppermute | solution.py:33
  152.0 7.1 %collective-permute-start.9 = (f32[54,128]{1,0:T(8,128)S(1)}, f32[54,128]{1,0:T(8,128)S(1)}, u32[]{:S(2)}, u32[]{:S(2)}) collective-permute-start(f32[54,128]{1,0:T(8,128)S(1)} %add.88), channel_id=1, source_target_pairs={{0,64},{1,65},{2,66},{3,67},{32,96},{33,97},{34,98},{35,99},{64,0}... | collective-permute-start | bytes 82952 | tf_op jit(solution)/shard_map/ppermute | solution.py:33
  159.8 8.8 %collective-permute-start.10 = (f32[54,128]{1,0:T(8,128)}, f32[54,128]{1,0:T(8,128)}, u32[]{:S(2)}, u32[]{:S(2)}) collective-permute-start(f32[54,128]{1,0:T(8,128)} %add.89), channel_id=1, source_target_pairs={{0,128},{1,129},{2,130},{3,131},{32,160},{33,161},{34,162},{35,163... | collective-permute-start | bytes 82952 | tf_op jit(solution)/shard_map/ppermute | solution.py:33
  169.3 10.6 %collective-permute-start.11 = (f32[54,128]{1,0:T(8,128)S(1)}, f32[54,128]{1,0:T(8,128)S(1)}, u32[]{:S(2)}, u32[]{:S(2)}) collective-permute-start(f32[54,128]{1,0:T(8,128)S(1)} %add.90), channel_id=1, source_target_pairs={{0,256},{1,257},{2,258},{3,259},{32,288},{33,289},{34,290},{35,291... | collective-permute-start | bytes 82952 | tf_op jit(solution)/shard_map/ppermute | solution.py:33
  174.6 12.1 %collective-permute-start.16 = (f32[1,2,2,32,256]{4,3,2,1,0:T(8,128)S(1)}, f32[1,2,2,32,256]{4,3,2,1,0:T(8,128)S(1)}, u32[]{:S(2)}, u32[]{:S(2)}) collective-permute-start(f32[1,2,2,32,256]{4,3,2,1,0:T(8,128)S(1)} %dynamic-slice_bitcast_fusion.1), channel_id=1, source_target_pairs={{0,16},{4,20},{8,24},{12,28},{16,0},{20,4},{24,8},{28,12},{1,17},{... | collective-permute-start | bytes 393224 | tf_op jit(solution)/shard_map/ppermute | solution.py:130

commit v5 on v3

--- a/solution.py
+++ b/solution.py
@@ -27,9 +27,16 @@
         count *= size
     if count & (count - 1):
         return lax.psum(values, axes)
+    inner = lax.axis_size(axes[-1])
+
+    def label(i):
+        low = i % inner
+        return i - low + (low ^ (low >> 1))
+
+    owner = {label(i): i for i in range(count)}
     step = 1
     while step < count:
-        pairs = [(i, i ^ step) for i in range(count)]
+        pairs = [(i, owner[label(i) ^ step]) for i in range(count)]
         values = values + lax.ppermute(values, axes, pairs)
         step *= 2
     return values

time: 185 us -> 185 us (level)
  no operation moved by 1% of the time
where the time goes in v5:
time: 185 us; the launch traced here: 183 us
  starting transfers between devices  65.8 us (36%)
  local copies, waits for them, and re-layouts  39.8 us (22%)
  waiting for transfers between devices  31.5 us (17%)
  blocking collectives  27.9 us (15%)
  other arithmetic  10.1 us (5%)
  matrix products  6.18 us (3%)
    ppermute x6, starting transfers between devices, butterfly_sum(): values = values + lax.ppermute(values, axes, pairs)  33.7 us
    all_gather x1, blocking collectives, shards(): slab_rows = lax.all_gather(level_loc, 'height', axis=3, tiled=True)  27.9 us
    ppermute x3, waiting for transfers between devices, near_first_scatter(): grid = jnp.squeeze(keep + lax.ppermute(send, axis, pairs), axis_pos)  18.8 us
    another operation x14, local copies, waits for them, and re-layouts, delta_shifts(): jnp.stack([dpad[:, :, 2 - kh:2 - kh + hsize, 2 - kw:2 - kw + wsize] for k...  18.5 us
    ppermute x4, starting transfers between devices, extended(): lax.ppermute(lax.slice_in_dim(block, block.shape[dim] - width, None, axis...  13.2 us
    ppermute x3, starting transfers between devices, near_first_scatter(): grid = jnp.squeeze(keep + lax.ppermute(send, axis, pairs), axis_pos)  11.1 us
    ppermute x4, starting transfers between devices, extended(): lax.ppermute(lax.slice_in_dim(block, 0, width, axis=dim), axis, backward)  7.84 us
    unnamed x37, local copies, waits for them, and re-layouts  7.03 us
  transfers between devices with their start and end apart: 17, of which 10 were waited for; matrix products, arithmetic and copies ran while one was open for 8% of the time, Pallas kernels for 0%

profile of v5, /device:TPU:8, one launch (start us, length us, event | category | flops | bytes accessed | tf_op | source)
XLA Modules:
  0.0 182.7 jit_solution(8363752191844550454)
XLA Ops:
  5.3 2.2 %collective-permute-done.1 = bf16[1,4,1,4,512]{4,3,2,1,0:T(4,128)(2,1)S(1)} collective-permute-done((bf16[1,4,1,4,512]{4,3,2,1,0:T(4,128)(2,1)S(1)}, bf16[1,4,1,4,512]{4,3,2,1,0:T(4,128)(2,1)S(1)}, u32[]{:S(2)}, u32[]{:S(2)}) %collective-permute-start.1) | collective-permute-done | bytes 16416 | tf_op jit(solution)/shard_map/ppermute | solution.py:18
  7.6 3.5 %collective-permute-start.2 = (bf16[1,4,6,1,512]{4,3,2,1,0:T(2,128)(2,1)S(1)}, bf16[1,4,6,1,512]{4,3,2,1,0:T(2,128)(2,1)S(1)}, u32[]{:S(2)}, u32[]{:S(2)}) collective-permute-start(bf16[1,4,6,1,512]{4,3,2,1,0:T(2,128)(2,1)S(1)} %get-tuple-element.57), channel_id=1, source_target_pairs={{0,4},{4,8},{8,12},{12,16},{16,20},{20,24},{24,28},{1,5},{5,9},{9,... | collective-permute-start | bytes 73736 | tf_op jit(solution)/shard_map/ppermute | solution.py:15
  11.1 3.8 %collective-permute-start.3 = (bf16[1,4,6,1,512]{4,3,2,1,0:T(2,128)(2,1)S(1)}, bf16[1,4,6,1,512]{4,3,2,1,0:T(2,128)(2,1)S(1)}, u32[]{:S(2)}, u32[]{:S(2)}) collective-permute-start(bf16[1,4,6,1,512]{4,3,2,1,0:T(2,128)(2,1)S(1)} %get-tuple-element.58), channel_id=1, source_target_pairs={{4,0},{8,4},{12,8},{16,12},{20,16},{24,20},{28,24},{5,1},{9,5},{13... | collective-permute-start | bytes 73736 | tf_op jit(solution)/shard_map/ppermute | solution.py:18
  23.7 11.4 %stack.168 = bf16[4,9,6,6,512]{4,1,0,3,2:T(8,128)(2,1)S(1)} concatenate(bf16[4,1,6,6,512]{4,1,0,3,2:T(2,128)(2,1)S(1)} %copy.378, bf16[4,1,6,6,512]{4,1,0,3,2:T(2,128)(2,1)S(1)} %copy.379, bf16[4,1,6,6,512]{4,1,0,3,2:T(2,128)(2,1)S(1)} %copy.380, bf16[4,1,6,6,512]{4,1,0,3,2:T(2,128)(2,1)S(1)} %copy.381, bf16[4,1,6,6,512]{4,1,0,3,2:T(2,128)(2,1)} %copy.382, ...), dimensions={1} | concatenate | bytes 2654208 | tf_op jit(solution)/shard_map/stack | solution.py:65
  37.9 2.6 %copy.392 = f32[1,32,4,4,512]{1,4,3,2,0:T(8,128)} copy(f32[1,32,4,4,512]{4,1,3,2,0:T(8,128)S(1)} %fusion.61) | data formatting | bytes 2097152 | tf_op jit(solution)/shard_map/add | solution.py:142
  40.5 4.8 %reduce_sum.21 = f32[32,2,2,256]{0,3,2,1:T(8,128)S(1)} reduce(f32[32,2,2,2,2,256,2]{0,6,5,4,3,2,1:T(2,128)} %bitcast.266, f32[]{:T(128)} %constant.17.clone.1), dimensions={2,4,6}, to_apply=%region_0.1 | reduce | flops 229376 | bytes 1179652 | tf_op jit(solution)/shard_map/reduce_sum | solution.py:152
  45.5 27.9 %all-gather = bf16[32,2,16,256]{3,0,2,1:T(8,128)(2,1)S(1)} all-gather(bf16[32,2,2,256]{3,0,2,1:T(8,128)(2,1)S(1)} %multiply_convert_fusion.2), channel_id=2, replica_groups=mesh['depth'=16,'height'=8,'sample'=4] {'height'}, dimensions={2}, use_global_device_ids=true | all-gather | bytes 589824 | tf_op jit(solution)/shard_map/all_gather | solution.py:198
  83.8 2.8 %slice_bitcast_fusion.2 = (bf16[1,32,9,2,16,256]{5,1,2,0,4,3:T(8,128)(2,1)S(1)}, bf16[1,32,9,2,16,256]{5,1,2,0,4,3:T(8,128)(2,1)S(1)}, bf16[1,32,9,2,16,256]{5,1,2,0,4,3:T(8,128)(2,1)S(1)}) fusion(bf16[32,9,4,16,256]{4,0,1,3,2:T(8,128)(2,1)S(1)} %fusion.59), kind=kLoop, calls=%fused_computation.8 | loop fusion | bytes 28311552 | tf_op jit(solution)/shard_map/stack | solution.py:109
  86.5 2.6 %multiply_convert_fusion.1 = (bf16[8,2,16,256]{3,0,2,1:T(8,128)(2,1)S(1)}, f32[8,16,256]{2,0,1:T(8,128)S(1)}) fusion(f32[8,16,256]{2,0,1:T(8,128)S(1)} %copy.408, bf16[8,3,32,9,1,1]{2,0,3,1,5,4:T(8,128)(2,1)S(1)} %bitcast.281, bf16[1,32,9,2,16,256]{5,1,2,0,4,3:T(8,128)(2,1)S(1)} %get-tuple-element.31, ...), kind=kOutput, calls=%fused_computation.113 | convolution fusion | flops 128483328 | bytes 14562816 | tf_op jit(solution)/shard_map/dot_general | solution.py:112
  89.3 6.7 %collective-permute-start.12 = (bf16[1,8,1,16,256]{4,1,3,2,0:T(8,128)(2,1)S(1)}, bf16[1,8,1,16,256]{4,1,3,2,0:T(8,128)(2,1)S(1)}, u32[]{:S(2)}, u32[]{:S(2)}) collective-permute-start(bf16[1,8,1,16,256]{4,1,3,2,0:T(8,128)(2,1)S(1)} %get-tuple-element.55), channel_id=1, source_target_pairs={{0,32},{32,64},{64,96},{96,128},{128,160},{160,192},{192,224},{224... | collective-permute-start | bytes 196616 | tf_op jit(solution)/shard_map/ppermute | solution.py:15
  101.6 1.9 %collective-permute-start.14 = (f32[2,2,1,2,2,32,256]{6,5,4,3,0,2,1:T(8,128)S(1)}, f32[2,2,1,2,2,32,256]{6,5,4,3,0,2,1:T(8,128)S(1)}, u32[]{:S(2)}, u32[]{:S(2)}) collective-permute-start(f32[2,2,1,2,2,32,256]{6,5,4,3,0,2,1:T(8,128)S(1)} %copy.444), channel_id=1, source_target_pairs={{0,4},{4,0},{8,12},{12,8},{16,20},{20,16},{24,28},{28,24},{1,5},{5... | collective-permute-start | bytes 1572872 | tf_op jit(solution)/shard_map/ppermute | solution.py:137
  103.9 12.7 %collective-permute-done.14 = f32[2,2,1,2,2,32,256]{6,5,4,3,0,2,1:T(8,128)S(1)} collective-permute-done((f32[2,2,1,2,2,32,256]{6,5,4,3,0,2,1:T(8,128)S(1)}, f32[2,2,1,2,2,32,256]{6,5,4,3,0,2,1:T(8,128)S(1)}, u32[]{:S(2)}, u32[]{:S(2)}) %collective-permute-start.14) | collective-permute-done | bytes 524320 | tf_op jit(solution)/shard_map/ppermute | solution.py:137
  116.7 4.6 %collective-permute-start.15 = (f32[2,1,2,2,32,256]{5,4,3,2,0,1:T(8,128)S(1)}, f32[2,1,2,2,32,256]{5,4,3,2,0,1:T(8,128)}, u32[]{:S(2)}, u32[]{:S(2)}) collective-permute-start(f32[2,1,2,2,32,256]{5,4,3,2,0,1:T(8,128)S(1)} %dynamic-slice_bitcast_fusion), channel_id=1, source_target_pairs={{0,8},{4,12},{8,0},{12,4},{16,24},{20,28},{24,16},{28,20},{1,9},{5... | collective-permute-start | bytes 786440 | tf_op jit(solution)/shard_map/ppermute | solution.py:137
  124.7 6.1 %collective-permute-start.6 = (f32[54,128]{1,0:T(8,128)S(1)}, f32[54,128]{1,0:T(8,128)S(1)}, u32[]{:S(2)}, u32[]{:S(2)}) collective-permute-start(f32[54,128]{1,0:T(8,128)S(1)} %mul.80), channel_id=1, source_target_pairs={{0,1},{1,0},{2,3},{3,2},{32,33},{33,32},{34,35},{35,34},{64,65},{6... | collective-permute-start | bytes 82952 | tf_op jit(solution)/shard_map/ppermute | solution.py:40
  130.8 1.8 %collective-permute-done.6 = f32[54,128]{1,0:T(8,128)S(1)} collective-permute-done((f32[54,128]{1,0:T(8,128)S(1)}, f32[54,128]{1,0:T(8,128)S(1)}, u32[]{:S(2)}, u32[]{:S(2)}) %collective-permute-start.6) | collective-permute-done | bytes 27680 | tf_op jit(solution)/shard_map/ppermute | solution.py:40
  132.6 9.7 %collective-permute-start.7 = (f32[54,128]{1,0:T(8,128)S(1)}, f32[54,128]{1,0:T(8,128)S(1)}, u32[]{:S(2)}, u32[]{:S(2)}) collective-permute-start(f32[54,128]{1,0:T(8,128)S(1)} %add.86), channel_id=1, source_target_pairs={{0,3},{1,2},{2,1},{3,0},{32,35},{33,34},{34,33},{35,32},{64,67},{6... | collective-permute-start | bytes 82952 | tf_op jit(solution)/shard_map/ppermute | solution.py:40
  142.3 1.8 %collective-permute-done.7 = f32[54,128]{1,0:T(8,128)S(1)} collective-permute-done((f32[54,128]{1,0:T(8,128)S(1)}, f32[54,128]{1,0:T(8,128)S(1)}, u32[]{:S(2)}, u32[]{:S(2)}) %collective-permute-start.7) | collective-permute-done | bytes 27680 | tf_op jit(solution)/shard_map/ppermute | solution.py:40
  144.1 1.9 %collective-permute-start.8 = (f32[54,128]{1,0:T(8,128)S(1)}, f32[54,128]{1,0:T(8,128)S(1)}, u32[]{:S(2)}, u32[]{:S(2)}) collective-permute-start(f32[54,128]{1,0:T(8,128)S(1)} %add.87), channel_id=1, source_target_pairs={{0,32},{1,33},{2,34},{3,35},{32,0},{33,1},{34,2},{35,3},{64,96},{6... | collective-permute-start | bytes 82952 | tf_op jit(solution)/shard_map/ppermute | solution.py:40
  147.2 5.3 %collective-permute-start.9 = (f32[54,128]{1,0:T(8,128)S(1)}, f32[54,128]{1,0:T(8,128)S(1)}, u32[]{:S(2)}, u32[]{:S(2)}) collective-permute-start(f32[54,128]{1,0:T(8,128)S(1)} %add.88), channel_id=1, source_target_pairs={{0,64},{1,65},{2,66},{3,67},{32,96},{33,97},{34,98},{35,99},{64,0}... | collective-permute-start | bytes 82952 | tf_op jit(solution)/shard_map/ppermute | solution.py:40
  152.6 1.8 %collective-permute-done.9 = f32[54,128]{1,0:T(8,128)S(1)} collective-permute-done((f32[54,128]{1,0:T(8,128)S(1)}, f32[54,128]{1,0:T(8,128)S(1)}, u32[]{:S(2)}, u32[]{:S(2)}) %collective-permute-start.9) | collective-permute-done | bytes 27680 | tf_op jit(solution)/shard_map/ppermute | solution.py:40
  155.0 6.4 %collective-permute-start.10 = (f32[54,128]{1,0:T(8,128)}, f32[54,128]{1,0:T(8,128)}, u32[]{:S(2)}, u32[]{:S(2)}) collective-permute-start(f32[54,128]{1,0:T(8,128)} %add.89), channel_id=1, source_target_pairs={{0,128},{1,129},{2,130},{3,131},{32,160},{33,161},{34,162},{35,163... | collective-permute-start | bytes 82952 | tf_op jit(solution)/shard_map/ppermute | solution.py:40
  164.6 4.2 %collective-permute-start.11 = (f32[54,128]{1,0:T(8,128)S(1)}, f32[54,128]{1,0:T(8,128)S(1)}, u32[]{:S(2)}, u32[]{:S(2)}) collective-permute-start(f32[54,128]{1,0:T(8,128)S(1)} %add.90), channel_id=1, source_target_pairs={{0,256},{1,257},{2,258},{3,259},{32,288},{33,289},{34,290},{35,291... | collective-permute-start | bytes 82952 | tf_op jit(solution)/shard_map/ppermute | solution.py:40
  169.8 4.6 %collective-permute-start.16 = (f32[1,2,2,32,256]{4,3,2,1,0:T(8,128)S(1)}, f32[1,2,2,32,256]{4,3,2,1,0:T(8,128)S(1)}, u32[]{:S(2)}, u32[]{:S(2)}) collective-permute-start(f32[1,2,2,32,256]{4,3,2,1,0:T(8,128)S(1)} %dynamic-slice_bitcast_fusion.1), channel_id=1, source_target_pairs={{0,16},{4,20},{8,24},{12,28},{16,0},{20,4},{24,8},{28,12},{1,17},{... | collective-permute-start | bytes 393224 | tf_op jit(solution)/shard_map/ppermute | solution.py:137
  175.9 6.1 %collective-permute-done.16 = f32[1,2,2,32,256]{4,3,2,1,0:T(8,128)S(1)} collective-permute-done((f32[1,2,2,32,256]{4,3,2,1,0:T(8,128)S(1)}, f32[1,2,2,32,256]{4,3,2,1,0:T(8,128)S(1)}, u32[]{:S(2)}, u32[]{:S(2)}) %collective-permute-start.16) | collective-permute-done | bytes 131104 | tf_op jit(solution)/shard_map/ppermute | solution.py:137
  (114 shorter events, 44.1 us)
Async XLA Ops:
  1.4 3.0 %collective-permute-start = (bf16[1,4,1,4,512]{4,3,2,1,0:T(4,128)(2,1)S(1)}, bf16[1,4,1,4,512]{4,3,2,1,0:T(4,128)(2,1)S(1)}, u32[]{:S(2)}, u32[]{:S(2)}) collective-permute-start(bf16[1,4,1,4,512]{4,3,2,1,0:T(4,128)(2,1)S(1)} %get-tuple-element.60), channel_id=1, source_target_pairs={{0,32},{32,64},{64,96},{96,128},{128,160},{160,192},{192,224},{224... | collective-permute-start | bytes 49160 | tf_op jit(solution)/shard_map/ppermute | solution.py:15
  3.1 4.4 %collective-permute-start.1 = (bf16[1,4,1,4,512]{4,3,2,1,0:T(4,128)(2,1)S(1)}, bf16[1,4,1,4,512]{4,3,2,1,0:T(4,128)(2,1)S(1)}, u32[]{:S(2)}, u32[]{:S(2)}) collective-permute-start(bf16[1,4,1,4,512]{4,3,2,1,0:T(4,128)(2,1)S(1)} %get-tuple-element.59), channel_id=1, source_target_pairs={{32,0},{64,32},{96,64},{128,96},{160,128},{192,160},{224,192},{256... | collective-permute-start | bytes 49160 | tf_op jit(solution)/shard_map/ppermute | solution.py:18
  7.6 8.8 %collective-permute-start.2 = (bf16[1,4,6,1,512]{4,3,2,1,0:T(2,128)(2,1)S(1)}, bf16[1,4,6,1,512]{4,3,2,1,0:T(2,128)(2,1)S(1)}, u32[]{:S(2)}, u32[]{:S(2)}) collective-permute-start(bf16[1,4,6,1,512]{4,3,2,1,0:T(2,128)(2,1)S(1)} %get-tuple-element.57), channel_id=1, source_target_pairs={{0,4},{4,8},{8,12},{12,16},{16,20},{20,24},{24,28},{1,5},{5,9},{9,... | collective-permute-start | bytes 73736 | tf_op jit(solution)/shard_map/ppermute | solution.py:15
  11.1 6.0 %collective-permute-start.3 = (bf16[1,4,6,1,512]{4,3,2,1,0:T(2,128)(2,1)S(1)}, bf16[1,4,6,1,512]{4,3,2,1,0:T(2,128)(2,1)S(1)}, u32[]{:S(2)}, u32[]{:S(2)}) collective-permute-start(bf16[1,4,6,1,512]{4,3,2,1,0:T(2,128)(2,1)S(1)} %get-tuple-element.58), channel_id=1, source_target_pairs={{4,0},{8,4},{12,8},{16,12},{20,16},{24,20},{28,24},{5,1},{9,5},{13... | collective-permute-start | bytes 73736 | tf_op jit(solution)/shard_map/ppermute | solution.py:18
  35.1 0.7 copy-start.1
  45.3 31.0 %copy-start.3 = (bf16[8,864]{1,0:T(8,128)(2,1)S(1)}, bf16[8,864]{1,0:T(8,128)(2,1)}, u32[]{:S(2)}) copy-start(bf16[8,864]{1,0:T(8,128)(2,1)} %param.6) | copy-start | bytes 41476
  45.3 32.8 %copy-start.2 = (bf16[1,8,1,1024]{3,1,2,0:T(8,128)(2,1)S(1)}, bf16[1,8,1,1024]{3,1,2,0:T(8,128)(2,1)}, u32[]{:S(2)}) copy-start(bf16[1,8,1,1024]{3,1,2,0:T(8,128)(2,1)} %param.7) | copy-start | bytes 49156
  73.5 5.6 %collective-permute-start.4 = (bf16[1,32,1,16,256]{4,1,3,2,0:T(8,128)(2,1)S(1)}, bf16[1,32,1,16,256]{4,1,3,2,0:T(8,128)(2,1)S(1)}, u32[]{:S(2)}, u32[]{:S(2)}) collective-permute-start(bf16[1,32,1,16,256]{4,1,3,2,0:T(8,128)(2,1)S(1)} %get-tuple-element.41), channel_id=1, source_target_pairs={{0,32},{32,64},{64,96},{96,128},{128,160},{160,192},{192,224},{224... | collective-permute-start | bytes 786440 | tf_op jit(solution)/shard_map/ppermute | solution.py:15
  74.8 6.0 %collective-permute-start.5 = (bf16[1,32,1,16,256]{4,1,3,2,0:T(8,128)(2,1)S(1)}, bf16[1,32,1,16,256]{4,1,3,2,0:T(8,128)(2,1)S(1)}, u32[]{:S(2)}, u32[]{:S(2)}) collective-permute-start(bf16[1,32,1,16,256]{4,1,3,2,0:T(8,128)(2,1)S(1)} %get-tuple-element.42), channel_id=1, source_target_pairs={{32,0},{64,32},{96,64},{128,96},{160,128},{192,160},{224,192},{256... | collective-permute-start | bytes 786440 | tf_op jit(solution)/shard_map/ppermute | solution.py:18
  83.8 2.8 %copy-start = (bf16[8,3,32,3,3]{2,0,4,3,1:T(8,128)(2,1)S(1)}, bf16[8,3,32,3,3]{2,0,4,3,1:T(8,128)(2,1)}, u32[]{:S(2)}) copy-start(bf16[8,3,32,3,3]{2,0,4,3,1:T(8,128)(2,1)} %copy.405) | copy-start | bytes 41476
  89.3 8.2 %collective-permute-start.12 = (bf16[1,8,1,16,256]{4,1,3,2,0:T(8,128)(2,1)S(1)}, bf16[1,8,1,16,256]{4,1,3,2,0:T(8,128)(2,1)S(1)}, u32[]{:S(2)}, u32[]{:S(2)}) collective-permute-start(bf16[1,8,1,16,256]{4,1,3,2,0:T(8,128)(2,1)S(1)} %get-tuple-element.55), channel_id=1, source_target_pairs={{0,32},{32,64},{64,96},{96,128},{128,160},{160,192},{192,224},{224... | collective-permute-start | bytes 196616 | tf_op jit(solution)/shard_map/ppermute | solution.py:15
  96.0 3.1 %collective-permute-start.13 = (bf16[1,8,1,16,256]{4,1,3,2,0:T(8,128)(2,1)S(1)}, bf16[1,8,1,16,256]{4,1,3,2,0:T(8,128)(2,1)S(1)}, u32[]{:S(2)}, u32[]{:S(2)}) collective-permute-start(bf16[1,8,1,16,256]{4,1,3,2,0:T(8,128)(2,1)S(1)} %get-tuple-element.56), channel_id=1, source_target_pairs={{32,0},{64,32},{96,64},{128,96},{160,128},{192,160},{224,192},{256... | collective-permute-start | bytes 196616 | tf_op jit(solution)/shard_map/ppermute | solution.py:18
  101.6 15.0 %collective-permute-start.14 = (f32[2,2,1,2,2,32,256]{6,5,4,3,0,2,1:T(8,128)S(1)}, f32[2,2,1,2,2,32,256]{6,5,4,3,0,2,1:T(8,128)S(1)}, u32[]{:S(2)}, u32[]{:S(2)}) collective-permute-start(f32[2,2,1,2,2,32,256]{6,5,4,3,0,2,1:T(8,128)S(1)} %copy.444), channel_id=1, source_target_pairs={{0,4},{4,0},{8,12},{12,8},{16,20},{20,16},{24,28},{28,24},{1,5},{5... | collective-permute-start | bytes 1572872 | tf_op jit(solution)/shard_map/ppermute | solution.py:137
  116.7 52.1 %collective-permute-start.15 = (f32[2,1,2,2,32,256]{5,4,3,2,0,1:T(8,128)S(1)}, f32[2,1,2,2,32,256]{5,4,3,2,0,1:T(8,128)}, u32[]{:S(2)}, u32[]{:S(2)}) collective-permute-start(f32[2,1,2,2,32,256]{5,4,3,2,0,1:T(8,128)S(1)} %dynamic-slice_bitcast_fusion), channel_id=1, source_target_pairs={{0,8},{4,12},{8,0},{12,4},{16,24},{20,28},{24,16},{28,20},{1,9},{5... | collective-permute-start | bytes 786440 | tf_op jit(solution)/shard_map/ppermute | solution.py:137
  124.7 7.9 %collective-permute-start.6 = (f32[54,128]{1,0:T(8,128)S(1)}, f32[54,128]{1,0:T(8,128)S(1)}, u32[]{:S(2)}, u32[]{:S(2)}) collective-permute-start(f32[54,128]{1,0:T(8,128)S(1)} %mul.80), channel_id=1, source_target_pairs={{0,1},{1,0},{2,3},{3,2},{32,33},{33,32},{34,35},{35,34},{64,65},{6... | collective-permute-start | bytes 82952 | tf_op jit(solution)/shard_map/ppermute | solution.py:40
  132.6 11.5 %collective-permute-start.7 = (f32[54,128]{1,0:T(8,128)S(1)}, f32[54,128]{1,0:T(8,128)S(1)}, u32[]{:S(2)}, u32[]{:S(2)}) collective-permute-start(f32[54,128]{1,0:T(8,128)S(1)} %add.86), channel_id=1, source_target_pairs={{0,3},{1,2},{2,1},{3,0},{32,35},{33,34},{34,33},{35,32},{64,67},{6... | collective-permute-start | bytes 82952 | tf_op jit(solution)/shard_map/ppermute | solution.py:40
  144.1 3.1 %collective-permute-start.8 = (f32[54,128]{1,0:T(8,128)S(1)}, f32[54,128]{1,0:T(8,128)S(1)}, u32[]{:S(2)}, u32[]{:S(2)}) collective-permute-start(f32[54,128]{1,0:T(8,128)S(1)} %add.87), channel_id=1, source_target_pairs={{0,32},{1,33},{2,34},{3,35},{32,0},{33,1},{34,2},{35,3},{64,96},{6... | collective-permute-start | bytes 82952 | tf_op jit(solution)/shard_map/ppermute | solution.py:40
  147.2 7.2 %collective-permute-start.9 = (f32[54,128]{1,0:T(8,128)S(1)}, f32[54,128]{1,0:T(8,128)S(1)}, u32[]{:S(2)}, u32[]{:S(2)}) collective-permute-start(f32[54,128]{1,0:T(8,128)S(1)} %add.88), channel_id=1, source_target_pairs={{0,64},{1,65},{2,66},{3,67},{32,96},{33,97},{34,98},{35,99},{64,0}... | collective-permute-start | bytes 82952 | tf_op jit(solution)/shard_map/ppermute | solution.py:40
  155.0 8.8 %collective-permute-start.10 = (f32[54,128]{1,0:T(8,128)}, f32[54,128]{1,0:T(8,128)}, u32[]{:S(2)}, u32[]{:S(2)}) collective-permute-start(f32[54,128]{1,0:T(8,128)} %add.89), channel_id=1, source_target_pairs={{0,128},{1,129},{2,130},{3,131},{32,160},{33,161},{34,162},{35,163... | collective-permute-start | bytes 82952 | tf_op jit(solution)/shard_map/ppermute | solution.py:40
  164.6 10.6 %collective-permute-start.11 = (f32[54,128]{1,0:T(8,128)S(1)}, f32[54,128]{1,0:T(8,128)S(1)}, u32[]{:S(2)}, u32[]{:S(2)}) collective-permute-start(f32[54,128]{1,0:T(8,128)S(1)} %add.90), channel_id=1, source_target_pairs={{0,256},{1,257},{2,258},{3,259},{32,288},{33,289},{34,290},{35,291... | collective-permute-start | bytes 82952 | tf_op jit(solution)/shard_map/ppermute | solution.py:40
  169.8 12.1 %collective-permute-start.16 = (f32[1,2,2,32,256]{4,3,2,1,0:T(8,128)S(1)}, f32[1,2,2,32,256]{4,3,2,1,0:T(8,128)S(1)}, u32[]{:S(2)}, u32[]{:S(2)}) collective-permute-start(f32[1,2,2,32,256]{4,3,2,1,0:T(8,128)S(1)} %dynamic-slice_bitcast_fusion.1), channel_id=1, source_target_pairs={{0,16},{4,20},{8,24},{12,28},{16,0},{20,4},{24,8},{28,12},{1,17},{... | collective-permute-start | bytes 393224 | tf_op jit(solution)/shard_map/ppermute | solution.py:137

commit v6 on v5

--- a/solution.py
+++ b/solution.py
@@ -31,7 +31,9 @@
 
     def label(i):
         low = i % inner
-        return i - low + (low ^ (low >> 1))
+        i = i - low + (low ^ (low >> 1))
+        mid = (i // (inner * 2)) % 4
+        return i + (((mid ^ (mid >> 1)) - mid) * inner * 2)
 
     owner = {label(i): i for i in range(count)}
     step = 1

time: 185 us -> 184 us (level)
  no operation moved by 1% of the time
where the time goes in v6:
time: 184 us; the launch traced here: 182 us
  starting transfers between devices  65.5 us (36%)
  local copies, waits for them, and re-layouts  39.8 us (22%)
  waiting for transfers between devices  31.5 us (17%)
  blocking collectives  27.9 us (15%)
  other arithmetic  10.1 us (5%)
  matrix products  6.18 us (3%)
    ppermute x6, starting transfers between devices, butterfly_sum(): values = values + lax.ppermute(values, axes, pairs)  33.4 us
    all_gather x1, blocking collectives, shards(): slab_rows = lax.all_gather(level_loc, 'height', axis=3, tiled=True)  27.9 us
    ppermute x3, waiting for transfers between devices, near_first_scatter(): grid = jnp.squeeze(keep + lax.ppermute(send, axis, pairs), axis_pos)  18.7 us
    another operation x14, local copies, waits for them, and re-layouts, delta_shifts(): jnp.stack([dpad[:, :, 2 - kh:2 - kh + hsize, 2 - kw:2 - kw + wsize] for k...  18.5 us
    ppermute x4, starting transfers between devices, extended(): lax.ppermute(lax.slice_in_dim(block, block.shape[dim] - width, None, axis...  13.2 us
    ppermute x3, starting transfers between devices, near_first_scatter(): grid = jnp.squeeze(keep + lax.ppermute(send, axis, pairs), axis_pos)  11.1 us
    ppermute x4, starting transfers between devices, extended(): lax.ppermute(lax.slice_in_dim(block, 0, width, axis=dim), axis, backward)  7.84 us
    unnamed x37, local copies, waits for them, and re-layouts  7.03 us
  transfers between devices with their start and end apart: 17, of which 10 were waited for; matrix products, arithmetic and copies ran while one was open for 8% of the time, Pallas kernels for 0%

profile of v6, /device:TPU:8, one launch (start us, length us, event | category | flops | bytes accessed | tf_op | source)
XLA Modules:
  0.0 182.4 jit_solution(10404301565494377352)
XLA Ops:
  5.3 2.2 %collective-permute-done.1 = bf16[1,4,1,4,512]{4,3,2,1,0:T(4,128)(2,1)S(1)} collective-permute-done((bf16[1,4,1,4,512]{4,3,2,1,0:T(4,128)(2,1)S(1)}, bf16[1,4,1,4,512]{4,3,2,1,0:T(4,128)(2,1)S(1)}, u32[]{:S(2)}, u32[]{:S(2)}) %collective-permute-start.1) | collective-permute-done | bytes 16416 | tf_op jit(solution)/shard_map/ppermute | solution.py:18
  7.6 3.5 %collective-permute-start.2 = (bf16[1,4,6,1,512]{4,3,2,1,0:T(2,128)(2,1)S(1)}, bf16[1,4,6,1,512]{4,3,2,1,0:T(2,128)(2,1)S(1)}, u32[]{:S(2)}, u32[]{:S(2)}) collective-permute-start(bf16[1,4,6,1,512]{4,3,2,1,0:T(2,128)(2,1)S(1)} %get-tuple-element.57), channel_id=1, source_target_pairs={{0,4},{4,8},{8,12},{12,16},{16,20},{20,24},{24,28},{1,5},{5,9},{9,... | collective-permute-start | bytes 73736 | tf_op jit(solution)/shard_map/ppermute | solution.py:15
  11.1 3.8 %collective-permute-start.3 = (bf16[1,4,6,1,512]{4,3,2,1,0:T(2,128)(2,1)S(1)}, bf16[1,4,6,1,512]{4,3,2,1,0:T(2,128)(2,1)S(1)}, u32[]{:S(2)}, u32[]{:S(2)}) collective-permute-start(bf16[1,4,6,1,512]{4,3,2,1,0:T(2,128)(2,1)S(1)} %get-tuple-element.58), channel_id=1, source_target_pairs={{4,0},{8,4},{12,8},{16,12},{20,16},{24,20},{28,24},{5,1},{9,5},{13... | collective-permute-start | bytes 73736 | tf_op jit(solution)/shard_map/ppermute | solution.py:18
  23.7 11.4 %stack.168 = bf16[4,9,6,6,512]{4,1,0,3,2:T(8,128)(2,1)S(1)} concatenate(bf16[4,1,6,6,512]{4,1,0,3,2:T(2,128)(2,1)S(1)} %copy.378, bf16[4,1,6,6,512]{4,1,0,3,2:T(2,128)(2,1)S(1)} %copy.379, bf16[4,1,6,6,512]{4,1,0,3,2:T(2,128)(2,1)S(1)} %copy.380, bf16[4,1,6,6,512]{4,1,0,3,2:T(2,128)(2,1)S(1)} %copy.381, bf16[4,1,6,6,512]{4,1,0,3,2:T(2,128)(2,1)} %copy.382, ...), dimensions={1} | concatenate | bytes 2654208 | tf_op jit(solution)/shard_map/stack | solution.py:67
  37.9 2.6 %copy.392 = f32[1,32,4,4,512]{1,4,3,2,0:T(8,128)} copy(f32[1,32,4,4,512]{4,1,3,2,0:T(8,128)S(1)} %fusion.61) | data formatting | bytes 2097152 | tf_op jit(solution)/shard_map/add | solution.py:144
  40.5 4.8 %reduce_sum.21 = f32[32,2,2,256]{0,3,2,1:T(8,128)S(1)} reduce(f32[32,2,2,2,2,256,2]{0,6,5,4,3,2,1:T(2,128)} %bitcast.266, f32[]{:T(128)} %constant.17.clone.1), dimensions={2,4,6}, to_apply=%region_0.1 | reduce | flops 229376 | bytes 1179652 | tf_op jit(solution)/shard_map/reduce_sum | solution.py:154
  45.5 27.9 %all-gather = bf16[32,2,16,256]{3,0,2,1:T(8,128)(2,1)S(1)} all-gather(bf16[32,2,2,256]{3,0,2,1:T(8,128)(2,1)S(1)} %multiply_convert_fusion.2), channel_id=2, replica_groups=mesh['depth'=16,'height'=8,'sample'=4] {'height'}, dimensions={2}, use_global_device_ids=true | all-gather | bytes 589824 | tf_op jit(solution)/shard_map/all_gather | solution.py:200
  83.8 2.8 %slice_bitcast_fusion.2 = (bf16[1,32,9,2,16,256]{5,1,2,0,4,3:T(8,128)(2,1)S(1)}, bf16[1,32,9,2,16,256]{5,1,2,0,4,3:T(8,128)(2,1)S(1)}, bf16[1,32,9,2,16,256]{5,1,2,0,4,3:T(8,128)(2,1)S(1)}) fusion(bf16[32,9,4,16,256]{4,0,1,3,2:T(8,128)(2,1)S(1)} %fusion.59), kind=kLoop, calls=%fused_computation.8 | loop fusion | bytes 28311552 | tf_op jit(solution)/shard_map/stack | solution.py:111
  86.5 2.6 %multiply_convert_fusion.1 = (bf16[8,2,16,256]{3,0,2,1:T(8,128)(2,1)S(1)}, f32[8,16,256]{2,0,1:T(8,128)S(1)}) fusion(f32[8,16,256]{2,0,1:T(8,128)S(1)} %copy.408, bf16[8,3,32,9,1,1]{2,0,3,1,5,4:T(8,128)(2,1)S(1)} %bitcast.281, bf16[1,32,9,2,16,256]{5,1,2,0,4,3:T(8,128)(2,1)S(1)} %get-tuple-element.31, ...), kind=kOutput, calls=%fused_computation.113 | convolution fusion | flops 128483328 | bytes 14562816 | tf_op jit(solution)/shard_map/dot_general | solution.py:114
  89.3 6.7 %collective-permute-start.12 = (bf16[1,8,1,16,256]{4,1,3,2,0:T(8,128)(2,1)S(1)}, bf16[1,8,1,16,256]{4,1,3,2,0:T(8,128)(2,1)S(1)}, u32[]{:S(2)}, u32[]{:S(2)}) collective-permute-start(bf16[1,8,1,16,256]{4,1,3,2,0:T(8,128)(2,1)S(1)} %get-tuple-element.55), channel_id=1, source_target_pairs={{0,32},{32,64},{64,96},{96,128},{128,160},{160,192},{192,224},{224... | collective-permute-start | bytes 196616 | tf_op jit(solution)/shard_map/ppermute | solution.py:15
  101.6 1.9 %collective-permute-start.14 = (f32[2,2,1,2,2,32,256]{6,5,4,3,0,2,1:T(8,128)S(1)}, f32[2,2,1,2,2,32,256]{6,5,4,3,0,2,1:T(8,128)S(1)}, u32[]{:S(2)}, u32[]{:S(2)}) collective-permute-start(f32[2,2,1,2,2,32,256]{6,5,4,3,0,2,1:T(8,128)S(1)} %copy.444), channel_id=1, source_target_pairs={{0,4},{4,0},{8,12},{12,8},{16,20},{20,16},{24,28},{28,24},{1,5},{5... | collective-permute-start | bytes 1572872 | tf_op jit(solution)/shard_map/ppermute | solution.py:139
  103.9 12.7 %collective-permute-done.14 = f32[2,2,1,2,2,32,256]{6,5,4,3,0,2,1:T(8,128)S(1)} collective-permute-done((f32[2,2,1,2,2,32,256]{6,5,4,3,0,2,1:T(8,128)S(1)}, f32[2,2,1,2,2,32,256]{6,5,4,3,0,2,1:T(8,128)S(1)}, u32[]{:S(2)}, u32[]{:S(2)}) %collective-permute-start.14) | collective-permute-done | bytes 524320 | tf_op jit(solution)/shard_map/ppermute | solution.py:139
  116.7 4.6 %collective-permute-start.15 = (f32[2,1,2,2,32,256]{5,4,3,2,0,1:T(8,128)S(1)}, f32[2,1,2,2,32,256]{5,4,3,2,0,1:T(8,128)}, u32[]{:S(2)}, u32[]{:S(2)}) collective-permute-start(f32[2,1,2,2,32,256]{5,4,3,2,0,1:T(8,128)S(1)} %dynamic-slice_bitcast_fusion), channel_id=1, source_target_pairs={{0,8},{4,12},{8,0},{12,4},{16,24},{20,28},{24,16},{28,20},{1,9},{5... | collective-permute-start | bytes 786440 | tf_op jit(solution)/shard_map/ppermute | solution.py:139
  124.7 6.1 %collective-permute-start.6 = (f32[54,128]{1,0:T(8,128)S(1)}, f32[54,128]{1,0:T(8,128)S(1)}, u32[]{:S(2)}, u32[]{:S(2)}) collective-permute-start(f32[54,128]{1,0:T(8,128)S(1)} %mul.80), channel_id=1, source_target_pairs={{0,1},{1,0},{2,3},{3,2},{32,33},{33,32},{34,35},{35,34},{64,65},{6... | collective-permute-start | bytes 82952 | tf_op jit(solution)/shard_map/ppermute | solution.py:42
  130.8 1.8 %collective-permute-done.6 = f32[54,128]{1,0:T(8,128)S(1)} collective-permute-done((f32[54,128]{1,0:T(8,128)S(1)}, f32[54,128]{1,0:T(8,128)S(1)}, u32[]{:S(2)}, u32[]{:S(2)}) %collective-permute-start.6) | collective-permute-done | bytes 27680 | tf_op jit(solution)/shard_map/ppermute | solution.py:42
  132.6 9.7 %collective-permute-start.7 = (f32[54,128]{1,0:T(8,128)S(1)}, f32[54,128]{1,0:T(8,128)S(1)}, u32[]{:S(2)}, u32[]{:S(2)}) collective-permute-start(f32[54,128]{1,0:T(8,128)S(1)} %add.86), channel_id=1, source_target_pairs={{0,3},{1,2},{2,1},{3,0},{32,35},{33,34},{34,33},{35,32},{64,67},{6... | collective-permute-start | bytes 82952 | tf_op jit(solution)/shard_map/ppermute | solution.py:42
  142.3 1.8 %collective-permute-done.7 = f32[54,128]{1,0:T(8,128)S(1)} collective-permute-done((f32[54,128]{1,0:T(8,128)S(1)}, f32[54,128]{1,0:T(8,128)S(1)}, u32[]{:S(2)}, u32[]{:S(2)}) %collective-permute-start.7) | collective-permute-done | bytes 27680 | tf_op jit(solution)/shard_map/ppermute | solution.py:42
  144.1 1.9 %collective-permute-start.8 = (f32[54,128]{1,0:T(8,128)S(1)}, f32[54,128]{1,0:T(8,128)S(1)}, u32[]{:S(2)}, u32[]{:S(2)}) collective-permute-start(f32[54,128]{1,0:T(8,128)S(1)} %add.87), channel_id=1, source_target_pairs={{0,32},{1,33},{2,34},{3,35},{32,0},{33,1},{34,2},{35,3},{64,96},{6... | collective-permute-start | bytes 82952 | tf_op jit(solution)/shard_map/ppermute | solution.py:42
  147.2 5.3 %collective-permute-start.9 = (f32[54,128]{1,0:T(8,128)S(1)}, f32[54,128]{1,0:T(8,128)S(1)}, u32[]{:S(2)}, u32[]{:S(2)}) collective-permute-start(f32[54,128]{1,0:T(8,128)S(1)} %add.88), channel_id=1, source_target_pairs={{0,64},{1,65},{2,66},{3,67},{32,96},{33,97},{34,98},{35,99},{64,0}... | collective-permute-start | bytes 82952 | tf_op jit(solution)/shard_map/ppermute | solution.py:42
  152.6 1.8 %collective-permute-done.9 = f32[54,128]{1,0:T(8,128)S(1)} collective-permute-done((f32[54,128]{1,0:T(8,128)S(1)}, f32[54,128]{1,0:T(8,128)S(1)}, u32[]{:S(2)}, u32[]{:S(2)}) %collective-permute-start.9) | collective-permute-done | bytes 27680 | tf_op jit(solution)/shard_map/ppermute | solution.py:42
  155.0 7.0 %collective-permute-start.10 = (f32[54,128]{1,0:T(8,128)}, f32[54,128]{1,0:T(8,128)}, u32[]{:S(2)}, u32[]{:S(2)}) collective-permute-start(f32[54,128]{1,0:T(8,128)} %add.89), channel_id=1, source_target_pairs={{0,192},{1,193},{2,194},{3,195},{32,224},{33,225},{34,226},{35,227... | collective-permute-start | bytes 82952 | tf_op jit(solution)/shard_map/ppermute | solution.py:42
  165.1 3.4 %collective-permute-start.11 = (f32[54,128]{1,0:T(8,128)S(1)}, f32[54,128]{1,0:T(8,128)S(1)}, u32[]{:S(2)}, u32[]{:S(2)}) collective-permute-start(f32[54,128]{1,0:T(8,128)S(1)} %add.90), channel_id=1, source_target_pairs={{0,256},{1,257},{2,258},{3,259},{32,288},{33,289},{34,290},{35,291... | collective-permute-start | bytes 82952 | tf_op jit(solution)/shard_map/ppermute | solution.py:42
  169.5 4.6 %collective-permute-start.16 = (f32[1,2,2,32,256]{4,3,2,1,0:T(8,128)S(1)}, f32[1,2,2,32,256]{4,3,2,1,0:T(8,128)S(1)}, u32[]{:S(2)}, u32[]{:S(2)}) collective-permute-start(f32[1,2,2,32,256]{4,3,2,1,0:T(8,128)S(1)} %dynamic-slice_bitcast_fusion.1), channel_id=1, source_target_pairs={{0,16},{4,20},{8,24},{12,28},{16,0},{20,4},{24,8},{28,12},{1,17},{... | collective-permute-start | bytes 393224 | tf_op jit(solution)/shard_map/ppermute | solution.py:139
  175.6 6.1 %collective-permute-done.16 = f32[1,2,2,32,256]{4,3,2,1,0:T(8,128)S(1)} collective-permute-done((f32[1,2,2,32,256]{4,3,2,1,0:T(8,128)S(1)}, f32[1,2,2,32,256]{4,3,2,1,0:T(8,128)S(1)}, u32[]{:S(2)}, u32[]{:S(2)}) %collective-permute-start.16) | collective-permute-done | bytes 131104 | tf_op jit(solution)/shard_map/ppermute | solution.py:139
  (114 shorter events, 44.1 us)
Async XLA Ops:
  1.4 3.0 %collective-permute-start = (bf16[1,4,1,4,512]{4,3,2,1,0:T(4,128)(2,1)S(1)}, bf16[1,4,1,4,512]{4,3,2,1,0:T(4,128)(2,1)S(1)}, u32[]{:S(2)}, u32[]{:S(2)}) collective-permute-start(bf16[1,4,1,4,512]{4,3,2,1,0:T(4,128)(2,1)S(1)} %get-tuple-element.60), channel_id=1, source_target_pairs={{0,32},{32,64},{64,96},{96,128},{128,160},{160,192},{192,224},{224... | collective-permute-start | bytes 49160 | tf_op jit(solution)/shard_map/ppermute | solution.py:15
  3.1 4.4 %collective-permute-start.1 = (bf16[1,4,1,4,512]{4,3,2,1,0:T(4,128)(2,1)S(1)}, bf16[1,4,1,4,512]{4,3,2,1,0:T(4,128)(2,1)S(1)}, u32[]{:S(2)}, u32[]{:S(2)}) collective-permute-start(bf16[1,4,1,4,512]{4,3,2,1,0:T(4,128)(2,1)S(1)} %get-tuple-element.59), channel_id=1, source_target_pairs={{32,0},{64,32},{96,64},{128,96},{160,128},{192,160},{224,192},{256... | collective-permute-start | bytes 49160 | tf_op jit(solution)/shard_map/ppermute | solution.py:18
  7.6 8.8 %collective-permute-start.2 = (bf16[1,4,6,1,512]{4,3,2,1,0:T(2,128)(2,1)S(1)}, bf16[1,4,6,1,512]{4,3,2,1,0:T(2,128)(2,1)S(1)}, u32[]{:S(2)}, u32[]{:S(2)}) collective-permute-start(bf16[1,4,6,1,512]{4,3,2,1,0:T(2,128)(2,1)S(1)} %get-tuple-element.57), channel_id=1, source_target_pairs={{0,4},{4,8},{8,12},{12,16},{16,20},{20,24},{24,28},{1,5},{5,9},{9,... | collective-permute-start | bytes 73736 | tf_op jit(solution)/shard_map/ppermute | solution.py:15
  11.1 6.0 %collective-permute-start.3 = (bf16[1,4,6,1,512]{4,3,2,1,0:T(2,128)(2,1)S(1)}, bf16[1,4,6,1,512]{4,3,2,1,0:T(2,128)(2,1)S(1)}, u32[]{:S(2)}, u32[]{:S(2)}) collective-permute-start(bf16[1,4,6,1,512]{4,3,2,1,0:T(2,128)(2,1)S(1)} %get-tuple-element.58), channel_id=1, source_target_pairs={{4,0},{8,4},{12,8},{16,12},{20,16},{24,20},{28,24},{5,1},{9,5},{13... | collective-permute-start | bytes 73736 | tf_op jit(solution)/shard_map/ppermute | solution.py:18
  35.1 0.7 copy-start.1
  45.3 31.0 %copy-start.3 = (bf16[8,864]{1,0:T(8,128)(2,1)S(1)}, bf16[8,864]{1,0:T(8,128)(2,1)}, u32[]{:S(2)}) copy-start(bf16[8,864]{1,0:T(8,128)(2,1)} %param.6) | copy-start | bytes 41476
  45.3 32.8 %copy-start.2 = (bf16[1,8,1,1024]{3,1,2,0:T(8,128)(2,1)S(1)}, bf16[1,8,1,1024]{3,1,2,0:T(8,128)(2,1)}, u32[]{:S(2)}) copy-start(bf16[1,8,1,1024]{3,1,2,0:T(8,128)(2,1)} %param.7) | copy-start | bytes 49156
  73.5 5.6 %collective-permute-start.4 = (bf16[1,32,1,16,256]{4,1,3,2,0:T(8,128)(2,1)S(1)}, bf16[1,32,1,16,256]{4,1,3,2,0:T(8,128)(2,1)S(1)}, u32[]{:S(2)}, u32[]{:S(2)}) collective-permute-start(bf16[1,32,1,16,256]{4,1,3,2,0:T(8,128)(2,1)S(1)} %get-tuple-element.41), channel_id=1, source_target_pairs={{0,32},{32,64},{64,96},{96,128},{128,160},{160,192},{192,224},{224... | collective-permute-start | bytes 786440 | tf_op jit(solution)/shard_map/ppermute | solution.py:15
  74.8 6.0 %collective-permute-start.5 = (bf16[1,32,1,16,256]{4,1,3,2,0:T(8,128)(2,1)S(1)}, bf16[1,32,1,16,256]{4,1,3,2,0:T(8,128)(2,1)S(1)}, u32[]{:S(2)}, u32[]{:S(2)}) collective-permute-start(bf16[1,32,1,16,256]{4,1,3,2,0:T(8,128)(2,1)S(1)} %get-tuple-element.42), channel_id=1, source_target_pairs={{32,0},{64,32},{96,64},{128,96},{160,128},{192,160},{224,192},{256... | collective-permute-start | bytes 786440 | tf_op jit(solution)/shard_map/ppermute | solution.py:18
  83.8 2.8 %copy-start = (bf16[8,3,32,3,3]{2,0,4,3,1:T(8,128)(2,1)S(1)}, bf16[8,3,32,3,3]{2,0,4,3,1:T(8,128)(2,1)}, u32[]{:S(2)}) copy-start(bf16[8,3,32,3,3]{2,0,4,3,1:T(8,128)(2,1)} %copy.405) | copy-start | bytes 41476
  89.3 8.2 %collective-permute-start.12 = (bf16[1,8,1,16,256]{4,1,3,2,0:T(8,128)(2,1)S(1)}, bf16[1,8,1,16,256]{4,1,3,2,0:T(8,128)(2,1)S(1)}, u32[]{:S(2)}, u32[]{:S(2)}) collective-permute-start(bf16[1,8,1,16,256]{4,1,3,2,0:T(8,128)(2,1)S(1)} %get-tuple-element.55), channel_id=1, source_target_pairs={{0,32},{32,64},{64,96},{96,128},{128,160},{160,192},{192,224},{224... | collective-permute-start | bytes 196616 | tf_op jit(solution)/shard_map/ppermute | solution.py:15
  96.0 3.1 %collective-permute-start.13 = (bf16[1,8,1,16,256]{4,1,3,2,0:T(8,128)(2,1)S(1)}, bf16[1,8,1,16,256]{4,1,3,2,0:T(8,128)(2,1)S(1)}, u32[]{:S(2)}, u32[]{:S(2)}) collective-permute-start(bf16[1,8,1,16,256]{4,1,3,2,0:T(8,128)(2,1)S(1)} %get-tuple-element.56), channel_id=1, source_target_pairs={{32,0},{64,32},{96,64},{128,96},{160,128},{192,160},{224,192},{256... | collective-permute-start | bytes 196616 | tf_op jit(solution)/shard_map/ppermute | solution.py:18
  101.6 15.0 %collective-permute-start.14 = (f32[2,2,1,2,2,32,256]{6,5,4,3,0,2,1:T(8,128)S(1)}, f32[2,2,1,2,2,32,256]{6,5,4,3,0,2,1:T(8,128)S(1)}, u32[]{:S(2)}, u32[]{:S(2)}) collective-permute-start(f32[2,2,1,2,2,32,256]{6,5,4,3,0,2,1:T(8,128)S(1)} %copy.444), channel_id=1, source_target_pairs={{0,4},{4,0},{8,12},{12,8},{16,20},{20,16},{24,28},{28,24},{1,5},{5... | collective-permute-start | bytes 1572872 | tf_op jit(solution)/shard_map/ppermute | solution.py:139
  116.7 51.9 %collective-permute-start.15 = (f32[2,1,2,2,32,256]{5,4,3,2,0,1:T(8,128)S(1)}, f32[2,1,2,2,32,256]{5,4,3,2,0,1:T(8,128)}, u32[]{:S(2)}, u32[]{:S(2)}) collective-permute-start(f32[2,1,2,2,32,256]{5,4,3,2,0,1:T(8,128)S(1)} %dynamic-slice_bitcast_fusion), channel_id=1, source_target_pairs={{0,8},{4,12},{8,0},{12,4},{16,24},{20,28},{24,16},{28,20},{1,9},{5... | collective-permute-start | bytes 786440 | tf_op jit(solution)/shard_map/ppermute | solution.py:139
  124.7 7.9 %collective-permute-start.6 = (f32[54,128]{1,0:T(8,128)S(1)}, f32[54,128]{1,0:T(8,128)S(1)}, u32[]{:S(2)}, u32[]{:S(2)}) collective-permute-start(f32[54,128]{1,0:T(8,128)S(1)} %mul.80), channel_id=1, source_target_pairs={{0,1},{1,0},{2,3},{3,2},{32,33},{33,32},{34,35},{35,34},{64,65},{6... | collective-permute-start | bytes 82952 | tf_op jit(solution)/shard_map/ppermute | solution.py:42
  132.6 11.5 %collective-permute-start.7 = (f32[54,128]{1,0:T(8,128)S(1)}, f32[54,128]{1,0:T(8,128)S(1)}, u32[]{:S(2)}, u32[]{:S(2)}) collective-permute-start(f32[54,128]{1,0:T(8,128)S(1)} %add.86), channel_id=1, source_target_pairs={{0,3},{1,2},{2,1},{3,0},{32,35},{33,34},{34,33},{35,32},{64,67},{6... | collective-permute-start | bytes 82952 | tf_op jit(solution)/shard_map/ppermute | solution.py:42
  144.1 3.1 %collective-permute-start.8 = (f32[54,128]{1,0:T(8,128)S(1)}, f32[54,128]{1,0:T(8,128)S(1)}, u32[]{:S(2)}, u32[]{:S(2)}) collective-permute-start(f32[54,128]{1,0:T(8,128)S(1)} %add.87), channel_id=1, source_target_pairs={{0,32},{1,33},{2,34},{3,35},{32,0},{33,1},{34,2},{35,3},{64,96},{6... | collective-permute-start | bytes 82952 | tf_op jit(solution)/shard_map/ppermute | solution.py:42
  147.2 7.2 %collective-permute-start.9 = (f32[54,128]{1,0:T(8,128)S(1)}, f32[54,128]{1,0:T(8,128)S(1)}, u32[]{:S(2)}, u32[]{:S(2)}) collective-permute-start(f32[54,128]{1,0:T(8,128)S(1)} %add.88), channel_id=1, source_target_pairs={{0,64},{1,65},{2,66},{3,67},{32,96},{33,97},{34,98},{35,99},{64,0}... | collective-permute-start | bytes 82952 | tf_op jit(solution)/shard_map/ppermute | solution.py:42
  155.0 9.3 %collective-permute-start.10 = (f32[54,128]{1,0:T(8,128)}, f32[54,128]{1,0:T(8,128)}, u32[]{:S(2)}, u32[]{:S(2)}) collective-permute-start(f32[54,128]{1,0:T(8,128)} %add.89), channel_id=1, source_target_pairs={{0,192},{1,193},{2,194},{3,195},{32,224},{33,225},{34,226},{35,227... | collective-permute-start | bytes 82952 | tf_op jit(solution)/shard_map/ppermute | solution.py:42
  165.1 9.8 %collective-permute-start.11 = (f32[54,128]{1,0:T(8,128)S(1)}, f32[54,128]{1,0:T(8,128)S(1)}, u32[]{:S(2)}, u32[]{:S(2)}) collective-permute-start(f32[54,128]{1,0:T(8,128)S(1)} %add.90), channel_id=1, source_target_pairs={{0,256},{1,257},{2,258},{3,259},{32,288},{33,289},{34,290},{35,291... | collective-permute-start | bytes 82952 | tf_op jit(solution)/shard_map/ppermute | solution.py:42
  169.5 12.1 %collective-permute-start.16 = (f32[1,2,2,32,256]{4,3,2,1,0:T(8,128)S(1)}, f32[1,2,2,32,256]{4,3,2,1,0:T(8,128)S(1)}, u32[]{:S(2)}, u32[]{:S(2)}) collective-permute-start(f32[1,2,2,32,256]{4,3,2,1,0:T(8,128)S(1)} %dynamic-slice_bitcast_fusion.1), channel_id=1, source_target_pairs={{0,16},{4,20},{8,24},{12,28},{16,0},{20,4},{24,8},{28,12},{1,17},{... | collective-permute-start | bytes 393224 | tf_op jit(solution)/shard_map/ppermute | solution.py:139
